TPU v7x, 32 devices: a whole 2x2x4 slice. The times are simulated.
32 devices in a mesh: grp: 2 (over x), seq: 16 (over z, y, core).
Axes of the slice: x: 2, y: 2, z: 4, core: 2. Of those that a mesh axis runs over, the one named last changes fastest.
Arguments:
- queries: bfloat16 [16384, 4096], P(('grp', 'seq')), parts along dimension 0, may hold values from -16 to 16
- keys: bfloat16 [16384, 2048], P(('grp', 'seq')), parts along dimension 0, may hold values from -16 to 16
- values: bfloat16 [16384, 2048], P(('grp', 'seq')), parts along dimension 0, may hold values from -6 to 6
- segment_ids: int32 [16384], P(('grp', 'seq')), parts along dimension 0, may hold values from 0 to 15, never falling along the last dimension, each value on 1 to 2048 neighbouring positions
Outputs:
- attended: bfloat16 [16384, 4096], P(('grp', 'seq')), parts along dimension 0
There are 2 independent parts, one for each index of `grp`. A program takes and returns all parts, laid end to end along the dimension named above; each array names one. Nothing has to cross between parts.
Inputs may be any that keep to these rules, and one draw needn't show every extreme that they name: `segment_ids`: segment ids never fall along the tokens; every document holds 1 to 2048 tokens and one holds exactly 2048.
All inputs are finite; a program needn't handle non-finite values.
Results may differ from a plain program's by a relative error of at most 0.0039.
Values may be sent and summed in bfloat16 or wider, within the bound.
No kernel may reach another device: no remote copies, remote signals or barrier semaphores. Data moves between devices by JAX's collectives and lax.ppermute only.
A program may use at most 128 MiB of HBM per device.

v0:
```python
import jax
import jax.numpy as jnp
from jax import lax
from jax.sharding import PartitionSpec as P

H = 32
KVH = 16
HD = 128
W = 1024


query_scale = 168.0 ** (-0.5)


def carried_in(value, axis, join, neutral):
    count, mine = (lax.axis_size(axis), lax.axis_index(axis))
    pieces = jax.tree.map(lambda part: lax.all_gather(part, axis), value)
    subtotal = jax.tree.map(
        lambda part, zero: jnp.full_like(part, 0) + jnp.asarray(zero, part.dtype), value, neutral
    )

    def turn(position, subtotal):
        longer = join(subtotal, jax.tree.map(lambda part: part[position], pieces))
        return jax.tree.map(lambda new, old: jnp.where(position < mine, new, old), longer, subtotal)

    return lax.fori_loop(0, count - 1, turn, subtotal)


def passed_along(value, axis, steps):
    count = lax.axis_size(axis)
    first, last = (max(0, -steps), min(count, count - steps))
    return lax.ppermute(value, axis, [(source, source + steps) for source in range(first, last)])


def rotate(x, doc_pos):
    half = x.shape[-1] // 2
    freqs = 10000.0 ** (-2.0 * jnp.arange(half, dtype=jnp.float32) / x.shape[-1])
    angles = doc_pos.astype(jnp.float32)[:, None] * freqs[None, :]
    cosine = jnp.concatenate([jnp.cos(angles), jnp.cos(angles)], -1)[:, None, :]
    sine = jnp.concatenate([jnp.sin(angles), jnp.sin(angles)], -1)[:, None, :]
    turned = jnp.concatenate([-x[..., half:], x[..., :half]], -1)
    return x * cosine + turned * sine


def combine(earlier, later):
    empty = later[0] < 0
    same = earlier[0] == later[0]
    doc_last = jnp.where(empty, earlier[0], later[0])
    extended = later[1] + jnp.where((later[2] == 1) & same, earlier[1], 0)
    run_length = jnp.where(empty, earlier[1], extended)
    whole = (later[2] == 1) & ((earlier[2] == 1) & same | (earlier[0] < 0))
    uniform = jnp.where(empty, earlier[2], jnp.where(whole, 1, 0).astype(jnp.int32))
    return (doc_last, run_length, uniform)


def local(queries, keys, values, segment_ids):
    rows_here = queries.shape[0]
    hop_count = W // rows_here
    places = jnp.arange(rows_here, dtype=jnp.int32)
    previous = jnp.concatenate([segment_ids[:1], segment_ids[:-1]])
    boundary = (segment_ids != previous) | (places == 0)
    starts = lax.cummax(jnp.where(boundary, places, 0), axis=0)
    local_pos = places - starts
    summary = (
        segment_ids[-1],
        rows_here - starts[-1],
        jnp.where(starts[-1] == 0, 1, 0).astype(jnp.int32),
    )
    identity = (jnp.int32(-1), jnp.int32(0), jnp.int32(1))
    shard_index = lax.axis_index("seq")
    carried = carried_in(summary, "seq", combine, identity)
    joined = (starts == 0) & (segment_ids == carried[0])
    doc_pos = local_pos + jnp.where(joined, carried[1], 0)
    q_rot = rotate(queries.astype(jnp.float32).reshape(rows_here, H, HD), doc_pos)
    q_rot = q_rot.astype(jnp.bfloat16).reshape(rows_here, H * HD)
    k_rot = rotate(keys.astype(jnp.float32).reshape(rows_here, KVH, HD), doc_pos)
    k_rot = k_rot.astype(jnp.bfloat16).reshape(rows_here, KVH * HD)
    tails = [passed_along((k_rot, values), "seq", distance) for distance in range(1, hop_count + 1)]
    key_rows = jnp.concatenate([pair[0] for pair in reversed(tails)] + [k_rot], 0)
    value_rows = jnp.concatenate([pair[1] for pair in reversed(tails)] + [values], 0)
    q_glob = shard_index * rows_here + places
    k_glob = (shard_index - hop_count) * rows_here + jnp.arange(
        (hop_count + 1) * rows_here, dtype=jnp.int32
    )
    gap = q_glob[:, None] - k_glob[None, :]
    visible = (gap >= 0) & (gap < W) & (gap <= doc_pos[:, None])

    def head_out(head):
        query_head = lax.dynamic_slice_in_dim(q_rot, head * 2 * HD, 2 * HD, 1).reshape(
            rows_here, 2, HD
        )
        key_head = lax.dynamic_slice_in_dim(key_rows, head * HD, HD, 1)
        value_head = lax.dynamic_slice_in_dim(value_rows, head * HD, HD, 1)
        scores = (
            jnp.einsum("qgd,kd->gqk", query_head, key_head, preferred_element_type=jnp.float32)
            * query_scale
        )
        scores = jnp.where(visible[None], scores, -1e30)
        row_max = jnp.max(scores, axis=-1, keepdims=True)
        weights = jnp.where(visible[None], jnp.exp(scores - row_max), 0.0)
        totals = jnp.sum(weights, axis=-1, keepdims=True)
        summed = jnp.einsum(
            "gqk,kd->qgd",
            weights.astype(jnp.bfloat16),
            value_head,
            preferred_element_type=jnp.float32,
        )
        result = summed / jnp.transpose(totals, (1, 0, 2))
        return result.reshape(rows_here, 2 * HD).astype(jnp.bfloat16)

    per_head = lax.map(head_out, jnp.arange(KVH, dtype=jnp.int32))
    return jnp.transpose(per_head, (1, 0, 2)).reshape(rows_here, H * HD)


def solution(mesh):
    return jax.shard_map(
        local,
        mesh=mesh,
        in_specs=(
            P(("grp", "seq"), None),
            P(("grp", "seq"), None),
            P(("grp", "seq"), None),
            P(("grp", "seq")),
        ),
        out_specs=P(("grp", "seq"), None),
        check_vma=False,
    )
```

profile of v0, /device:TPU:10, one launch (start us, length us, event | category | flops | bytes accessed | tf_op | source)
XLA Modules:
  0.0 483.7 jit_solution(14352571319756821800)
XLA Ops:
  7.1 11.2 %all-reduce.3 = (s32[16]{0:T(128)S(1)}, s32[16]{0:T(128)S(1)}, s32[16]{0:T(128)S(1)}) all-reduce(s32[16]{0:T(128)S(1)} %get-tuple-element.289, s32[16]{0:T(128)S(1)} %subtract_dynamic-update-slice_fusion, s32[16]{0:T(128)S(1)} %fusion.43), channel_id=1, replica_groups=mesh['grp'=2,'seq'=16] {'seq'}, use_global_device_ids=true, to_apply=%add | all-reduce | flops 48 | bytes 384
  18.3 80.3 %while.28 = (s32[]{:T(128)}, s32[]{:T(128)}, s32[]{:T(128)}, s32[]{:T(128)}, s32[16]{0:T(128)S(1)}, /*index=5*/s32[16]{0:T(128)S(1)}, s32[16]{0:T(128)S(1)}, s32[]{:T(128)}, s32[]{:T(128)}, s32[1]{0:T(128)}) while((s32[]{:T(128)}, s32[]{:T(128)}, s32[]{:T(128)}, s32[]{:T(128)}, s32[16]{0:T(128)S(1)}, /*index=5*/s32[16]{0:T(128)S(1)}, ...), condition=%wide.region_3.4_spmd, body=%wide.region_2.3_spmd.sunk | while | flops 13 | bytes 253 | solution.py:26
  103.1 4.6 slice_negate_fusion.1
  107.9 4.6 maximum_multiply_fusion.1
  114.1 3.9 fusion.41
  118.0 2.8 collective-permute-start.2
  122.7 3.9 copy.12
  126.7 3.0 collective-permute-start
  129.6 2.8 collective-permute-start.1
  132.4 6.4 %copy.17 = bf16[512,4096]{0,1:T(8,128)(2,1)} copy(bf16[512,4096]{1,0:T(8,128)(2,1)} %param.8) | data formatting | bytes 8388608 | tf_op args[0]
  138.8 6.7 %convert = f32[512,32,128]{0,2,1:T(8,128)} convert(bf16[512,32,128]{0,2,1:T(8,128)(2,1)} %bitcast.96) | non-fusion elementwise | flops 2097152 | bytes 12582912 | tf_op jit(solution)/shard_map/reshape | solution.py:74
  148.1 4.9 %slice_negate_fusion = f32[512,32,64]{0,2,1:T(8,128)} fusion(f32[512,32,128]{0,2,1:T(8,128)} %convert), kind=kLoop, calls=%fused_computation.43 | loop fusion | flops 1048576 | bytes 8388608 | tf_op jit(solution)/shard_map/neg | solution.py:41
  153.0 5.1 %maximum_multiply_fusion = f32[512,32,128]{0,2,1:T(8,128)S(1)} fusion(f32[512,32,64]{0,2,1:T(8,128)} %slice.45, f32[512,32,64]{0,2,1:T(8,128)} %slice_negate_fusion, f32[512,128]{0,1:T(8,128)S(1)} %pad_maximum_fusion.3), kind=kLoop, calls=%fused_computation.33 | loop fusion | flops 4194304 | bytes 17039360 | tf_op jit(solution)/shard_map/mul | solution.py:42
  158.1 4.8 fusion.39
  162.9 6.8 %collective-permute-done.2 = bf16[512,2048]{1,0:T(8,128)(2,1)} collective-permute-done((bf16[512,2048]{1,0:T(8,128)(2,1)}, bf16[512,2048]{1,0:T(8,128)(2,1)}, u32[]{:S(2)}, u32[]{:S(2)}) %collective-permute-start.2) | collective-permute-done | bytes 2097184 | tf_op jit(solution)/shard_map/ppermute | solution.py:32
  169.6 37.8 %collective-permute-done.3 = bf16[512,2048]{1,0:T(8,128)(2,1)} collective-permute-done((bf16[512,2048]{1,0:T(8,128)(2,1)}, bf16[512,2048]{1,0:T(8,128)(2,1)}, u32[]{:S(2)}, u32[]{:S(2)}) %collective-permute-start.3) | collective-permute-done | bytes 2097184 | tf_op jit(solution)/shard_map/ppermute | solution.py:32
  207.5 5.9 %pad_maximum_fusion.1 = bf16[1536,2048]{1,0:T(8,128)(2,1)} fusion(bf16[512,2048]{1,0:T(8,128)(2,1)} %fusion.41, bf16[512,2048]{1,0:T(8,128)(2,1)} %collective-permute-done.3, bf16[512,2048]{1,0:T(8,128)(2,1)} %collective-permute-done.2), kind=kLoop, calls=%fused_computation.38 | loop fusion | flops 18874368 | bytes 12582912 | tf_op jit(solution)/shard_map/concatenate | solution.py:79
  214.6 41.4 %collective-permute-done.1 = bf16[512,2048]{0,1:T(8,128)(2,1)} collective-permute-done((bf16[512,2048]{0,1:T(8,128)(2,1)}, bf16[512,2048]{0,1:T(8,128)(2,1)}, u32[]{:S(2)}, u32[]{:S(2)}) %collective-permute-start.1) | collective-permute-done | bytes 2097184 | tf_op jit(solution)/shard_map/ppermute | solution.py:32
  256.0 6.3 %pad_maximum_fusion = bf16[1536,2048]{0,1:T(8,128)(2,1)} fusion(bf16[512,2048]{0,1:T(8,128)(2,1)} %copy.12, bf16[512,2048]{0,1:T(8,128)(2,1)} %collective-permute-done.1, bf16[512,2048]{0,1:T(8,128)(2,1)} %collective-permute-done), kind=kLoop, calls=%fused_computation.37 | loop fusion | flops 18874368 | bytes 12582912 | tf_op jit(solution)/shard_map/concatenate | solution.py:80
  262.3 215.1 %while.29 = (s32[]{:T(128)}, bf16[16,512,256]{1,2,0:T(8,128)(2,1)}, s32[16]{0:T(128)S(1)}, bf16[1536,2048]{0,1:T(8,128)(2,1)}, bf16[1536,2048]{1,0:T(8,128)(2,1)...) while((s32[]{:T(128)}, bf16[16,512,256]{1,2,0:T(8,128)(2,1)}, ...), condition=%wide.region_7.8_spmd.clone, body=%wide.region_4.7_spmd.clone.sunk | while | flops 819725824 | bytes 11029249 | solution.py:111
  266.3 6.0 %fusion.63 = (f32[2,512]{1,0:T(2,128)S(1)}, bf16[2,512,1536]{1,2,0:T(8,128)(2,1)}) fusion(pred[512,1536]{0,1:T(8,128)(4,1)S(1)} %fusion.62, bf16[512,2,128]{0,2,1:T(8,128)(2,1)S(1)} %bitcast.101, bf16[1536,2048]{1,0:T(8,128)(2,1)} %get-tuple-element.458, s32[]{:T(128)S(6)} %select_n.118), kind=kOutput, calls=%fused_computation.65.clone.1 | convolution fusion | flops 412091904 | bytes 5378052 | tf_op jit(solution)/shard_map/while/body/eval_jaxpr/sub | solution.py:100
  272.4 2.6 fusion.64
  279.8 6.0 %fusion.63 = (f32[2,512]{1,0:T(2,128)S(1)}, bf16[2,512,1536]{1,2,0:T(8,128)(2,1)}) fusion(pred[512,1536]{0,1:T(8,128)(4,1)S(1)} %fusion.62, bf16[512,2,128]{0,2,1:T(8,128)(2,1)S(1)} %bitcast.101, bf16[1536,2048]{1,0:T(8,128)(2,1)} %get-tuple-element.458, s32[]{:T(128)S(6)} %select_n.118), kind=kOutput, calls=%fused_computation.65.clone.1 | convolution fusion | flops 412091904 | bytes 5378052 | tf_op jit(solution)/shard_map/while/body/eval_jaxpr/sub | solution.py:100
  285.8 2.6 fusion.64
  293.2 6.0 %fusion.63 = (f32[2,512]{1,0:T(2,128)S(1)}, bf16[2,512,1536]{1,2,0:T(8,128)(2,1)}) fusion(pred[512,1536]{0,1:T(8,128)(4,1)S(1)} %fusion.62, bf16[512,2,128]{0,2,1:T(8,128)(2,1)S(1)} %bitcast.101, bf16[1536,2048]{1,0:T(8,128)(2,1)} %get-tuple-element.458, s32[]{:T(128)S(6)} %select_n.118), kind=kOutput, calls=%fused_computation.65.clone.1 | convolution fusion | flops 412091904 | bytes 5378052 | tf_op jit(solution)/shard_map/while/body/eval_jaxpr/sub | solution.py:100
  299.3 2.6 fusion.64
  306.7 6.0 %fusion.63 = (f32[2,512]{1,0:T(2,128)S(1)}, bf16[2,512,1536]{1,2,0:T(8,128)(2,1)}) fusion(pred[512,1536]{0,1:T(8,128)(4,1)S(1)} %fusion.62, bf16[512,2,128]{0,2,1:T(8,128)(2,1)S(1)} %bitcast.101, bf16[1536,2048]{1,0:T(8,128)(2,1)} %get-tuple-element.458, s32[]{:T(128)S(6)} %select_n.118), kind=kOutput, calls=%fused_computation.65.clone.1 | convolution fusion | flops 412091904 | bytes 5378052 | tf_op jit(solution)/shard_map/while/body/eval_jaxpr/sub | solution.py:100
  320.1 6.0 %fusion.63 = (f32[2,512]{1,0:T(2,128)S(1)}, bf16[2,512,1536]{1,2,0:T(8,128)(2,1)}) fusion(pred[512,1536]{0,1:T(8,128)(4,1)S(1)} %fusion.62, bf16[512,2,128]{0,2,1:T(8,128)(2,1)S(1)} %bitcast.101, bf16[1536,2048]{1,0:T(8,128)(2,1)} %get-tuple-element.458, s32[]{:T(128)S(6)} %select_n.118), kind=kOutput, calls=%fused_computation.65.clone.1 | convolution fusion | flops 412091904 | bytes 5378052 | tf_op jit(solution)/shard_map/while/body/eval_jaxpr/sub | solution.py:100
  326.2 2.6 fusion.64
  333.6 6.0 %fusion.63 = (f32[2,512]{1,0:T(2,128)S(1)}, bf16[2,512,1536]{1,2,0:T(8,128)(2,1)}) fusion(pred[512,1536]{0,1:T(8,128)(4,1)S(1)} %fusion.62, bf16[512,2,128]{0,2,1:T(8,128)(2,1)S(1)} %bitcast.101, bf16[1536,2048]{1,0:T(8,128)(2,1)} %get-tuple-element.458, s32[]{:T(128)S(6)} %select_n.118), kind=kOutput, calls=%fused_computation.65.clone.1 | convolution fusion | flops 412091904 | bytes 5378052 | tf_op jit(solution)/shard_map/while/body/eval_jaxpr/sub | solution.py:100
  339.6 2.6 fusion.64
  347.0 6.0 %fusion.63 = (f32[2,512]{1,0:T(2,128)S(1)}, bf16[2,512,1536]{1,2,0:T(8,128)(2,1)}) fusion(pred[512,1536]{0,1:T(8,128)(4,1)S(1)} %fusion.62, bf16[512,2,128]{0,2,1:T(8,128)(2,1)S(1)} %bitcast.101, bf16[1536,2048]{1,0:T(8,128)(2,1)} %get-tuple-element.458, s32[]{:T(128)S(6)} %select_n.118), kind=kOutput, calls=%fused_computation.65.clone.1 | convolution fusion | flops 412091904 | bytes 5378052 | tf_op jit(solution)/shard_map/while/body/eval_jaxpr/sub | solution.py:100
  360.4 6.0 %fusion.63 = (f32[2,512]{1,0:T(2,128)S(1)}, bf16[2,512,1536]{1,2,0:T(8,128)(2,1)}) fusion(pred[512,1536]{0,1:T(8,128)(4,1)S(1)} %fusion.62, bf16[512,2,128]{0,2,1:T(8,128)(2,1)S(1)} %bitcast.101, bf16[1536,2048]{1,0:T(8,128)(2,1)} %get-tuple-element.458, s32[]{:T(128)S(6)} %select_n.118), kind=kOutput, calls=%fused_computation.65.clone.1 | convolution fusion | flops 412091904 | bytes 5378052 | tf_op jit(solution)/shard_map/while/body/eval_jaxpr/sub | solution.py:100
  366.4 2.6 fusion.64
  373.9 6.0 %fusion.63 = (f32[2,512]{1,0:T(2,128)S(1)}, bf16[2,512,1536]{1,2,0:T(8,128)(2,1)}) fusion(pred[512,1536]{0,1:T(8,128)(4,1)S(1)} %fusion.62, bf16[512,2,128]{0,2,1:T(8,128)(2,1)S(1)} %bitcast.101, bf16[1536,2048]{1,0:T(8,128)(2,1)} %get-tuple-element.458, s32[]{:T(128)S(6)} %select_n.118), kind=kOutput, calls=%fused_computation.65.clone.1 | convolution fusion | flops 412091904 | bytes 5378052 | tf_op jit(solution)/shard_map/while/body/eval_jaxpr/sub | solution.py:100
  379.9 2.6 fusion.64
  387.3 6.0 %fusion.63 = (f32[2,512]{1,0:T(2,128)S(1)}, bf16[2,512,1536]{1,2,0:T(8,128)(2,1)}) fusion(pred[512,1536]{0,1:T(8,128)(4,1)S(1)} %fusion.62, bf16[512,2,128]{0,2,1:T(8,128)(2,1)S(1)} %bitcast.101, bf16[1536,2048]{1,0:T(8,128)(2,1)} %get-tuple-element.458, s32[]{:T(128)S(6)} %select_n.118), kind=kOutput, calls=%fused_computation.65.clone.1 | convolution fusion | flops 412091904 | bytes 5378052 | tf_op jit(solution)/shard_map/while/body/eval_jaxpr/sub | solution.py:100
  400.8 6.0 %fusion.63 = (f32[2,512]{1,0:T(2,128)S(1)}, bf16[2,512,1536]{1,2,0:T(8,128)(2,1)}) fusion(pred[512,1536]{0,1:T(8,128)(4,1)S(1)} %fusion.62, bf16[512,2,128]{0,2,1:T(8,128)(2,1)S(1)} %bitcast.101, bf16[1536,2048]{1,0:T(8,128)(2,1)} %get-tuple-element.458, s32[]{:T(128)S(6)} %select_n.118), kind=kOutput, calls=%fused_computation.65.clone.1 | convolution fusion | flops 412091904 | bytes 5378052 | tf_op jit(solution)/shard_map/while/body/eval_jaxpr/sub | solution.py:100
  406.8 2.6 fusion.64
  414.2 6.0 %fusion.63 = (f32[2,512]{1,0:T(2,128)S(1)}, bf16[2,512,1536]{1,2,0:T(8,128)(2,1)}) fusion(pred[512,1536]{0,1:T(8,128)(4,1)S(1)} %fusion.62, bf16[512,2,128]{0,2,1:T(8,128)(2,1)S(1)} %bitcast.101, bf16[1536,2048]{1,0:T(8,128)(2,1)} %get-tuple-element.458, s32[]{:T(128)S(6)} %select_n.118), kind=kOutput, calls=%fused_computation.65.clone.1 | convolution fusion | flops 412091904 | bytes 5378052 | tf_op jit(solution)/shard_map/while/body/eval_jaxpr/sub | solution.py:100
  420.2 2.6 fusion.64
  427.6 6.0 %fusion.63 = (f32[2,512]{1,0:T(2,128)S(1)}, bf16[2,512,1536]{1,2,0:T(8,128)(2,1)}) fusion(pred[512,1536]{0,1:T(8,128)(4,1)S(1)} %fusion.62, bf16[512,2,128]{0,2,1:T(8,128)(2,1)S(1)} %bitcast.101, bf16[1536,2048]{1,0:T(8,128)(2,1)} %get-tuple-element.458, s32[]{:T(128)S(6)} %select_n.118), kind=kOutput, calls=%fused_computation.65.clone.1 | convolution fusion | flops 412091904 | bytes 5378052 | tf_op jit(solution)/shard_map/while/body/eval_jaxpr/sub | solution.py:100
  441.1 6.0 %fusion.63 = (f32[2,512]{1,0:T(2,128)S(1)}, bf16[2,512,1536]{1,2,0:T(8,128)(2,1)}) fusion(pred[512,1536]{0,1:T(8,128)(4,1)S(1)} %fusion.62, bf16[512,2,128]{0,2,1:T(8,128)(2,1)S(1)} %bitcast.101, bf16[1536,2048]{1,0:T(8,128)(2,1)} %get-tuple-element.458, s32[]{:T(128)S(6)} %select_n.118), kind=kOutput, calls=%fused_computation.65.clone.1 | convolution fusion | flops 412091904 | bytes 5378052 | tf_op jit(solution)/shard_map/while/body/eval_jaxpr/sub | solution.py:100
  454.5 6.0 %fusion.63 = (f32[2,512]{1,0:T(2,128)S(1)}, bf16[2,512,1536]{1,2,0:T(8,128)(2,1)}) fusion(pred[512,1536]{0,1:T(8,128)(4,1)S(1)} %fusion.62, bf16[512,2,128]{0,2,1:T(8,128)(2,1)S(1)} %bitcast.101, bf16[1536,2048]{1,0:T(8,128)(2,1)} %get-tuple-element.458, s32[]{:T(128)S(6)} %select_n.118), kind=kOutput, calls=%fused_computation.65.clone.1 | convolution fusion | flops 412091904 | bytes 5378052 | tf_op jit(solution)/shard_map/while/body/eval_jaxpr/sub | solution.py:100
  460.5 2.6 fusion.64
  468.0 6.0 %fusion.63 = (f32[2,512]{1,0:T(2,128)S(1)}, bf16[2,512,1536]{1,2,0:T(8,128)(2,1)}) fusion(pred[512,1536]{0,1:T(8,128)(4,1)S(1)} %fusion.62, bf16[512,2,128]{0,2,1:T(8,128)(2,1)S(1)} %bitcast.101, bf16[1536,2048]{1,0:T(8,128)(2,1)} %get-tuple-element.458, s32[]{:T(128)S(6)} %select_n.118), kind=kOutput, calls=%fused_computation.65.clone.1 | convolution fusion | flops 412091904 | bytes 5378052 | tf_op jit(solution)/shard_map/while/body/eval_jaxpr/sub | solution.py:100
  474.0 2.6 fusion.64
  477.3 6.3 %copy.21 = bf16[512,4096]{1,0:T(8,128)(2,1)} copy(bf16[512,4096]{0,1:T(8,128)(2,1)} %bitcast.10) | data formatting | bytes 8388608 | tf_op jit(solution)/shard_map/reshape | solution.py:112
  (150 shorter events, 118.6 us)
Async XLA Ops:
  112.5 1.6 copy-start.2
  118.0 51.6 %collective-permute-start.2 = (bf16[512,2048]{1,0:T(8,128)(2,1)}, bf16[512,2048]{1,0:T(8,128)(2,1)}, u32[]{:S(2)}, u32[]{:S(2)}) collective-permute-start(bf16[512,2048]{1,0:T(8,128)(2,1)} %fusion.41), channel_id=1, source_target_pairs={{0,2},{1,3},{2,4},{3,5},{4,6},{5,7},{6,8},{7,9},{8,10},{9,11},{10,... | collective-permute-start | bytes 6291464 | tf_op jit(solution)/shard_map/ppermute | solution.py:32
  120.8 86.7 %collective-permute-start.3 = (bf16[512,2048]{1,0:T(8,128)(2,1)}, bf16[512,2048]{1,0:T(8,128)(2,1)}, u32[]{:S(2)}, u32[]{:S(2)}) collective-permute-start(bf16[512,2048]{1,0:T(8,128)(2,1)} %fusion.41), channel_id=1, source_target_pairs={{0,1},{1,2},{2,3},{3,4},{4,5},{5,6},{6,7},{7,8},{8,9},{9,10},{10,1... | collective-permute-start | bytes 6291464 | tf_op jit(solution)/shard_map/ppermute | solution.py:32
  126.7 87.9 %collective-permute-start = (bf16[512,2048]{0,1:T(8,128)(2,1)}, bf16[512,2048]{0,1:T(8,128)(2,1)}, u32[]{:S(2)}, u32[]{:S(2)}) collective-permute-start(bf16[512,2048]{0,1:T(8,128)(2,1)} %copy.12), channel_id=1, source_target_pairs={{0,2},{1,3},{2,4},{3,5},{4,6},{5,7},{6,8},{7,9},{8,10},{9,11},{10,... | collective-permute-start | bytes 6291464 | tf_op jit(solution)/shard_map/ppermute | solution.py:32
  129.6 126.3 %collective-permute-start.1 = (bf16[512,2048]{0,1:T(8,128)(2,1)}, bf16[512,2048]{0,1:T(8,128)(2,1)}, u32[]{:S(2)}, u32[]{:S(2)}) collective-permute-start(bf16[512,2048]{0,1:T(8,128)(2,1)} %copy.12), channel_id=1, source_target_pairs={{0,1},{1,2},{2,3},{3,4},{4,5},{5,6},{6,7},{7,8},{8,9},{9,10},{10,1... | collective-permute-start | bytes 6291464 | tf_op jit(solution)/shard_map/ppermute | solution.py:32
  138.8 6.7 %copy-start = (bf16[512,4096]{0,1:T(8,128)(2,1)S(1)}, bf16[512,4096]{0,1:T(8,128)(2,1)}, u32[]{:S(2)}) copy-start(bf16[512,4096]{0,1:T(8,128)(2,1)} %copy.17) | copy-start | bytes 12582916
  153.0 5.1 %copy-start.1 = (bf16[512,4096]{0,1:T(8,128)(2,1)S(1)}, bf16[512,4096]{0,1:T(8,128)(2,1)}, u32[]{:S(2)}) copy-start(bf16[512,4096]{0,1:T(8,128)(2,1)} %copy.17) | copy-start | bytes 12582916
where the time goes:
time: 487 us; the launch traced here: 484 us
  matrix products  138 us (28%)
  local copies, waits for them, and re-layouts  92.1 us (19%)
  waiting for transfers between devices  87.2 us (18%)
  other arithmetic  73.9 us (15%)
  loops' own time  70.8 us (15%)
  blocking collectives  11.2 us (2%)
  starting transfers between devices  10.4 us (2%)
    sub x16, matrix products, head_out(): weights = jnp.where(visible[None], jnp.exp(scores - row_max), 0.0)  96.3 us
    ppermute x4, waiting for transfers between devices, passed_along(): lax.ppermute(value, axis, [(source, source + steps) for source in range(f...  87.2 us
    another operation x1, loops' own time, carried_in(): return lax.fori_loop(0, count - 1, turn, subtotal)  50.8 us
    dot_general x16, matrix products, head_out(): jnp.einsum('gqk,kd->qgd', weights.astype(jnp.bfloat16), value_head, prefe...  41.7 us
    dynamic_slice x45, local copies, waits for them, and re-layouts, turn(): longer = join(subtotal, jax.tree.map(lambda part: part[position], pieces))  29.6 us
    and x16, other arithmetic, local(): visible = (gap >= 0) & (gap < W) & (gap <= doc_pos[:, None])  20.1 us
    another operation x1, loops' own time, local(): per_head = lax.map(head_out, jnp.arange(KVH, dtype=jnp.int32))  20 us
    dynamic_slice x16, local copies, waits for them, and re-layouts, head_out(): lax.dynamic_slice_in_dim(q_rot, head * 2 * HD, 2 * HD, 1)  15.6 us
  transfers between devices with their start and end apart: 4, of which 4 were waited for; matrix products, arithmetic and copies ran while one was open for 8% of the time, Pallas kernels for 0%

commit v1 on v0

v1 whole, which is shorter than its diff:
```python
import functools

import jax
import jax.numpy as jnp
from jax import lax
from jax.experimental import pallas as pl
from jax.experimental.pallas import tpu as pltpu
from jax.sharding import PartitionSpec as P

H = 32
KVH = 16
HD = 128
W = 1024


query_scale = 168.0 ** (-0.5)


def passed_along(value, axis, steps):
    count = lax.axis_size(axis)
    first, last = (max(0, -steps), min(count, count - steps))
    return lax.ppermute(value, axis, [(source, source + steps) for source in range(first, last)])


def rope_tables(doc_pos):
    half = HD // 2
    freqs = 10000.0 ** (-2.0 * jnp.arange(half, dtype=jnp.float32) / HD)
    angles = doc_pos.astype(jnp.float32)[:, None] * freqs[None, :]
    cos, sin = jnp.cos(angles), jnp.sin(angles)
    return jnp.concatenate([cos, cos], -1), jnp.concatenate([-sin, sin], -1)


def attend_kernel(pos_ref, cos_ref, sin_ref, q_ref, *refs, rows, hops):
    k_refs = refs[:hops + 1]
    v_refs = refs[hops + 1:2 * hops + 2]
    o_ref = refs[2 * hops + 2]
    span = (hops + 1) * rows
    cos = cos_ref[...]
    sin = sin_ref[...]

    def rot(x, c, s):
        return x * c + pltpu.roll(x, HD // 2, 1) * s

    k = jnp.concatenate([r[...] for r in k_refs], 0).astype(jnp.float32)
    k = rot(k, cos, sin).astype(jnp.bfloat16)
    v = jnp.concatenate([r[...] for r in v_refs], 0)
    qc = cos[span - rows:]
    qs = sin[span - rows:]
    dp = pos_ref[...]
    r = lax.broadcasted_iota(jnp.int32, (rows, span), 0)
    c = lax.broadcasted_iota(jnp.int32, (rows, span), 1)
    gap = (span - rows) + r - c
    vis = (gap >= 0) & (gap < W) & (gap <= dp)
    for g in range(2):
        q = q_ref[:, g * HD:(g + 1) * HD].astype(jnp.float32)
        q = rot(q, qc, qs).astype(jnp.bfloat16)
        s = lax.dot_general(q, k, (((1,), (1,)), ((), ())), preferred_element_type=jnp.float32)
        s = jnp.where(vis, s * query_scale, -1e30)
        m = jnp.max(s, axis=1, keepdims=True)
        w = jnp.where(vis, jnp.exp(s - m), 0.0)
        tot = jnp.sum(w, axis=1, keepdims=True)
        pv = jnp.dot(w.astype(jnp.bfloat16), v, preferred_element_type=jnp.float32)
        o_ref[:, g * HD:(g + 1) * HD] = (pv / tot).astype(jnp.bfloat16)


def local(queries, keys, values, segment_ids):
    rows = queries.shape[0]
    hops = W // rows
    span = (hops + 1) * rows
    shard = lax.axis_index("seq")
    tails = [passed_along((keys, values), "seq", d) for d in range(hops, 0, -1)]
    seg_all = lax.all_gather(segment_ids, "seq", tiled=True)
    total = seg_all.shape[0]
    places = jnp.arange(total, dtype=jnp.int32)
    previous = jnp.concatenate([seg_all[:1], seg_all[:-1]])
    boundary = (seg_all != previous) | (places == 0)
    starts = lax.cummax(jnp.where(boundary, places, 0), axis=0)
    pos_all = jnp.concatenate([jnp.zeros((hops * rows,), jnp.int32), places - starts])
    pos_win = lax.dynamic_slice_in_dim(pos_all, shard * rows, span, 0)
    cos, sin = rope_tables(pos_win)
    pos_q = pos_win[span - rows:].reshape(rows, 1)
    k_list = [t[0] for t in tails] + [keys]
    v_list = [t[1] for t in tails] + [values]
    kv_spec = pl.BlockSpec((rows, HD), lambda h: (0, h))
    full = lambda shape: pl.BlockSpec(shape, lambda h: (0, 0))
    kernel = functools.partial(attend_kernel, rows=rows, hops=hops)
    heads = keys.shape[1] // HD
    return pl.pallas_call(
        kernel,
        grid=(heads,),
        in_specs=[full((rows, 1)), full((span, HD)), full((span, HD)),
                  pl.BlockSpec((rows, 2 * HD), lambda h: (0, h))]
        + [kv_spec] * (2 * hops + 2),
        out_specs=pl.BlockSpec((rows, 2 * HD), lambda h: (0, h)),
        out_shape=jax.ShapeDtypeStruct(queries.shape, jnp.bfloat16),
        compiler_params=pltpu.CompilerParams(dimension_semantics=("arbitrary",)),
    )(pos_q, cos, sin, queries, *k_list, *v_list)


def solution(mesh):
    return jax.shard_map(
        local,
        mesh=mesh,
        in_specs=(
            P(("grp", "seq"), None),
            P(("grp", "seq"), None),
            P(("grp", "seq"), None),
            P(("grp", "seq")),
        ),
        out_specs=P(("grp", "seq"), None),
        check_vma=False,
    )
```

time: 487 us -> 227 us (0.47)
  the two profiles are of different devices: /device:TPU:10 before, /device:TPU:0 now
where the time goes in v1:
time: 227 us
  blocking collectives  137 us (60%)
  Pallas kernels  64.5 us (28%)
  starting transfers between devices  16.2 us (7%)
  other arithmetic  5.8 us (3%)
  local copies, waits for them, and re-layouts  2.98 us (1%)
    all_gather x1, blocking collectives, local(): seg_all = lax.all_gather(segment_ids, 'seq', tiled=True)  137 us
    pallas_call x1, Pallas kernels, local(): pl.pallas_call(kernel, grid=(heads,), in_specs=[full((rows, 1)), full((sp...  64.5 us
    ppermute x4, starting transfers between devices, passed_along(): lax.ppermute(value, axis, [(source, source + steps) for source in range(f...  16.2 us
  transfers between devices with their start and end apart: 4, of which 0 were waited for; matrix products, arithmetic and copies ran while one was open for 3% of the time, Pallas kernels for 0%

profile of v1, /device:TPU:0, one launch (start us, length us, event | category | flops | bytes accessed | tf_op | source)
XLA Modules:
  0.0 226.6 jit_solution(10654844245597371074)
XLA Ops:
  0.0 5.0 %collective-permute-start = (bf16[512,2048]{1,0:T(8,128)(2,1)}, bf16[512,2048]{1,0:T(8,128)(2,1)S(1)}, u32[]{:S(2)}, u32[]{:S(2)}) collective-permute-start(bf16[512,2048]{1,0:T(8,128)(2,1)} %refs_2_.1), channel_id=1, source_target_pairs={{0,2},{1,3},{2,4},{3,5},{4,6},{5,7},{6,8},{7,9},{8,10},{9,11},{10,... | collective-permute-start | bytes 6291464 | tf_op jit(solution)/shard_map/ppermute | solution.py:22
  5.0 2.8 %collective-permute-start.1 = (bf16[512,2048]{1,0:T(8,128)(2,1)}, bf16[512,2048]{1,0:T(8,128)(2,1)}, u32[]{:S(2)}, u32[]{:S(2)}) collective-permute-start(bf16[512,2048]{1,0:T(8,128)(2,1)} %refs_2_.1), channel_id=1, source_target_pairs={{0,1},{1,2},{2,3},{3,4},{4,5},{5,6},{6,7},{7,8},{8,9},{9,10},{10,1... | collective-permute-start | bytes 6291464 | tf_op jit(solution)/shard_map/ppermute | solution.py:22
  7.8 3.8 %collective-permute-start.2 = (bf16[512,2048]{1,0:T(8,128)(2,1)}, bf16[512,2048]{1,0:T(8,128)(2,1)}, u32[]{:S(2)}, u32[]{:S(2)}) collective-permute-start(bf16[512,2048]{1,0:T(8,128)(2,1)} %refs_5_.1), channel_id=1, source_target_pairs={{0,2},{1,3},{2,4},{3,5},{4,6},{5,7},{6,8},{7,9},{8,10},{9,11},{10,... | collective-permute-start | bytes 6291464 | tf_op jit(solution)/shard_map/ppermute | solution.py:22
  11.6 4.6 %collective-permute-start.3 = (bf16[512,2048]{1,0:T(8,128)(2,1)}, bf16[512,2048]{1,0:T(8,128)(2,1)}, u32[]{:S(2)}, u32[]{:S(2)}) collective-permute-start(bf16[512,2048]{1,0:T(8,128)(2,1)} %refs_5_.1), channel_id=1, source_target_pairs={{0,1},{1,2},{2,3},{3,4},{4,5},{5,6},{6,7},{7,8},{8,9},{9,10},{10,1... | collective-permute-start | bytes 6291464 | tf_op jit(solution)/shard_map/ppermute | solution.py:22
  16.2 137.0 %all-gather = s32[16,1,512]{2,1,0:T(1,128)S(1)} all-gather(s32[1,1,512]{2,1,0:T(1,128)} %bitcast.12), channel_id=1, replica_groups=mesh['grp'=2,'seq'=16] {'seq'}, dimensions={0}, use_global_device_ids=true | all-gather | bytes 34816 | tf_op jit(solution)/shard_map/all_gather | solution.py:72
  153.2 0.5 slice.21
  153.7 0.7 select_bitcast_fusion
  154.4 0.3 reduce-window.9
  154.7 0.1 slice.23
  154.8 0.1 reduce-window.12
  154.9 0.1 slice_reduce_fusion
  155.0 0.1 bitcast_subtract_fusion
  155.1 0.1 pad_dynamic-slice_fusion
  155.2 0.9 copy.6.pos_ref
  156.1 0.1 fusion.2
  156.2 2.8 %fusion = (f32[1536,64]{1,0:T(8,128)S(1)}, f32[1536,64]{1,0:T(8,128)S(1)}, f32[1536,64]{1,0:T(8,128)S(1)}) fusion(f32[64]{0:T(128)S(1)} %multiply_power_fusion, f32[1536]{0:T(1024)S(1)} %fusion.2), kind=kLoop, calls=%fused_computation.4 | loop fusion | flops 196608 | bytes 1186048 | tf_op jit(solution)/shard_map/neg | solution.py:30
  159.0 1.7 pad_maximum_fusion
  160.7 0.0 collective-permute-done.refs_0_
  160.7 0.0 copy-start
  160.7 0.0 collective-permute-done.1.refs_1_
  160.7 0.0 collective-permute-done.2.refs_3_
  160.7 0.0 collective-permute-done.3.refs_4_
  160.7 1.3 copy-done
  162.1 64.5 %shard_map.46 = bf16[512,4096]{1,0:T(8,128)(2,1)} custom-call(s32[512,1]{1,0:T(8,128)} %copy.6.pos_ref, f32[1536,128]{1,0:T(8,128)} %get-tuple-element.8.cos_ref, f32[1536,128]{1,0:T(8,128)} %get-tuple-element.9.sin_ref, bf16[512,4096]{1,0:T(8,128)(2,1)} %q_ref.1, bf16[512,2048]{1,0:T(8,128)(2,1)} %copy-done, ...), custom_call_target="tpu_custom_call" | custom-call | tf_op jit(solution)/shard_map/pallas_call | solution.py:88
  (1 shorter events, 0.0 us)
Async XLA Ops:
  0.0 160.7 %collective-permute-start = (bf16[512,2048]{1,0:T(8,128)(2,1)}, bf16[512,2048]{1,0:T(8,128)(2,1)S(1)}, u32[]{:S(2)}, u32[]{:S(2)}) collective-permute-start(bf16[512,2048]{1,0:T(8,128)(2,1)} %refs_2_.1), channel_id=1, source_target_pairs={{0,2},{1,3},{2,4},{3,5},{4,6},{5,7},{6,8},{7,9},{8,10},{9,11},{10,... | collective-permute-start | bytes 6291464 | tf_op jit(solution)/shard_map/ppermute | solution.py:22
  5.0 155.7 %collective-permute-start.1 = (bf16[512,2048]{1,0:T(8,128)(2,1)}, bf16[512,2048]{1,0:T(8,128)(2,1)}, u32[]{:S(2)}, u32[]{:S(2)}) collective-permute-start(bf16[512,2048]{1,0:T(8,128)(2,1)} %refs_2_.1), channel_id=1, source_target_pairs={{0,1},{1,2},{2,3},{3,4},{4,5},{5,6},{6,7},{7,8},{8,9},{9,10},{10,1... | collective-permute-start | bytes 6291464 | tf_op jit(solution)/shard_map/ppermute | solution.py:22
  7.8 152.9 %collective-permute-start.2 = (bf16[512,2048]{1,0:T(8,128)(2,1)}, bf16[512,2048]{1,0:T(8,128)(2,1)}, u32[]{:S(2)}, u32[]{:S(2)}) collective-permute-start(bf16[512,2048]{1,0:T(8,128)(2,1)} %refs_5_.1), channel_id=1, source_target_pairs={{0,2},{1,3},{2,4},{3,5},{4,6},{5,7},{6,8},{7,9},{8,10},{9,11},{10,... | collective-permute-start | bytes 6291464 | tf_op jit(solution)/shard_map/ppermute | solution.py:22
  11.6 149.1 %collective-permute-start.3 = (bf16[512,2048]{1,0:T(8,128)(2,1)}, bf16[512,2048]{1,0:T(8,128)(2,1)}, u32[]{:S(2)}, u32[]{:S(2)}) collective-permute-start(bf16[512,2048]{1,0:T(8,128)(2,1)} %refs_5_.1), channel_id=1, source_target_pairs={{0,1},{1,2},{2,3},{3,4},{4,5},{5,6},{6,7},{7,8},{8,9},{9,10},{10,1... | collective-permute-start | bytes 6291464 | tf_op jit(solution)/shard_map/ppermute | solution.py:22
  160.7 1.4 copy-start

commit v2 on v1

--- a/solution.py
+++ b/solution.py
@@ -30,10 +30,8 @@
     return jnp.concatenate([cos, cos], -1), jnp.concatenate([-sin, sin], -1)
 
 
-def attend_kernel(pos_ref, cos_ref, sin_ref, q_ref, *refs, rows, hops):
-    k_refs = refs[:hops + 1]
-    v_refs = refs[hops + 1:2 * hops + 2]
-    o_ref = refs[2 * hops + 2]
+def attend_kernel(par_ref, pos_ref, cos_ref, sin_ref, q_ref, k2a, k2b, k1, k0, v2a, v2b, v1, v0,
+                  o_ref, *, rows, hops):
     span = (hops + 1) * rows
     cos = cos_ref[...]
     sin = sin_ref[...]
@@ -41,9 +39,12 @@
     def rot(x, c, s):
         return x * c + pltpu.roll(x, HD // 2, 1) * s
 
-    k = jnp.concatenate([r[...] for r in k_refs], 0).astype(jnp.float32)
+    even = par_ref[0] == 0
+    k2 = jnp.where(even, k2a[...], k2b[...])
+    v2 = jnp.where(even, v2a[...], v2b[...])
+    k = jnp.concatenate([k2, k1[...], k0[...]], 0).astype(jnp.float32)
     k = rot(k, cos, sin).astype(jnp.bfloat16)
-    v = jnp.concatenate([r[...] for r in v_refs], 0)
+    v = jnp.concatenate([v2, v1[...], v0[...]], 0)
     qc = cos[span - rows:]
     qs = sin[span - rows:]
     dp = pos_ref[...]
@@ -66,10 +67,15 @@
 def local(queries, keys, values, segment_ids):
     rows = queries.shape[0]
     hops = W // rows
+    assert hops == 2
     span = (hops + 1) * rows
     shard = lax.axis_index("seq")
-    tails = [passed_along((keys, values), "seq", d) for d in range(hops, 0, -1)]
+    count = lax.axis_size("seq")
     seg_all = lax.all_gather(segment_ids, "seq", tiled=True)
+    keys, values, seg_all = lax.optimization_barrier((keys, values, seg_all))
+    near = lax.ppermute((keys, values), "seq", [(s, s + 1) for s in range(count - 1)])
+    far = lax.ppermute((keys, values), "seq", [(s, s + 2) for s in range(0, count - 2, 2)])
+    relay = lax.ppermute(near, "seq", [(s, s + 1) for s in range(0, count - 1, 2)])
     total = seg_all.shape[0]
     places = jnp.arange(total, dtype=jnp.int32)
     previous = jnp.concatenate([seg_all[:1], seg_all[:-1]])
@@ -79,22 +85,25 @@
     pos_win = lax.dynamic_slice_in_dim(pos_all, shard * rows, span, 0)
     cos, sin = rope_tables(pos_win)
     pos_q = pos_win[span - rows:].reshape(rows, 1)
-    k_list = [t[0] for t in tails] + [keys]
-    v_list = [t[1] for t in tails] + [values]
-    kv_spec = pl.BlockSpec((rows, HD), lambda h: (0, h))
-    full = lambda shape: pl.BlockSpec(shape, lambda h: (0, 0))
+    parity = (shard % 2).astype(jnp.int32).reshape(1)
+    kv_spec = pl.BlockSpec((rows, HD), lambda h, p: (0, h))
+    full = lambda shape: pl.BlockSpec(shape, lambda h, p: (0, 0))
     kernel = functools.partial(attend_kernel, rows=rows, hops=hops)
     heads = keys.shape[1] // HD
+    grid_spec = pltpu.PrefetchScalarGridSpec(
+        num_scalar_prefetch=1,
+        grid=(heads,),
+        in_specs=[full((rows, 1)), full((span, HD)), full((span, HD)),
+                  pl.BlockSpec((rows, 2 * HD), lambda h, p: (0, h))] + [kv_spec] * 8,
+        out_specs=pl.BlockSpec((rows, 2 * HD), lambda h, p: (0, h)),
+    )
     return pl.pallas_call(
         kernel,
-        grid=(heads,),
-        in_specs=[full((rows, 1)), full((span, HD)), full((span, HD)),
-                  pl.BlockSpec((rows, 2 * HD), lambda h: (0, h))]
-        + [kv_spec] * (2 * hops + 2),
-        out_specs=pl.BlockSpec((rows, 2 * HD), lambda h: (0, h)),
+        grid_spec=grid_spec,
         out_shape=jax.ShapeDtypeStruct(queries.shape, jnp.bfloat16),
         compiler_params=pltpu.CompilerParams(dimension_semantics=("arbitrary",)),
-    )(pos_q, cos, sin, queries, *k_list, *v_list)
+    )(parity, pos_q, cos, sin, queries, far[0], relay[0], near[0], keys,
+      far[1], relay[1], near[1], values)
 
 
 def solution(mesh):

time: 227 us -> 187 us (0.82)
  blocking collectives: 137 us -> 23.4 us
  starting transfers between devices: 16.2 us -> 90.8 us
    all_gather x1, blocking collectives: 137 us -> 23.4 us  [local(): seg_all = lax.all_gather(segment_ids, 'seq', tiled=True)]
    ppermute x4 -> x6, starting transfers between devices: 16.2 us -> 90.8 us  [the longest x2 80 us: local(): lax.ppermute(near, 'seq', [(s, s + 1) for s in range(0, count - 1, 2)])]
  transfers between devices with their start and end apart: 4 -> 6, of which waited for: 0 -> 0; matrix products, arithmetic and copies ran while one was open for 3% -> 4% of each run, Pallas kernels for 0% -> 0%
where the time goes in v2:
time: 187 us
  starting transfers between devices  90.8 us (49%)
  Pallas kernels  65.1 us (35%)
  blocking collectives  23.4 us (13%)
  other arithmetic  5.77 us (3%)
    ppermute x2, starting transfers between devices, local(): lax.ppermute(near, 'seq', [(s, s + 1) for s in range(0, count - 1, 2)])  80 us
    pallas_call x1, Pallas kernels, local(): pl.pallas_call(kernel, grid_spec=grid_spec, out_shape=jax.ShapeDtypeStruc...  65.1 us
    all_gather x1, blocking collectives, local(): seg_all = lax.all_gather(segment_ids, 'seq', tiled=True)  23.4 us
    ppermute x2, starting transfers between devices, local(): lax.ppermute((keys, values), 'seq', [(s, s + 1) for s in range(count - 1)])  5.56 us
    ppermute x2, starting transfers between devices, local(): lax.ppermute((keys, values), 'seq', [(s, s + 2) for s in range(0, count -...  5.26 us
  transfers between devices with their start and end apart: 6, of which 0 were waited for; matrix products, arithmetic and copies ran while one was open for 4% of the time, Pallas kernels for 0%

profile of v2, /device:TPU:0, one launch (start us, length us, event | category | flops | bytes accessed | tf_op | source)
XLA Modules:
  0.0 186.8 jit_solution(5296464631747442434)
XLA Ops:
  0.0 23.4 %all-gather = s32[16,1,512]{2,1,0:T(1,128)S(1)} all-gather(s32[1,1,512]{2,1,0:T(1,128)} %bitcast.13), channel_id=1, replica_groups=mesh['grp'=2,'seq'=16] {'seq'}, dimensions={0}, use_global_device_ids=true | all-gather | bytes 34816 | tf_op jit(solution)/shard_map/all_gather | solution.py:74
  23.4 2.4 %collective-permute-start.1 = (bf16[512,2048]{1,0:T(8,128)(2,1)}, bf16[512,2048]{1,0:T(8,128)(2,1)S(1)}, u32[]{:S(2)}, u32[]{:S(2)}) collective-permute-start(bf16[512,2048]{1,0:T(8,128)(2,1)} %k0), channel_id=1, source_target_pairs={{0,1},{1,2},{2,3},{3,4},{4,5},{5,6},{6,7},{7,8},{8,9},{9,10},{10,1... | collective-permute-start | bytes 6291464 | tf_op jit(solution)/shard_map/ppermute | solution.py:76
  25.8 3.2 %collective-permute-start.4 = (bf16[512,2048]{1,0:T(8,128)(2,1)}, bf16[512,2048]{1,0:T(8,128)(2,1)}, u32[]{:S(2)}, u32[]{:S(2)}) collective-permute-start(bf16[512,2048]{1,0:T(8,128)(2,1)} %v0), channel_id=1, source_target_pairs={{0,1},{1,2},{2,3},{3,4},{4,5},{5,6},{6,7},{7,8},{8,9},{9,10},{10,1... | collective-permute-start | bytes 6291464 | tf_op jit(solution)/shard_map/ppermute | solution.py:76
  29.0 2.6 %collective-permute-start = (bf16[512,2048]{1,0:T(8,128)(2,1)}, bf16[512,2048]{1,0:T(8,128)(2,1)}, u32[]{:S(2)}, u32[]{:S(2)}) collective-permute-start(bf16[512,2048]{1,0:T(8,128)(2,1)} %k0), channel_id=1, source_target_pairs={{0,2},{2,4},{4,6},{6,8},{8,10},{10,12},{12,14},{16,18},{18,20},{20... | collective-permute-start | bytes 6291464 | tf_op jit(solution)/shard_map/ppermute | solution.py:77
  31.6 2.6 %collective-permute-start.3 = (bf16[512,2048]{1,0:T(8,128)(2,1)}, bf16[512,2048]{1,0:T(8,128)(2,1)}, u32[]{:S(2)}, u32[]{:S(2)}) collective-permute-start(bf16[512,2048]{1,0:T(8,128)(2,1)} %v0), channel_id=1, source_target_pairs={{0,2},{2,4},{4,6},{6,8},{8,10},{10,12},{12,14},{16,18},{18,20},{20... | collective-permute-start | bytes 6291464 | tf_op jit(solution)/shard_map/ppermute | solution.py:77
  34.3 0.0 collective-permute-done.1.k1
  34.3 0.0 copy-start
  34.3 35.1 %collective-permute-start.2 = (bf16[512,2048]{1,0:T(8,128)(2,1)S(1)}, bf16[512,2048]{1,0:T(8,128)(2,1)}, u32[]{:S(2)}, u32[]{:S(2)}) collective-permute-start(bf16[512,2048]{1,0:T(8,128)(2,1)S(1)} %collective-permute-done.1.k1), channel_id=1, source_target_pairs={{0,1},{2,3},{4,5},{6,7},{8,9},{10,11},{12,13},{14,15},{16,17},{18,... | collective-permute-start | bytes 6291464 | tf_op jit(solution)/shard_map/ppermute | solution.py:78
  69.3 0.0 collective-permute-done.4.v1
  69.4 44.9 %collective-permute-start.5 = (bf16[512,2048]{1,0:T(8,128)(2,1)}, bf16[512,2048]{1,0:T(8,128)(2,1)}, u32[]{:S(2)}, u32[]{:S(2)}) collective-permute-start(bf16[512,2048]{1,0:T(8,128)(2,1)} %collective-permute-done.4.v1), channel_id=1, source_target_pairs={{0,1},{2,3},{4,5},{6,7},{8,9},{10,11},{12,13},{14,15},{16,17},{18,... | collective-permute-start | bytes 6291464 | tf_op jit(solution)/shard_map/ppermute | solution.py:78
  114.3 0.5 slice.16
  114.8 0.7 select_bitcast_fusion
  115.5 0.3 reduce-window.9
  115.8 0.1 slice.21
  115.9 0.1 reduce-window.12
  116.0 0.1 slice_reduce_fusion
  116.1 0.1 bitcast_subtract_fusion
  116.2 0.1 pad_dynamic-slice_fusion
  116.3 0.9 copy.6.pos_ref
  117.2 0.1 fusion.2
  117.2 2.8 %fusion = (f32[1536,64]{1,0:T(8,128)S(1)}, f32[1536,64]{1,0:T(8,128)S(1)}, f32[1536,64]{1,0:T(8,128)S(1)}) fusion(f32[64]{0:T(128)S(1)} %multiply_power_fusion, f32[1536]{0:T(1024)S(1)} %fusion.2), kind=kLoop, calls=%fused_computation.4 | loop fusion | flops 196608 | bytes 1186048 | tf_op jit(solution)/shard_map/neg | solution.py:30
  120.1 1.7 pad_maximum_fusion
  121.7 0.0 copy-done
  121.7 0.0 collective-permute-done.k2a
  121.7 0.0 collective-permute-done.3.v2a
  121.7 0.0 collective-permute-done.2.k2b
  121.7 0.0 collective-permute-done.5.v2b
  121.8 65.1 %shard_map.46 = bf16[512,4096]{1,0:T(8,128)(2,1)} custom-call(s32[1]{0:T(128)} %bitcast.par_ref, s32[512,1]{1,0:T(8,128)} %copy.6.pos_ref, f32[1536,128]{1,0:T(8,128)} %get-tuple-element.14.cos_ref, f32[1536,128]{1,0:T(8,128)} %get-tuple-element.15.sin_ref, bf16[512,4096]{1,0:T(8,128)(2,1)} %q_ref.1, bf16[512,2048]{1,0:T(8,128)(2,1)} %collective-permute-done.k2a, ...), custom_call_target="tpu_custom_call" | custom-call | tf_op jit(solution)/shard_map/pallas_call | solution.py:100
  (1 shorter events, 0.0 us)
Async XLA Ops:
  23.4 10.8 %collective-permute-start.1 = (bf16[512,2048]{1,0:T(8,128)(2,1)}, bf16[512,2048]{1,0:T(8,128)(2,1)S(1)}, u32[]{:S(2)}, u32[]{:S(2)}) collective-permute-start(bf16[512,2048]{1,0:T(8,128)(2,1)} %k0), channel_id=1, source_target_pairs={{0,1},{1,2},{2,3},{3,4},{4,5},{5,6},{6,7},{7,8},{8,9},{9,10},{10,1... | collective-permute-start | bytes 6291464 | tf_op jit(solution)/shard_map/ppermute | solution.py:76
  25.8 43.5 %collective-permute-start.4 = (bf16[512,2048]{1,0:T(8,128)(2,1)}, bf16[512,2048]{1,0:T(8,128)(2,1)}, u32[]{:S(2)}, u32[]{:S(2)}) collective-permute-start(bf16[512,2048]{1,0:T(8,128)(2,1)} %v0), channel_id=1, source_target_pairs={{0,1},{1,2},{2,3},{3,4},{4,5},{5,6},{6,7},{7,8},{8,9},{9,10},{10,1... | collective-permute-start | bytes 6291464 | tf_op jit(solution)/shard_map/ppermute | solution.py:76
  29.0 92.7 %collective-permute-start = (bf16[512,2048]{1,0:T(8,128)(2,1)}, bf16[512,2048]{1,0:T(8,128)(2,1)}, u32[]{:S(2)}, u32[]{:S(2)}) collective-permute-start(bf16[512,2048]{1,0:T(8,128)(2,1)} %k0), channel_id=1, source_target_pairs={{0,2},{2,4},{4,6},{6,8},{8,10},{10,12},{12,14},{16,18},{18,20},{20... | collective-permute-start | bytes 6291464 | tf_op jit(solution)/shard_map/ppermute | solution.py:77
  31.6 90.1 %collective-permute-start.3 = (bf16[512,2048]{1,0:T(8,128)(2,1)}, bf16[512,2048]{1,0:T(8,128)(2,1)}, u32[]{:S(2)}, u32[]{:S(2)}) collective-permute-start(bf16[512,2048]{1,0:T(8,128)(2,1)} %v0), channel_id=1, source_target_pairs={{0,2},{2,4},{4,6},{6,8},{8,10},{10,12},{12,14},{16,18},{18,20},{20... | collective-permute-start | bytes 6291464 | tf_op jit(solution)/shard_map/ppermute | solution.py:77
  34.3 87.5 %copy-start = (bf16[512,2048]{1,0:T(8,128)(2,1)}, bf16[512,2048]{1,0:T(8,128)(2,1)S(1)}, u32[]{:S(2)}) copy-start(bf16[512,2048]{1,0:T(8,128)(2,1)S(1)} %collective-permute-done.1.k1) | copy-start | bytes 6291460
  34.3 87.5 %collective-permute-start.2 = (bf16[512,2048]{1,0:T(8,128)(2,1)S(1)}, bf16[512,2048]{1,0:T(8,128)(2,1)}, u32[]{:S(2)}, u32[]{:S(2)}) collective-permute-start(bf16[512,2048]{1,0:T(8,128)(2,1)S(1)} %collective-permute-done.1.k1), channel_id=1, source_target_pairs={{0,1},{2,3},{4,5},{6,7},{8,9},{10,11},{12,13},{14,15},{16,17},{18,... | collective-permute-start | bytes 6291464 | tf_op jit(solution)/shard_map/ppermute | solution.py:78
  69.4 52.4 %collective-permute-start.5 = (bf16[512,2048]{1,0:T(8,128)(2,1)}, bf16[512,2048]{1,0:T(8,128)(2,1)}, u32[]{:S(2)}, u32[]{:S(2)}) collective-permute-start(bf16[512,2048]{1,0:T(8,128)(2,1)} %collective-permute-done.4.v1), channel_id=1, source_target_pairs={{0,1},{2,3},{4,5},{6,7},{8,9},{10,11},{12,13},{14,15},{16,17},{18,... | collective-permute-start | bytes 6291464 | tf_op jit(solution)/shard_map/ppermute | solution.py:78

commit v3 on v2

--- a/solution.py
+++ b/solution.py
@@ -31,8 +31,21 @@
 
 
 def attend_kernel(par_ref, pos_ref, cos_ref, sin_ref, q_ref, k2a, k2b, k1, k0, v2a, v2b, v1, v0,
-                  o_ref, *, rows, hops):
+                  o_ref, bias_ref, *, rows, hops, tile):
     span = (hops + 1) * rows
+    band = W + tile
+    tiles = rows // tile
+
+    @pl.when(pl.program_id(0) == 0)
+    def _():
+        dp = pos_ref[...]
+        for a in range(tiles):
+            r = lax.broadcasted_iota(jnp.int32, (tile, band), 0)
+            c = lax.broadcasted_iota(jnp.int32, (tile, band), 1)
+            gap = W + r - c
+            vis = (gap >= 0) & (gap < W) & (gap <= dp[a * tile:(a + 1) * tile])
+            bias_ref[a] = jnp.where(vis, 0.0, -1e30).astype(jnp.float32)
+
     cos = cos_ref[...]
     sin = sin_ref[...]
 
@@ -45,23 +58,24 @@
     k = jnp.concatenate([k2, k1[...], k0[...]], 0).astype(jnp.float32)
     k = rot(k, cos, sin).astype(jnp.bfloat16)
     v = jnp.concatenate([v2, v1[...], v0[...]], 0)
-    qc = cos[span - rows:]
-    qs = sin[span - rows:]
-    dp = pos_ref[...]
-    r = lax.broadcasted_iota(jnp.int32, (rows, span), 0)
-    c = lax.broadcasted_iota(jnp.int32, (rows, span), 1)
-    gap = (span - rows) + r - c
-    vis = (gap >= 0) & (gap < W) & (gap <= dp)
-    for g in range(2):
-        q = q_ref[:, g * HD:(g + 1) * HD].astype(jnp.float32)
-        q = rot(q, qc, qs).astype(jnp.bfloat16)
-        s = lax.dot_general(q, k, (((1,), (1,)), ((), ())), preferred_element_type=jnp.float32)
-        s = jnp.where(vis, s * query_scale, -1e30)
-        m = jnp.max(s, axis=1, keepdims=True)
-        w = jnp.where(vis, jnp.exp(s - m), 0.0)
-        tot = jnp.sum(w, axis=1, keepdims=True)
-        pv = jnp.dot(w.astype(jnp.bfloat16), v, preferred_element_type=jnp.float32)
-        o_ref[:, g * HD:(g + 1) * HD] = (pv / tot).astype(jnp.bfloat16)
+    off = span - rows
+    for a in range(tiles):
+        lo = a * tile
+        kk = k[lo:lo + band]
+        vv = v[lo:lo + band]
+        bias = bias_ref[a]
+        qc = cos[off + lo:off + lo + tile]
+        qs = sin[off + lo:off + lo + tile]
+        for g in range(2):
+            q = q_ref[lo:lo + tile, g * HD:(g + 1) * HD].astype(jnp.float32)
+            q = rot(q, qc, qs).astype(jnp.bfloat16)
+            s = lax.dot_general(q, kk, (((1,), (1,)), ((), ())), preferred_element_type=jnp.float32)
+            s = s * query_scale + bias
+            m = jnp.max(s, axis=1, keepdims=True)
+            w = jnp.exp(s - m)
+            tot = jnp.sum(w, axis=1, keepdims=True)
+            pv = jnp.dot(w.astype(jnp.bfloat16), vv, preferred_element_type=jnp.float32)
+            o_ref[lo:lo + tile, g * HD:(g + 1) * HD] = (pv / tot).astype(jnp.bfloat16)
 
 
 def local(queries, keys, values, segment_ids):
@@ -88,7 +102,8 @@
     parity = (shard % 2).astype(jnp.int32).reshape(1)
     kv_spec = pl.BlockSpec((rows, HD), lambda h, p: (0, h))
     full = lambda shape: pl.BlockSpec(shape, lambda h, p: (0, 0))
-    kernel = functools.partial(attend_kernel, rows=rows, hops=hops)
+    tile = 128
+    kernel = functools.partial(attend_kernel, rows=rows, hops=hops, tile=tile)
     heads = keys.shape[1] // HD
     grid_spec = pltpu.PrefetchScalarGridSpec(
         num_scalar_prefetch=1,
@@ -96,6 +111,7 @@
         in_specs=[full((rows, 1)), full((span, HD)), full((span, HD)),
                   pl.BlockSpec((rows, 2 * HD), lambda h, p: (0, h))] + [kv_spec] * 8,
         out_specs=pl.BlockSpec((rows, 2 * HD), lambda h, p: (0, h)),
+        scratch_shapes=[pltpu.VMEM((rows // tile, tile, W + tile), jnp.float32)],
     )
     return pl.pallas_call(
         kernel,

time: 187 us -> 181 us (0.968)
  Pallas kernels: 65.1 us -> 58.8 us
    pallas_call x1, Pallas kernels: 65.1 us -> 58.8 us  [local(): pl.pallas_call(kernel, grid_spec=grid_spec, out_shape=jax.ShapeDtypeStruc...]
where the time goes in v3:
time: 181 us
  starting transfers between devices  90.8 us (50%)
  Pallas kernels  58.8 us (32%)
  blocking collectives  23.4 us (13%)
  other arithmetic  5.77 us (3%)
    ppermute x2, starting transfers between devices, local(): lax.ppermute(near, 'seq', [(s, s + 1) for s in range(0, count - 1, 2)])  80 us
    pallas_call x1, Pallas kernels, local(): pl.pallas_call(kernel, grid_spec=grid_spec, out_shape=jax.ShapeDtypeStruc...  58.8 us
    all_gather x1, blocking collectives, local(): seg_all = lax.all_gather(segment_ids, 'seq', tiled=True)  23.4 us
    ppermute x2, starting transfers between devices, local(): lax.ppermute((keys, values), 'seq', [(s, s + 1) for s in range(count - 1)])  5.56 us
    ppermute x2, starting transfers between devices, local(): lax.ppermute((keys, values), 'seq', [(s, s + 2) for s in range(0, count -...  5.26 us
  transfers between devices with their start and end apart: 6, of which 0 were waited for; matrix products, arithmetic and copies ran while one was open for 4% of the time, Pallas kernels for 0%

profile of v3, /device:TPU:0, one launch (start us, length us, event | category | flops | bytes accessed | tf_op | source)
XLA Modules:
  0.0 180.5 jit_solution(4624421146466142818)
XLA Ops:
  0.0 23.4 %all-gather = s32[16,1,512]{2,1,0:T(1,128)S(1)} all-gather(s32[1,1,512]{2,1,0:T(1,128)} %bitcast.13), channel_id=1, replica_groups=mesh['grp'=2,'seq'=16] {'seq'}, dimensions={0}, use_global_device_ids=true | all-gather | bytes 34816 | tf_op jit(solution)/shard_map/all_gather | solution.py:88
  23.4 2.4 %collective-permute-start.1 = (bf16[512,2048]{1,0:T(8,128)(2,1)}, bf16[512,2048]{1,0:T(8,128)(2,1)S(1)}, u32[]{:S(2)}, u32[]{:S(2)}) collective-permute-start(bf16[512,2048]{1,0:T(8,128)(2,1)} %k0), channel_id=1, source_target_pairs={{0,1},{1,2},{2,3},{3,4},{4,5},{5,6},{6,7},{7,8},{8,9},{9,10},{10,1... | collective-permute-start | bytes 6291464 | tf_op jit(solution)/shard_map/ppermute | solution.py:90
  25.8 3.2 %collective-permute-start.4 = (bf16[512,2048]{1,0:T(8,128)(2,1)}, bf16[512,2048]{1,0:T(8,128)(2,1)}, u32[]{:S(2)}, u32[]{:S(2)}) collective-permute-start(bf16[512,2048]{1,0:T(8,128)(2,1)} %v0), channel_id=1, source_target_pairs={{0,1},{1,2},{2,3},{3,4},{4,5},{5,6},{6,7},{7,8},{8,9},{9,10},{10,1... | collective-permute-start | bytes 6291464 | tf_op jit(solution)/shard_map/ppermute | solution.py:90
  29.0 2.6 %collective-permute-start = (bf16[512,2048]{1,0:T(8,128)(2,1)}, bf16[512,2048]{1,0:T(8,128)(2,1)}, u32[]{:S(2)}, u32[]{:S(2)}) collective-permute-start(bf16[512,2048]{1,0:T(8,128)(2,1)} %k0), channel_id=1, source_target_pairs={{0,2},{2,4},{4,6},{6,8},{8,10},{10,12},{12,14},{16,18},{18,20},{20... | collective-permute-start | bytes 6291464 | tf_op jit(solution)/shard_map/ppermute | solution.py:91
  31.6 2.6 %collective-permute-start.3 = (bf16[512,2048]{1,0:T(8,128)(2,1)}, bf16[512,2048]{1,0:T(8,128)(2,1)}, u32[]{:S(2)}, u32[]{:S(2)}) collective-permute-start(bf16[512,2048]{1,0:T(8,128)(2,1)} %v0), channel_id=1, source_target_pairs={{0,2},{2,4},{4,6},{6,8},{8,10},{10,12},{12,14},{16,18},{18,20},{20... | collective-permute-start | bytes 6291464 | tf_op jit(solution)/shard_map/ppermute | solution.py:91
  34.3 0.0 collective-permute-done.1.k1
  34.3 0.0 copy-start
  34.3 35.1 %collective-permute-start.2 = (bf16[512,2048]{1,0:T(8,128)(2,1)S(1)}, bf16[512,2048]{1,0:T(8,128)(2,1)}, u32[]{:S(2)}, u32[]{:S(2)}) collective-permute-start(bf16[512,2048]{1,0:T(8,128)(2,1)S(1)} %collective-permute-done.1.k1), channel_id=1, source_target_pairs={{0,1},{2,3},{4,5},{6,7},{8,9},{10,11},{12,13},{14,15},{16,17},{18,... | collective-permute-start | bytes 6291464 | tf_op jit(solution)/shard_map/ppermute | solution.py:92
  69.3 0.0 collective-permute-done.4.v1
  69.4 44.9 %collective-permute-start.5 = (bf16[512,2048]{1,0:T(8,128)(2,1)}, bf16[512,2048]{1,0:T(8,128)(2,1)}, u32[]{:S(2)}, u32[]{:S(2)}) collective-permute-start(bf16[512,2048]{1,0:T(8,128)(2,1)} %collective-permute-done.4.v1), channel_id=1, source_target_pairs={{0,1},{2,3},{4,5},{6,7},{8,9},{10,11},{12,13},{14,15},{16,17},{18,... | collective-permute-start | bytes 6291464 | tf_op jit(solution)/shard_map/ppermute | solution.py:92
  114.3 0.5 slice.16
  114.8 0.7 select_bitcast_fusion
  115.5 0.3 reduce-window.9
  115.8 0.1 slice.21
  115.9 0.1 reduce-window.12
  116.0 0.1 slice_reduce_fusion
  116.1 0.1 bitcast_subtract_fusion
  116.2 0.1 pad_dynamic-slice_fusion
  116.3 0.9 copy.6.pos_ref
  117.2 0.1 fusion.2
  117.2 2.8 %fusion = (f32[1536,64]{1,0:T(8,128)S(1)}, f32[1536,64]{1,0:T(8,128)S(1)}, f32[1536,64]{1,0:T(8,128)S(1)}) fusion(f32[64]{0:T(128)S(1)} %multiply_power_fusion, f32[1536]{0:T(1024)S(1)} %fusion.2), kind=kLoop, calls=%fused_computation.4 | loop fusion | flops 196608 | bytes 1186048 | tf_op jit(solution)/shard_map/neg | solution.py:30
  120.1 1.7 pad_maximum_fusion
  121.7 0.0 copy-done
  121.7 0.0 collective-permute-done.k2a
  121.7 0.0 collective-permute-done.3.v2a
  121.7 0.0 collective-permute-done.2.k2b
  121.7 0.0 collective-permute-done.5.v2b
  121.8 58.8 %shard_map.46 = bf16[512,4096]{1,0:T(8,128)(2,1)} custom-call(s32[1]{0:T(128)} %bitcast.par_ref, s32[512,1]{1,0:T(8,128)} %copy.6.pos_ref, f32[1536,128]{1,0:T(8,128)} %get-tuple-element.14.cos_ref, f32[1536,128]{1,0:T(8,128)} %get-tuple-element.15.sin_ref, bf16[512,4096]{1,0:T(8,128)(2,1)} %q_ref.1, bf16[512,2048]{1,0:T(8,128)(2,1)} %collective-permute-done.k2a, ...), custom_call_target="tpu_custom_call" | custom-call | tf_op jit(solution)/shard_map/pallas_call | solution.py:116
  (1 shorter events, 0.0 us)
Async XLA Ops:
  23.4 10.8 %collective-permute-start.1 = (bf16[512,2048]{1,0:T(8,128)(2,1)}, bf16[512,2048]{1,0:T(8,128)(2,1)S(1)}, u32[]{:S(2)}, u32[]{:S(2)}) collective-permute-start(bf16[512,2048]{1,0:T(8,128)(2,1)} %k0), channel_id=1, source_target_pairs={{0,1},{1,2},{2,3},{3,4},{4,5},{5,6},{6,7},{7,8},{8,9},{9,10},{10,1... | collective-permute-start | bytes 6291464 | tf_op jit(solution)/shard_map/ppermute | solution.py:90
  25.8 43.5 %collective-permute-start.4 = (bf16[512,2048]{1,0:T(8,128)(2,1)}, bf16[512,2048]{1,0:T(8,128)(2,1)}, u32[]{:S(2)}, u32[]{:S(2)}) collective-permute-start(bf16[512,2048]{1,0:T(8,128)(2,1)} %v0), channel_id=1, source_target_pairs={{0,1},{1,2},{2,3},{3,4},{4,5},{5,6},{6,7},{7,8},{8,9},{9,10},{10,1... | collective-permute-start | bytes 6291464 | tf_op jit(solution)/shard_map/ppermute | solution.py:90
  29.0 92.7 %collective-permute-start = (bf16[512,2048]{1,0:T(8,128)(2,1)}, bf16[512,2048]{1,0:T(8,128)(2,1)}, u32[]{:S(2)}, u32[]{:S(2)}) collective-permute-start(bf16[512,2048]{1,0:T(8,128)(2,1)} %k0), channel_id=1, source_target_pairs={{0,2},{2,4},{4,6},{6,8},{8,10},{10,12},{12,14},{16,18},{18,20},{20... | collective-permute-start | bytes 6291464 | tf_op jit(solution)/shard_map/ppermute | solution.py:91
  31.6 90.1 %collective-permute-start.3 = (bf16[512,2048]{1,0:T(8,128)(2,1)}, bf16[512,2048]{1,0:T(8,128)(2,1)}, u32[]{:S(2)}, u32[]{:S(2)}) collective-permute-start(bf16[512,2048]{1,0:T(8,128)(2,1)} %v0), channel_id=1, source_target_pairs={{0,2},{2,4},{4,6},{6,8},{8,10},{10,12},{12,14},{16,18},{18,20},{20... | collective-permute-start | bytes 6291464 | tf_op jit(solution)/shard_map/ppermute | solution.py:91
  34.3 87.5 %copy-start = (bf16[512,2048]{1,0:T(8,128)(2,1)}, bf16[512,2048]{1,0:T(8,128)(2,1)S(1)}, u32[]{:S(2)}) copy-start(bf16[512,2048]{1,0:T(8,128)(2,1)S(1)} %collective-permute-done.1.k1) | copy-start | bytes 6291460
  34.3 87.5 %collective-permute-start.2 = (bf16[512,2048]{1,0:T(8,128)(2,1)S(1)}, bf16[512,2048]{1,0:T(8,128)(2,1)}, u32[]{:S(2)}, u32[]{:S(2)}) collective-permute-start(bf16[512,2048]{1,0:T(8,128)(2,1)S(1)} %collective-permute-done.1.k1), channel_id=1, source_target_pairs={{0,1},{2,3},{4,5},{6,7},{8,9},{10,11},{12,13},{14,15},{16,17},{18,... | collective-permute-start | bytes 6291464 | tf_op jit(solution)/shard_map/ppermute | solution.py:92
  69.4 52.4 %collective-permute-start.5 = (bf16[512,2048]{1,0:T(8,128)(2,1)}, bf16[512,2048]{1,0:T(8,128)(2,1)}, u32[]{:S(2)}, u32[]{:S(2)}) collective-permute-start(bf16[512,2048]{1,0:T(8,128)(2,1)} %collective-permute-done.4.v1), channel_id=1, source_target_pairs={{0,1},{2,3},{4,5},{6,7},{8,9},{10,11},{12,13},{14,15},{16,17},{18,... | collective-permute-start | bytes 6291464 | tf_op jit(solution)/shard_map/ppermute | solution.py:92

commit v4 on v3

v4 whole, which is shorter than its diff:
```python
import functools

import jax
import jax.numpy as jnp
from jax import lax
from jax.experimental import pallas as pl
from jax.experimental.pallas import tpu as pltpu
from jax.sharding import PartitionSpec as P

H = 32
KVH = 16
HD = 128
W = 1024


query_scale = 168.0 ** (-0.5)


def passed_along(value, axis, steps):
    count = lax.axis_size(axis)
    first, last = (max(0, -steps), min(count, count - steps))
    return lax.ppermute(value, axis, [(source, source + steps) for source in range(first, last)])


def rope_tables(doc_pos):
    half = HD // 2
    freqs = 10000.0 ** (-2.0 * jnp.arange(half, dtype=jnp.float32) / HD)
    angles = doc_pos.astype(jnp.float32)[:, None] * freqs[None, :]
    cos, sin = jnp.cos(angles), jnp.sin(angles)
    return jnp.concatenate([cos, cos], -1), jnp.concatenate([-sin, sin], -1)


def attend_kernel(par_ref, pos_ref, cos_ref, sin_ref, q_ref, *refs, rows, tile, first, final):
    if final:
        k2a, k2b, v2a, v2b, m_in, l_in, acc_in, o_ref, bias_ref = refs
    else:
        k1, k0, v1, v0, m_out, l_out, acc_out, bias_ref = refs
    tiles = rows // tile
    nkeys = bias_ref.shape[2]
    qoff = W

    def bounds(a):
        lo = max(0, a * tile - first)
        hi = min(nkeys, a * tile + W + tile - first)
        return lo, hi

    @pl.when(pl.program_id(0) == 0)
    def _():
        dp = pos_ref[...]
        for a in range(tiles):
            r = lax.broadcasted_iota(jnp.int32, (tile, nkeys), 0) + a * tile
            c = lax.broadcasted_iota(jnp.int32, (tile, nkeys), 1) + first
            gap = qoff + r - c
            vis = (gap >= 0) & (gap < W) & (gap <= dp[a * tile:(a + 1) * tile])
            bias_ref[a] = jnp.where(vis, 0.0, -1e30).astype(jnp.float32)

    cos = cos_ref[...]
    sin = sin_ref[...]

    def rot(x, c, s):
        return x * c + pltpu.roll(x, HD // 2, 1) * s

    if final:
        even = par_ref[0] == 0
        k = jnp.where(even, k2a[...], k2b[...])
        v = jnp.where(even, v2a[...], v2b[...])
    else:
        k = jnp.concatenate([k1[...], k0[...]], 0)
        v = jnp.concatenate([v1[...], v0[...]], 0)
    k = rot(k.astype(jnp.float32), cos[first:first + nkeys], sin[first:first + nkeys])
    k = k.astype(jnp.bfloat16)
    for a in range(tiles):
        lo, hi = bounds(a)
        r0 = a * tile
        kk = k[lo:hi]
        vv = v[lo:hi]
        bias = bias_ref[a, :, lo:hi]
        qc = cos[qoff + r0:qoff + r0 + tile]
        qs = sin[qoff + r0:qoff + r0 + tile]
        for g in range(2):
            cols = slice(g * HD, (g + 1) * HD)
            q = q_ref[r0:r0 + tile, cols].astype(jnp.float32)
            q = rot(q, qc, qs).astype(jnp.bfloat16)
            s = lax.dot_general(q, kk, (((1,), (1,)), ((), ())), preferred_element_type=jnp.float32)
            s = s * query_scale + bias
            m = jnp.max(s, axis=1, keepdims=True)
            if final:
                m1 = m_in[g, r0:r0 + tile]
                mm = jnp.maximum(m, m1)
                scale1 = jnp.exp(m1 - mm)
                w = jnp.exp(s - mm)
                tot = jnp.sum(w, axis=1, keepdims=True) + l_in[g, r0:r0 + tile] * scale1
                pv = jnp.dot(w.astype(jnp.bfloat16), vv, preferred_element_type=jnp.float32)
                pv = pv + acc_in[r0:r0 + tile, cols] * scale1
                o_ref[r0:r0 + tile, cols] = (pv / tot).astype(jnp.bfloat16)
            else:
                w = jnp.exp(s - m)
                m_out[g, r0:r0 + tile] = m
                l_out[g, r0:r0 + tile] = jnp.sum(w, axis=1, keepdims=True)
                acc_out[r0:r0 + tile, cols] = jnp.dot(
                    w.astype(jnp.bfloat16), vv, preferred_element_type=jnp.float32)


def local(queries, keys, values, segment_ids):
    rows = queries.shape[0]
    hops = W // rows
    assert hops == 2
    span = (hops + 1) * rows
    shard = lax.axis_index("seq")
    count = lax.axis_size("seq")
    seg_all = lax.all_gather(segment_ids, "seq", tiled=True)
    keys, values, seg_all = lax.optimization_barrier((keys, values, seg_all))
    near = lax.ppermute((keys, values), "seq", [(s, s + 1) for s in range(count - 1)])
    keys_b, values_b, near = lax.optimization_barrier((keys, values, near))
    far = lax.ppermute((keys_b, values_b), "seq", [(s, s + 2) for s in range(0, count - 2, 2)])
    relay = lax.ppermute(near, "seq", [(s, s + 1) for s in range(0, count - 1, 2)])
    total = seg_all.shape[0]
    places = jnp.arange(total, dtype=jnp.int32)
    previous = jnp.concatenate([seg_all[:1], seg_all[:-1]])
    boundary = (seg_all != previous) | (places == 0)
    starts = lax.cummax(jnp.where(boundary, places, 0), axis=0)
    pos_all = jnp.concatenate([jnp.zeros((hops * rows,), jnp.int32), places - starts])
    pos_win = lax.dynamic_slice_in_dim(pos_all, shard * rows, span, 0)
    cos, sin = rope_tables(pos_win)
    pos_q = pos_win[span - rows:].reshape(rows, 1)
    parity = (shard % 2).astype(jnp.int32).reshape(1)
    tile = 128
    heads = keys.shape[1] // HD
    kv_spec = pl.BlockSpec((rows, HD), lambda h, p: (0, h))
    full = lambda shape: pl.BlockSpec(shape, lambda h, p: (0, 0))
    head_spec = pl.BlockSpec((rows, 2 * HD), lambda h, p: (0, h))
    stat_spec = pl.BlockSpec((2, rows, 1), lambda h, p: (h, 0, 0))
    lead = [full((rows, 1)), full((span, HD)), full((span, HD)), head_spec]
    params = pltpu.CompilerParams(dimension_semantics=("arbitrary",))
    f32 = jnp.float32
    stat_shape = jax.ShapeDtypeStruct((2 * heads, rows, 1), f32)
    m1, l1, acc1 = pl.pallas_call(
        functools.partial(attend_kernel, rows=rows, tile=tile, first=rows, final=False),
        grid_spec=pltpu.PrefetchScalarGridSpec(
            num_scalar_prefetch=1, grid=(heads,),
            in_specs=lead + [kv_spec] * 4,
            out_specs=[stat_spec, stat_spec, head_spec],
            scratch_shapes=[pltpu.VMEM((rows // tile, tile, 2 * rows), f32)]),
        out_shape=[stat_shape, stat_shape, jax.ShapeDtypeStruct(queries.shape, f32)],
        compiler_params=params,
    )(parity, pos_q, cos, sin, queries, near[0], keys, near[1], values)
    return pl.pallas_call(
        functools.partial(attend_kernel, rows=rows, tile=tile, first=0, final=True),
        grid_spec=pltpu.PrefetchScalarGridSpec(
            num_scalar_prefetch=1, grid=(heads,),
            in_specs=lead + [kv_spec] * 4 + [stat_spec, stat_spec, head_spec],
            out_specs=head_spec,
            scratch_shapes=[pltpu.VMEM((rows // tile, tile, rows), f32)]),
        out_shape=jax.ShapeDtypeStruct(queries.shape, jnp.bfloat16),
        compiler_params=params,
    )(parity, pos_q, cos, sin, queries, far[0], relay[0], far[1], relay[1], m1, l1, acc1)


def solution(mesh):
    return jax.shard_map(
        local,
        mesh=mesh,
        in_specs=(
            P(("grp", "seq"), None),
            P(("grp", "seq"), None),
            P(("grp", "seq"), None),
            P(("grp", "seq")),
        ),
        out_specs=P(("grp", "seq"), None),
        check_vma=False,
    )
```

time: 181 us -> 185 us (1.022)
  Pallas kernels: 58.8 us -> 92.3 us
  starting transfers between devices: 90.8 us -> 57.3 us
  waiting for transfers between devices: 0.02 us -> 3.17 us
    ppermute x2, starting transfers between devices: 80 us -> 43.3 us  [local(): lax.ppermute(near, 'seq', [(s, s + 1) for s in range(0, count - 1, 2)])]
    pallas_call x1 -> x2, Pallas kernels: 58.8 us -> 92.3 us  [local(): pl.pallas_call(functools.partial(attend_kernel, rows=rows, tile=tile, fir...]
    ppermute x2, waiting for transfers between devices: 0.01 us -> 3.16 us  [local(): lax.ppermute((keys, values), 'seq', [(s, s + 1) for s in range(count - 1)])]
    ppermute x2, starting transfers between devices: 5.26 us -> 7.76 us  [local(): lax.ppermute((keys_b, values_b), 'seq', [(s, s + 2) for s in range(0, cou...]
  transfers between devices with their start and end apart: 6 -> 6, of which waited for: 0 -> 2; matrix products, arithmetic and copies ran while one was open for 4% -> 4% of each run, Pallas kernels for 0% -> 27%
where the time goes in v4:
time: 185 us
  Pallas kernels  92.3 us (50%)
  starting transfers between devices  57.3 us (31%)
  blocking collectives  23.4 us (13%)
  other arithmetic  5.71 us (3%)
  waiting for transfers between devices  3.17 us (2%)
  local copies, waits for them, and re-layouts  2.92 us (2%)
    pallas_call x2, Pallas kernels, local(): pl.pallas_call(functools.partial(attend_kernel, rows=rows, tile=tile, fir...  92.3 us
    ppermute x2, starting transfers between devices, local(): lax.ppermute(near, 'seq', [(s, s + 1) for s in range(0, count - 1, 2)])  43.3 us
    all_gather x1, blocking collectives, local(): seg_all = lax.all_gather(segment_ids, 'seq', tiled=True)  23.4 us
    ppermute x2, starting transfers between devices, local(): lax.ppermute((keys_b, values_b), 'seq', [(s, s + 2) for s in range(0, cou...  7.76 us
    ppermute x2, starting transfers between devices, local(): lax.ppermute((keys, values), 'seq', [(s, s + 1) for s in range(count - 1)])  6.19 us
  transfers between devices with their start and end apart: 6, of which 2 were waited for; matrix products, arithmetic and copies ran while one was open for 4% of the time, Pallas kernels for 27%

profile of v4, /device:TPU:0, one launch (start us, length us, event | category | flops | bytes accessed | tf_op | source)
XLA Modules:
  0.0 184.9 jit_solution(7452401844938891497)
XLA Ops:
  0.0 23.4 %all-gather = s32[16,1,512]{2,1,0:T(1,128)S(1)} all-gather(s32[1,1,512]{2,1,0:T(1,128)} %bitcast.13), channel_id=1, replica_groups=mesh['grp'=2,'seq'=16] {'seq'}, dimensions={0}, use_global_device_ids=true | all-gather | bytes 34816 | tf_op jit(solution)/shard_map/all_gather | solution.py:111
  23.4 3.6 %collective-permute-start = (bf16[512,2048]{1,0:T(8,128)(2,1)}, bf16[512,2048]{1,0:T(8,128)(2,1)}, u32[]{:S(2)}, u32[]{:S(2)}) collective-permute-start(bf16[512,2048]{1,0:T(8,128)(2,1)} %refs_1_), channel_id=1, source_target_pairs={{0,1},{1,2},{2,3},{3,4},{4,5},{5,6},{6,7},{7,8},{8,9},{9,10},{10,1... | collective-permute-start | bytes 6291464 | tf_op jit(solution)/shard_map/ppermute | solution.py:113
  27.0 2.6 %collective-permute-start.1 = (bf16[512,2048]{1,0:T(8,128)(2,1)}, bf16[512,2048]{1,0:T(8,128)(2,1)}, u32[]{:S(2)}, u32[]{:S(2)}) collective-permute-start(bf16[512,2048]{1,0:T(8,128)(2,1)} %refs_3_), channel_id=1, source_target_pairs={{0,1},{1,2},{2,3},{3,4},{4,5},{5,6},{6,7},{7,8},{8,9},{9,10},{10,1... | collective-permute-start | bytes 6291464 | tf_op jit(solution)/shard_map/ppermute | solution.py:113
  29.6 0.2 collective-permute-done.refs_0_
  29.8 3.0 %collective-permute-done.1.refs_2_ = bf16[512,2048]{1,0:T(8,128)(2,1)} collective-permute-done((bf16[512,2048]{1,0:T(8,128)(2,1)}, bf16[512,2048]{1,0:T(8,128)(2,1)}, u32[]{:S(2)}, u32[]{:S(2)}) %collective-permute-start.1) | collective-permute-done | bytes 2097184 | tf_op jit(solution)/shard_map/ppermute | solution.py:113
  32.8 40.7 %collective-permute-start.3 = (bf16[512,2048]{1,0:T(8,128)(2,1)}, bf16[512,2048]{1,0:T(8,128)(2,1)S(1)}, u32[]{:S(2)}, u32[]{:S(2)}) collective-permute-start(bf16[512,2048]{1,0:T(8,128)(2,1)} %collective-permute-done.refs_0_), channel_id=1, source_target_pairs={{0,1},{2,3},{4,5},{6,7},{8,9},{10,11},{12,13},{14,15},{16,17},{18,... | collective-permute-start | bytes 6291464 | tf_op jit(solution)/shard_map/ppermute | solution.py:116
  73.5 2.6 %collective-permute-start.5 = (bf16[512,2048]{1,0:T(8,128)(2,1)}, bf16[512,2048]{1,0:T(8,128)(2,1)}, u32[]{:S(2)}, u32[]{:S(2)}) collective-permute-start(bf16[512,2048]{1,0:T(8,128)(2,1)} %collective-permute-done.1.refs_2_), channel_id=1, source_target_pairs={{0,1},{2,3},{4,5},{6,7},{8,9},{10,11},{12,13},{14,15},{16,17},{18,... | collective-permute-start | bytes 6291464 | tf_op jit(solution)/shard_map/ppermute | solution.py:116
  76.1 5.0 %collective-permute-start.2 = (bf16[512,2048]{1,0:T(8,128)(2,1)}, bf16[512,2048]{1,0:T(8,128)(2,1)}, u32[]{:S(2)}, u32[]{:S(2)}) collective-permute-start(bf16[512,2048]{1,0:T(8,128)(2,1)} %refs_1_), channel_id=1, source_target_pairs={{0,2},{2,4},{4,6},{6,8},{8,10},{10,12},{12,14},{16,18},{18,20},{20... | collective-permute-start | bytes 6291464 | tf_op jit(solution)/shard_map/ppermute | solution.py:115
  81.1 2.7 %collective-permute-start.4 = (bf16[512,2048]{1,0:T(8,128)(2,1)}, bf16[512,2048]{1,0:T(8,128)(2,1)}, u32[]{:S(2)}, u32[]{:S(2)}) collective-permute-start(bf16[512,2048]{1,0:T(8,128)(2,1)} %refs_3_), channel_id=1, source_target_pairs={{0,2},{2,4},{4,6},{6,8},{8,10},{10,12},{12,14},{16,18},{18,20},{20... | collective-permute-start | bytes 6291464 | tf_op jit(solution)/shard_map/ppermute | solution.py:115
  83.9 0.5 slice.16
  84.4 0.7 select_bitcast_fusion
  85.1 0.3 reduce-window.9
  85.4 0.1 slice.21
  85.5 0.1 reduce-window.12
  85.6 0.1 slice_reduce_fusion
  85.7 0.1 bitcast_subtract_fusion
  85.8 0.1 pad_dynamic-slice_fusion
  85.8 0.9 copy.8.pos_ref
  86.7 0.1 fusion.2
  86.8 2.8 %fusion = (f32[1536,64]{1,0:T(8,128)S(1)}, f32[1536,64]{1,0:T(8,128)S(1)}, f32[1536,64]{1,0:T(8,128)S(1)}) fusion(f32[64]{0:T(128)S(1)} %multiply_power_fusion, f32[1536]{0:T(1024)S(1)} %fusion.2), kind=kLoop, calls=%fused_computation.4 | loop fusion | flops 196608 | bytes 1186048 | tf_op jit(solution)/shard_map/neg | solution.py:30
  89.6 1.6 pad_maximum_fusion
  91.2 50.2 %shard_map.46 = (f32[32,512,1]{2,1,0:T(8,128)}, f32[32,512,1]{2,1,0:T(8,128)}, f32[512,4096]{1,0:T(8,128)}) custom-call(s32[1]{0:T(128)} %bitcast.par_ref, s32[512,1]{1,0:T(8,128)} %copy.8.pos_ref, f32[1536,128]{1,0:T(8,128)} %get-tuple-element.28.cos_ref, f32[1536,128]{1,0:T(8,128)} %get-tuple-element.29.sin_ref, bf16[512,4096]{1,0:T(8,128)(2,1)} %q_ref.3, ...), custom_call_target="tpu_custom_call" | custom-call | tf_op jit(solution)/shard_map/pallas_call | solution.py:137
  141.4 0.0 collective-permute-done.3.refs_1_
  141.4 0.0 copy-start
  141.4 0.0 collective-permute-done.5.refs_3_
  141.5 0.0 collective-permute-done.2.refs_0_
  141.5 0.0 collective-permute-done.4.refs_2_
  141.5 1.3 copy-done
  142.8 42.1 %shard_map.47 = bf16[512,4096]{1,0:T(8,128)(2,1)} custom-call(s32[1]{0:T(128)} %bitcast.par_ref, s32[512,1]{1,0:T(8,128)} %copy.8.pos_ref, f32[1536,128]{1,0:T(8,128)} %get-tuple-element.28.cos_ref, f32[1536,128]{1,0:T(8,128)} %get-tuple-element.29.sin_ref, bf16[512,4096]{1,0:T(8,128)(2,1)} %q_ref.3, bf16[512,2048]{1,0:T(8,128)(2,1)} %collective-permute-done.2.refs_0_, ...), custom_call_target="tpu_custom_call" | custom-call | tf_op jit(solution)/shard_map/pallas_call | solution.py:147
  (1 shorter events, 0.0 us)
Async XLA Ops:
  23.4 6.4 %collective-permute-start = (bf16[512,2048]{1,0:T(8,128)(2,1)}, bf16[512,2048]{1,0:T(8,128)(2,1)}, u32[]{:S(2)}, u32[]{:S(2)}) collective-permute-start(bf16[512,2048]{1,0:T(8,128)(2,1)} %refs_1_), channel_id=1, source_target_pairs={{0,1},{1,2},{2,3},{3,4},{4,5},{5,6},{6,7},{7,8},{8,9},{9,10},{10,1... | collective-permute-start | bytes 6291464 | tf_op jit(solution)/shard_map/ppermute | solution.py:113
  27.0 5.8 %collective-permute-start.1 = (bf16[512,2048]{1,0:T(8,128)(2,1)}, bf16[512,2048]{1,0:T(8,128)(2,1)}, u32[]{:S(2)}, u32[]{:S(2)}) collective-permute-start(bf16[512,2048]{1,0:T(8,128)(2,1)} %refs_3_), channel_id=1, source_target_pairs={{0,1},{1,2},{2,3},{3,4},{4,5},{5,6},{6,7},{7,8},{8,9},{9,10},{10,1... | collective-permute-start | bytes 6291464 | tf_op jit(solution)/shard_map/ppermute | solution.py:113
  32.8 108.7 %collective-permute-start.3 = (bf16[512,2048]{1,0:T(8,128)(2,1)}, bf16[512,2048]{1,0:T(8,128)(2,1)S(1)}, u32[]{:S(2)}, u32[]{:S(2)}) collective-permute-start(bf16[512,2048]{1,0:T(8,128)(2,1)} %collective-permute-done.refs_0_), channel_id=1, source_target_pairs={{0,1},{2,3},{4,5},{6,7},{8,9},{10,11},{12,13},{14,15},{16,17},{18,... | collective-permute-start | bytes 6291464 | tf_op jit(solution)/shard_map/ppermute | solution.py:116
  73.5 68.0 %collective-permute-start.5 = (bf16[512,2048]{1,0:T(8,128)(2,1)}, bf16[512,2048]{1,0:T(8,128)(2,1)}, u32[]{:S(2)}, u32[]{:S(2)}) collective-permute-start(bf16[512,2048]{1,0:T(8,128)(2,1)} %collective-permute-done.1.refs_2_), channel_id=1, source_target_pairs={{0,1},{2,3},{4,5},{6,7},{8,9},{10,11},{12,13},{14,15},{16,17},{18,... | collective-permute-start | bytes 6291464 | tf_op jit(solution)/shard_map/ppermute | solution.py:116
  76.1 65.4 %collective-permute-start.2 = (bf16[512,2048]{1,0:T(8,128)(2,1)}, bf16[512,2048]{1,0:T(8,128)(2,1)}, u32[]{:S(2)}, u32[]{:S(2)}) collective-permute-start(bf16[512,2048]{1,0:T(8,128)(2,1)} %refs_1_), channel_id=1, source_target_pairs={{0,2},{2,4},{4,6},{6,8},{8,10},{10,12},{12,14},{16,18},{18,20},{20... | collective-permute-start | bytes 6291464 | tf_op jit(solution)/shard_map/ppermute | solution.py:115
  81.1 60.3 %collective-permute-start.4 = (bf16[512,2048]{1,0:T(8,128)(2,1)}, bf16[512,2048]{1,0:T(8,128)(2,1)}, u32[]{:S(2)}, u32[]{:S(2)}) collective-permute-start(bf16[512,2048]{1,0:T(8,128)(2,1)} %refs_3_), channel_id=1, source_target_pairs={{0,2},{2,4},{4,6},{6,8},{8,10},{10,12},{12,14},{16,18},{18,20},{20... | collective-permute-start | bytes 6291464 | tf_op jit(solution)/shard_map/ppermute | solution.py:115
  141.4 1.3 copy-start

commit v5 on v3

--- a/solution.py
+++ b/solution.py
@@ -14,6 +14,7 @@
 
 
 query_scale = 168.0 ** (-0.5)
+exp2_scale = query_scale * 1.4426950408889634
 
 
 def passed_along(value, axis, steps):
@@ -70,9 +71,9 @@
             q = q_ref[lo:lo + tile, g * HD:(g + 1) * HD].astype(jnp.float32)
             q = rot(q, qc, qs).astype(jnp.bfloat16)
             s = lax.dot_general(q, kk, (((1,), (1,)), ((), ())), preferred_element_type=jnp.float32)
-            s = s * query_scale + bias
+            s = s + bias
             m = jnp.max(s, axis=1, keepdims=True)
-            w = jnp.exp(s - m)
+            w = jnp.exp2((s - m) * exp2_scale)
             tot = jnp.sum(w, axis=1, keepdims=True)
             pv = jnp.dot(w.astype(jnp.bfloat16), vv, preferred_element_type=jnp.float32)
             o_ref[lo:lo + tile, g * HD:(g + 1) * HD] = (pv / tot).astype(jnp.bfloat16)
@@ -85,9 +86,9 @@
     span = (hops + 1) * rows
     shard = lax.axis_index("seq")
     count = lax.axis_size("seq")
+    near = lax.ppermute((keys, values), "seq", [(s, s + 1) for s in range(count - 1)])
     seg_all = lax.all_gather(segment_ids, "seq", tiled=True)
     keys, values, seg_all = lax.optimization_barrier((keys, values, seg_all))
-    near = lax.ppermute((keys, values), "seq", [(s, s + 1) for s in range(count - 1)])
     far = lax.ppermute((keys, values), "seq", [(s, s + 2) for s in range(0, count - 2, 2)])
     relay = lax.ppermute(near, "seq", [(s, s + 1) for s in range(0, count - 1, 2)])
     total = seg_all.shape[0]

time: 181 us -> 170 us (0.939)
  starting transfers between devices: 90.8 us -> 18.9 us
  blocking collectives: 23.4 us -> 55.6 us
  waiting for transfers between devices: 0.02 us -> 29.6 us
    ppermute x2, starting transfers between devices: 80 us -> 5.19 us  [local(): lax.ppermute(near, 'seq', [(s, s + 1) for s in range(0, count - 1, 2)])]
    all_gather x1, blocking collectives: 23.4 us -> 55.6 us  [local(): seg_all = lax.all_gather(segment_ids, 'seq', tiled=True)]
    ppermute x2, waiting for transfers between devices: 0.01 us -> 29.6 us  [local(): lax.ppermute((keys, values), 'seq', [(s, s + 2) for s in range(0, count -...]
    ppermute x2, starting transfers between devices: 5.56 us -> 8.32 us  [local(): lax.ppermute((keys, values), 'seq', [(s, s + 1) for s in range(count - 1)])]
  transfers between devices with their start and end apart: 6 -> 6, of which waited for: 0 -> 2; matrix products, arithmetic and copies ran while one was open for 4% -> 4% of each run, Pallas kernels for 0% -> 0%
where the time goes in v5:
time: 170 us
  Pallas kernels  58 us (34%)
  blocking collectives  55.6 us (33%)
  waiting for transfers between devices  29.6 us (17%)
  starting transfers between devices  18.9 us (11%)
  other arithmetic  5.77 us (3%)
    pallas_call x1, Pallas kernels, local(): pl.pallas_call(kernel, grid_spec=grid_spec, out_shape=jax.ShapeDtypeStruc...  58 us
    all_gather x1, blocking collectives, local(): seg_all = lax.all_gather(segment_ids, 'seq', tiled=True)  55.6 us
    ppermute x2, waiting for transfers between devices, local(): lax.ppermute((keys, values), 'seq', [(s, s + 2) for s in range(0, count -...  29.6 us
    ppermute x2, starting transfers between devices, local(): lax.ppermute((keys, values), 'seq', [(s, s + 1) for s in range(count - 1)])  8.32 us
    ppermute x2, starting transfers between devices, local(): lax.ppermute((keys, values), 'seq', [(s, s + 2) for s in range(0, count -...  5.39 us
    ppermute x2, starting transfers between devices, local(): lax.ppermute(near, 'seq', [(s, s + 1) for s in range(0, count - 1, 2)])  5.19 us
  transfers between devices with their start and end apart: 6, of which 2 were waited for; matrix products, arithmetic and copies ran while one was open for 4% of the time, Pallas kernels for 0%

profile of v5, /device:TPU:0, one launch (start us, length us, event | category | flops | bytes accessed | tf_op | source)
XLA Modules:
  0.0 169.6 jit_solution(13728725418890895915)
XLA Ops:
  0.0 2.5 %collective-permute-start.1 = (bf16[512,2048]{1,0:T(8,128)(2,1)}, bf16[512,2048]{1,0:T(8,128)(2,1)S(1)}, u32[]{:S(2)}, u32[]{:S(2)}) collective-permute-start(bf16[512,2048]{1,0:T(8,128)(2,1)} %k0), channel_id=1, source_target_pairs={{0,1},{1,2},{2,3},{3,4},{4,5},{5,6},{6,7},{7,8},{8,9},{9,10},{10,1... | collective-permute-start | bytes 6291464 | tf_op jit(solution)/shard_map/ppermute | solution.py:89
  2.5 5.8 %collective-permute-start.4 = (bf16[512,2048]{1,0:T(8,128)(2,1)}, bf16[512,2048]{1,0:T(8,128)(2,1)}, u32[]{:S(2)}, u32[]{:S(2)}) collective-permute-start(bf16[512,2048]{1,0:T(8,128)(2,1)} %v0), channel_id=1, source_target_pairs={{0,1},{1,2},{2,3},{3,4},{4,5},{5,6},{6,7},{7,8},{8,9},{9,10},{10,1... | collective-permute-start | bytes 6291464 | tf_op jit(solution)/shard_map/ppermute | solution.py:89
  8.3 55.6 %all-gather = s32[16,1,512]{2,1,0:T(1,128)S(1)} all-gather(s32[1,1,512]{2,1,0:T(1,128)} %bitcast.13), channel_id=1, replica_groups=mesh['grp'=2,'seq'=16] {'seq'}, dimensions={0}, use_global_device_ids=true | all-gather | bytes 34816 | tf_op jit(solution)/shard_map/all_gather | solution.py:90
  63.9 2.6 %collective-permute-start = (bf16[512,2048]{1,0:T(8,128)(2,1)}, bf16[512,2048]{1,0:T(8,128)(2,1)}, u32[]{:S(2)}, u32[]{:S(2)}) collective-permute-start(bf16[512,2048]{1,0:T(8,128)(2,1)} %k0), channel_id=1, source_target_pairs={{0,2},{2,4},{4,6},{6,8},{8,10},{10,12},{12,14},{16,18},{18,20},{20... | collective-permute-start | bytes 6291464 | tf_op jit(solution)/shard_map/ppermute | solution.py:92
  66.5 2.8 %collective-permute-start.3 = (bf16[512,2048]{1,0:T(8,128)(2,1)}, bf16[512,2048]{1,0:T(8,128)(2,1)}, u32[]{:S(2)}, u32[]{:S(2)}) collective-permute-start(bf16[512,2048]{1,0:T(8,128)(2,1)} %v0), channel_id=1, source_target_pairs={{0,2},{2,4},{4,6},{6,8},{8,10},{10,12},{12,14},{16,18},{18,20},{20... | collective-permute-start | bytes 6291464 | tf_op jit(solution)/shard_map/ppermute | solution.py:92
  69.3 0.0 collective-permute-done.1.k1
  69.3 0.0 copy-start
  69.3 2.6 %collective-permute-start.2 = (bf16[512,2048]{1,0:T(8,128)(2,1)S(1)}, bf16[512,2048]{1,0:T(8,128)(2,1)}, u32[]{:S(2)}, u32[]{:S(2)}) collective-permute-start(bf16[512,2048]{1,0:T(8,128)(2,1)S(1)} %collective-permute-done.1.k1), channel_id=1, source_target_pairs={{0,1},{2,3},{4,5},{6,7},{8,9},{10,11},{12,13},{14,15},{16,17},{18,... | collective-permute-start | bytes 6291464 | tf_op jit(solution)/shard_map/ppermute | solution.py:93
  71.9 0.0 collective-permute-done.4.v1
  71.9 2.6 %collective-permute-start.5 = (bf16[512,2048]{1,0:T(8,128)(2,1)}, bf16[512,2048]{1,0:T(8,128)(2,1)}, u32[]{:S(2)}, u32[]{:S(2)}) collective-permute-start(bf16[512,2048]{1,0:T(8,128)(2,1)} %collective-permute-done.4.v1), channel_id=1, source_target_pairs={{0,1},{2,3},{4,5},{6,7},{8,9},{10,11},{12,13},{14,15},{16,17},{18,... | collective-permute-start | bytes 6291464 | tf_op jit(solution)/shard_map/ppermute | solution.py:93
  74.5 0.5 slice.16
  75.0 0.7 select_bitcast_fusion
  75.7 0.3 reduce-window.9
  76.0 0.1 slice.21
  76.1 0.1 reduce-window.12
  76.2 0.1 slice_reduce_fusion
  76.3 0.1 bitcast_subtract_fusion
  76.4 0.1 pad_dynamic-slice_fusion
  76.5 0.9 copy.6.pos_ref
  77.3 0.1 fusion.2
  77.4 2.8 %fusion = (f32[1536,64]{1,0:T(8,128)S(1)}, f32[1536,64]{1,0:T(8,128)S(1)}, f32[1536,64]{1,0:T(8,128)S(1)}) fusion(f32[64]{0:T(128)S(1)} %multiply_power_fusion, f32[1536]{0:T(1024)S(1)} %fusion.2), kind=kLoop, calls=%fused_computation.4 | loop fusion | flops 196608 | bytes 1186048 | tf_op jit(solution)/shard_map/neg | solution.py:31
  80.2 1.7 pad_maximum_fusion
  81.9 0.0 copy-done
  81.9 7.1 %collective-permute-done.k2a = bf16[512,2048]{1,0:T(8,128)(2,1)} collective-permute-done((bf16[512,2048]{1,0:T(8,128)(2,1)}, bf16[512,2048]{1,0:T(8,128)(2,1)}, u32[]{:S(2)}, u32[]{:S(2)}) %collective-permute-start) | collective-permute-done | bytes 2097184 | tf_op jit(solution)/shard_map/ppermute | solution.py:92
  89.0 22.5 %collective-permute-done.3.v2a = bf16[512,2048]{1,0:T(8,128)(2,1)} collective-permute-done((bf16[512,2048]{1,0:T(8,128)(2,1)}, bf16[512,2048]{1,0:T(8,128)(2,1)}, u32[]{:S(2)}, u32[]{:S(2)}) %collective-permute-start.3) | collective-permute-done | bytes 2097184 | tf_op jit(solution)/shard_map/ppermute | solution.py:92
  111.5 0.0 collective-permute-done.2.k2b
  111.5 0.0 collective-permute-done.5.v2b
  111.5 58.0 %shard_map.46 = bf16[512,4096]{1,0:T(8,128)(2,1)} custom-call(s32[1]{0:T(128)} %bitcast.par_ref, s32[512,1]{1,0:T(8,128)} %copy.6.pos_ref, f32[1536,128]{1,0:T(8,128)} %get-tuple-element.14.cos_ref, f32[1536,128]{1,0:T(8,128)} %get-tuple-element.15.sin_ref, bf16[512,4096]{1,0:T(8,128)(2,1)} %q_ref.1, bf16[512,2048]{1,0:T(8,128)(2,1)} %collective-permute-done.k2a, ...), custom_call_target="tpu_custom_call" | custom-call | tf_op jit(solution)/shard_map/pallas_call | solution.py:117
  (1 shorter events, 0.0 us)
Async XLA Ops:
  0.0 69.3 %collective-permute-start.1 = (bf16[512,2048]{1,0:T(8,128)(2,1)}, bf16[512,2048]{1,0:T(8,128)(2,1)S(1)}, u32[]{:S(2)}, u32[]{:S(2)}) collective-permute-start(bf16[512,2048]{1,0:T(8,128)(2,1)} %k0), channel_id=1, source_target_pairs={{0,1},{1,2},{2,3},{3,4},{4,5},{5,6},{6,7},{7,8},{8,9},{9,10},{10,1... | collective-permute-start | bytes 6291464 | tf_op jit(solution)/shard_map/ppermute | solution.py:89
  2.5 69.4 %collective-permute-start.4 = (bf16[512,2048]{1,0:T(8,128)(2,1)}, bf16[512,2048]{1,0:T(8,128)(2,1)}, u32[]{:S(2)}, u32[]{:S(2)}) collective-permute-start(bf16[512,2048]{1,0:T(8,128)(2,1)} %v0), channel_id=1, source_target_pairs={{0,1},{1,2},{2,3},{3,4},{4,5},{5,6},{6,7},{7,8},{8,9},{9,10},{10,1... | collective-permute-start | bytes 6291464 | tf_op jit(solution)/shard_map/ppermute | solution.py:89
  63.9 25.1 %collective-permute-start = (bf16[512,2048]{1,0:T(8,128)(2,1)}, bf16[512,2048]{1,0:T(8,128)(2,1)}, u32[]{:S(2)}, u32[]{:S(2)}) collective-permute-start(bf16[512,2048]{1,0:T(8,128)(2,1)} %k0), channel_id=1, source_target_pairs={{0,2},{2,4},{4,6},{6,8},{8,10},{10,12},{12,14},{16,18},{18,20},{20... | collective-permute-start | bytes 6291464 | tf_op jit(solution)/shard_map/ppermute | solution.py:92
  66.5 45.0 %collective-permute-start.3 = (bf16[512,2048]{1,0:T(8,128)(2,1)}, bf16[512,2048]{1,0:T(8,128)(2,1)}, u32[]{:S(2)}, u32[]{:S(2)}) collective-permute-start(bf16[512,2048]{1,0:T(8,128)(2,1)} %v0), channel_id=1, source_target_pairs={{0,2},{2,4},{4,6},{6,8},{8,10},{10,12},{12,14},{16,18},{18,20},{20... | collective-permute-start | bytes 6291464 | tf_op jit(solution)/shard_map/ppermute | solution.py:92
  69.3 12.6 %copy-start = (bf16[512,2048]{1,0:T(8,128)(2,1)}, bf16[512,2048]{1,0:T(8,128)(2,1)S(1)}, u32[]{:S(2)}) copy-start(bf16[512,2048]{1,0:T(8,128)(2,1)S(1)} %collective-permute-done.1.k1) | copy-start | bytes 6291460
  69.3 42.2 %collective-permute-start.2 = (bf16[512,2048]{1,0:T(8,128)(2,1)S(1)}, bf16[512,2048]{1,0:T(8,128)(2,1)}, u32[]{:S(2)}, u32[]{:S(2)}) collective-permute-start(bf16[512,2048]{1,0:T(8,128)(2,1)S(1)} %collective-permute-done.1.k1), channel_id=1, source_target_pairs={{0,1},{2,3},{4,5},{6,7},{8,9},{10,11},{12,13},{14,15},{16,17},{18,... | collective-permute-start | bytes 6291464 | tf_op jit(solution)/shard_map/ppermute | solution.py:93
  71.9 39.6 %collective-permute-start.5 = (bf16[512,2048]{1,0:T(8,128)(2,1)}, bf16[512,2048]{1,0:T(8,128)(2,1)}, u32[]{:S(2)}, u32[]{:S(2)}) collective-permute-start(bf16[512,2048]{1,0:T(8,128)(2,1)} %collective-permute-done.4.v1), channel_id=1, source_target_pairs={{0,1},{2,3},{4,5},{6,7},{8,9},{10,11},{12,13},{14,15},{16,17},{18,... | collective-permute-start | bytes 6291464 | tf_op jit(solution)/shard_map/ppermute | solution.py:93

commit v6 on v5

--- a/solution.py
+++ b/solution.py
@@ -87,10 +87,10 @@
     shard = lax.axis_index("seq")
     count = lax.axis_size("seq")
     near = lax.ppermute((keys, values), "seq", [(s, s + 1) for s in range(count - 1)])
-    seg_all = lax.all_gather(segment_ids, "seq", tiled=True)
-    keys, values, seg_all = lax.optimization_barrier((keys, values, seg_all))
     far = lax.ppermute((keys, values), "seq", [(s, s + 2) for s in range(0, count - 2, 2)])
     relay = lax.ppermute(near, "seq", [(s, s + 1) for s in range(0, count - 1, 2)])
+    segment_ids, near = lax.optimization_barrier((segment_ids, near))
+    seg_all = lax.all_gather(segment_ids, "seq", tiled=True)
     total = seg_all.shape[0]
     places = jnp.arange(total, dtype=jnp.int32)
     previous = jnp.concatenate([seg_all[:1], seg_all[:-1]])

time: 170 us -> 182 us (1.071)
  starting transfers between devices: 18.9 us -> 92.8 us
  blocking collectives: 55.6 us -> 23.7 us
  waiting for transfers between devices: 29.6 us -> 0.02 us
    ppermute x2, starting transfers between devices: 5.19 us -> 77.7 us  [local(): lax.ppermute(near, 'seq', [(s, s + 1) for s in range(0, count - 1, 2)])]
    all_gather x1, blocking collectives: 55.6 us -> 23.7 us  [local(): seg_all = lax.all_gather(segment_ids, 'seq', tiled=True)]
    ppermute x2, waiting for transfers between devices: 29.6 us -> 0.01 us  [local(): lax.ppermute((keys, values), 'seq', [(s, s + 2) for s in range(0, count -...]
  transfers between devices with their start and end apart: 6 -> 6, of which waited for: 2 -> 0; matrix products, arithmetic and copies ran while one was open for 4% -> 4% of each run, Pallas kernels for 0% -> 0%
where the time goes in v6:
time: 182 us
  starting transfers between devices  92.8 us (51%)
  Pallas kernels  58.1 us (32%)
  blocking collectives  23.7 us (13%)
  other arithmetic  5.76 us (3%)
    ppermute x2, starting transfers between devices, local(): lax.ppermute(near, 'seq', [(s, s + 1) for s in range(0, count - 1, 2)])  77.7 us
    pallas_call x1, Pallas kernels, local(): pl.pallas_call(kernel, grid_spec=grid_spec, out_shape=jax.ShapeDtypeStruc...  58.1 us
    all_gather x1, blocking collectives, local(): seg_all = lax.all_gather(segment_ids, 'seq', tiled=True)  23.7 us
    ppermute x2, starting transfers between devices, local(): lax.ppermute((keys, values), 'seq', [(s, s + 1) for s in range(count - 1)])  8.32 us
    ppermute x2, starting transfers between devices, local(): lax.ppermute((keys, values), 'seq', [(s, s + 2) for s in range(0, count -...  6.83 us
  transfers between devices with their start and end apart: 6, of which 0 were waited for; matrix products, arithmetic and copies ran while one was open for 4% of the time, Pallas kernels for 0%

profile of v6, /device:TPU:0, one launch (start us, length us, event | category | flops | bytes accessed | tf_op | source)
XLA Modules:
  0.0 182.1 jit_solution(271471833601899323)
XLA Ops:
  0.0 2.5 %collective-permute-start = (bf16[512,2048]{1,0:T(8,128)(2,1)}, bf16[512,2048]{1,0:T(8,128)(2,1)S(1)}, u32[]{:S(2)}, u32[]{:S(2)}) collective-permute-start(bf16[512,2048]{1,0:T(8,128)(2,1)} %k0.1), channel_id=1, source_target_pairs={{0,1},{1,2},{2,3},{3,4},{4,5},{5,6},{6,7},{7,8},{8,9},{9,10},{10,1... | collective-permute-start | bytes 6291464 | tf_op jit(solution)/shard_map/ppermute | solution.py:89
  2.5 5.8 %collective-permute-start.1 = (bf16[512,2048]{1,0:T(8,128)(2,1)}, bf16[512,2048]{1,0:T(8,128)(2,1)}, u32[]{:S(2)}, u32[]{:S(2)}) collective-permute-start(bf16[512,2048]{1,0:T(8,128)(2,1)} %v0.1), channel_id=1, source_target_pairs={{0,1},{1,2},{2,3},{3,4},{4,5},{5,6},{6,7},{7,8},{8,9},{9,10},{10,1... | collective-permute-start | bytes 6291464 | tf_op jit(solution)/shard_map/ppermute | solution.py:89
  8.3 3.4 %collective-permute-start.2 = (bf16[512,2048]{1,0:T(8,128)(2,1)}, bf16[512,2048]{1,0:T(8,128)(2,1)}, u32[]{:S(2)}, u32[]{:S(2)}) collective-permute-start(bf16[512,2048]{1,0:T(8,128)(2,1)} %k0.1), channel_id=1, source_target_pairs={{0,2},{2,4},{4,6},{6,8},{8,10},{10,12},{12,14},{16,18},{18,20},{20... | collective-permute-start | bytes 6291464 | tf_op jit(solution)/shard_map/ppermute | solution.py:90
  11.7 3.4 %collective-permute-start.4 = (bf16[512,2048]{1,0:T(8,128)(2,1)}, bf16[512,2048]{1,0:T(8,128)(2,1)}, u32[]{:S(2)}, u32[]{:S(2)}) collective-permute-start(bf16[512,2048]{1,0:T(8,128)(2,1)} %v0.1), channel_id=1, source_target_pairs={{0,2},{2,4},{4,6},{6,8},{8,10},{10,12},{12,14},{16,18},{18,20},{20... | collective-permute-start | bytes 6291464 | tf_op jit(solution)/shard_map/ppermute | solution.py:90
  15.2 0.0 collective-permute-done.k1
  15.2 0.0 copy-start
  15.2 32.8 %collective-permute-start.3 = (bf16[512,2048]{1,0:T(8,128)(2,1)S(1)}, bf16[512,2048]{1,0:T(8,128)(2,1)}, u32[]{:S(2)}, u32[]{:S(2)}) collective-permute-start(bf16[512,2048]{1,0:T(8,128)(2,1)S(1)} %collective-permute-done.k1), channel_id=1, source_target_pairs={{0,1},{2,3},{4,5},{6,7},{8,9},{10,11},{12,13},{14,15},{16,17},{18,... | collective-permute-start | bytes 6291464 | tf_op jit(solution)/shard_map/ppermute | solution.py:91
  47.9 0.0 collective-permute-done.1.v1
  47.9 44.9 %collective-permute-start.5 = (bf16[512,2048]{1,0:T(8,128)(2,1)}, bf16[512,2048]{1,0:T(8,128)(2,1)}, u32[]{:S(2)}, u32[]{:S(2)}) collective-permute-start(bf16[512,2048]{1,0:T(8,128)(2,1)} %collective-permute-done.1.v1), channel_id=1, source_target_pairs={{0,1},{2,3},{4,5},{6,7},{8,9},{10,11},{12,13},{14,15},{16,17},{18,... | collective-permute-start | bytes 6291464 | tf_op jit(solution)/shard_map/ppermute | solution.py:91
  92.9 23.7 %all-gather = s32[16,1,512]{2,1,0:T(1,128)S(1)} all-gather(s32[1,1,512]{2,1,0:T(1,128)} %bitcast.13), channel_id=1, replica_groups=mesh['grp'=2,'seq'=16] {'seq'}, dimensions={0}, use_global_device_ids=true | all-gather | bytes 34816 | tf_op jit(solution)/shard_map/all_gather | solution.py:93
  116.6 0.5 slice.21
  117.1 0.7 select_bitcast_fusion
  117.8 0.3 reduce-window.9
  118.1 0.1 slice.23
  118.2 0.1 reduce-window.12
  118.3 0.1 slice_reduce_fusion
  118.4 0.1 bitcast_subtract_fusion
  118.5 0.1 pad_dynamic-slice_fusion
  118.6 0.9 copy.6.pos_ref
  119.4 0.1 fusion.2
  119.5 2.8 %fusion = (f32[1536,64]{1,0:T(8,128)S(1)}, f32[1536,64]{1,0:T(8,128)S(1)}, f32[1536,64]{1,0:T(8,128)S(1)}) fusion(f32[64]{0:T(128)S(1)} %multiply_power_fusion, f32[1536]{0:T(1024)S(1)} %fusion.2), kind=kLoop, calls=%fused_computation.4 | loop fusion | flops 196608 | bytes 1186048 | tf_op jit(solution)/shard_map/neg | solution.py:31
  122.3 1.7 pad_maximum_fusion
  124.0 0.0 copy-done
  124.0 0.0 collective-permute-done.2.k2a
  124.0 0.0 collective-permute-done.4.v2a
  124.0 0.0 collective-permute-done.3.k2b
  124.0 0.0 collective-permute-done.5.v2b
  124.0 58.1 %shard_map.46 = bf16[512,4096]{1,0:T(8,128)(2,1)} custom-call(s32[1]{0:T(128)} %bitcast.par_ref, s32[512,1]{1,0:T(8,128)} %copy.6.pos_ref, f32[1536,128]{1,0:T(8,128)} %get-tuple-element.14.cos_ref, f32[1536,128]{1,0:T(8,128)} %get-tuple-element.15.sin_ref, bf16[512,4096]{1,0:T(8,128)(2,1)} %q_ref.1, bf16[512,2048]{1,0:T(8,128)(2,1)} %collective-permute-done.2.k2a, ...), custom_call_target="tpu_custom_call" | custom-call | tf_op jit(solution)/shard_map/pallas_call | solution.py:117
  (1 shorter events, 0.0 us)
Async XLA Ops:
  0.0 15.2 %collective-permute-start = (bf16[512,2048]{1,0:T(8,128)(2,1)}, bf16[512,2048]{1,0:T(8,128)(2,1)S(1)}, u32[]{:S(2)}, u32[]{:S(2)}) collective-permute-start(bf16[512,2048]{1,0:T(8,128)(2,1)} %k0.1), channel_id=1, source_target_pairs={{0,1},{1,2},{2,3},{3,4},{4,5},{5,6},{6,7},{7,8},{8,9},{9,10},{10,1... | collective-permute-start | bytes 6291464 | tf_op jit(solution)/shard_map/ppermute | solution.py:89
  2.5 45.4 %collective-permute-start.1 = (bf16[512,2048]{1,0:T(8,128)(2,1)}, bf16[512,2048]{1,0:T(8,128)(2,1)}, u32[]{:S(2)}, u32[]{:S(2)}) collective-permute-start(bf16[512,2048]{1,0:T(8,128)(2,1)} %v0.1), channel_id=1, source_target_pairs={{0,1},{1,2},{2,3},{3,4},{4,5},{5,6},{6,7},{7,8},{8,9},{9,10},{10,1... | collective-permute-start | bytes 6291464 | tf_op jit(solution)/shard_map/ppermute | solution.py:89
  8.3 115.7 %collective-permute-start.2 = (bf16[512,2048]{1,0:T(8,128)(2,1)}, bf16[512,2048]{1,0:T(8,128)(2,1)}, u32[]{:S(2)}, u32[]{:S(2)}) collective-permute-start(bf16[512,2048]{1,0:T(8,128)(2,1)} %k0.1), channel_id=1, source_target_pairs={{0,2},{2,4},{4,6},{6,8},{8,10},{10,12},{12,14},{16,18},{18,20},{20... | collective-permute-start | bytes 6291464 | tf_op jit(solution)/shard_map/ppermute | solution.py:90
  11.7 112.3 %collective-permute-start.4 = (bf16[512,2048]{1,0:T(8,128)(2,1)}, bf16[512,2048]{1,0:T(8,128)(2,1)}, u32[]{:S(2)}, u32[]{:S(2)}) collective-permute-start(bf16[512,2048]{1,0:T(8,128)(2,1)} %v0.1), channel_id=1, source_target_pairs={{0,2},{2,4},{4,6},{6,8},{8,10},{10,12},{12,14},{16,18},{18,20},{20... | collective-permute-start | bytes 6291464 | tf_op jit(solution)/shard_map/ppermute | solution.py:90
  15.2 108.8 %copy-start = (bf16[512,2048]{1,0:T(8,128)(2,1)}, bf16[512,2048]{1,0:T(8,128)(2,1)S(1)}, u32[]{:S(2)}) copy-start(bf16[512,2048]{1,0:T(8,128)(2,1)S(1)} %collective-permute-done.k1) | copy-start | bytes 6291460
  15.2 108.8 %collective-permute-start.3 = (bf16[512,2048]{1,0:T(8,128)(2,1)S(1)}, bf16[512,2048]{1,0:T(8,128)(2,1)}, u32[]{:S(2)}, u32[]{:S(2)}) collective-permute-start(bf16[512,2048]{1,0:T(8,128)(2,1)S(1)} %collective-permute-done.k1), channel_id=1, source_target_pairs={{0,1},{2,3},{4,5},{6,7},{8,9},{10,11},{12,13},{14,15},{16,17},{18,... | collective-permute-start | bytes 6291464 | tf_op jit(solution)/shard_map/ppermute | solution.py:91
  47.9 76.1 %collective-permute-start.5 = (bf16[512,2048]{1,0:T(8,128)(2,1)}, bf16[512,2048]{1,0:T(8,128)(2,1)}, u32[]{:S(2)}, u32[]{:S(2)}) collective-permute-start(bf16[512,2048]{1,0:T(8,128)(2,1)} %collective-permute-done.1.v1), channel_id=1, source_target_pairs={{0,1},{2,3},{4,5},{6,7},{8,9},{10,11},{12,13},{14,15},{16,17},{18,... | collective-permute-start | bytes 6291464 | tf_op jit(solution)/shard_map/ppermute | solution.py:91

commit v7 on v4

--- a/solution.py
+++ b/solution.py
@@ -14,6 +14,7 @@
 
 
 query_scale = 168.0 ** (-0.5)
+exp2_scale = query_scale * 1.4426950408889634
 
 
 def passed_along(value, axis, steps):
@@ -32,9 +33,9 @@
 
 def attend_kernel(par_ref, pos_ref, cos_ref, sin_ref, q_ref, *refs, rows, tile, first, final):
     if final:
-        k2a, k2b, v2a, v2b, m_in, l_in, acc_in, o_ref, bias_ref = refs
+        k2a, k2b, v2a, v2b, st_in, acc_in, o_ref, bias_ref = refs
     else:
-        k1, k0, v1, v0, m_out, l_out, acc_out, bias_ref = refs
+        k1, k0, v1, v0, st_out, acc_out, bias_ref = refs
     tiles = rows // tile
     nkeys = bias_ref.shape[2]
     qoff = W
@@ -82,21 +83,21 @@
             q = q_ref[r0:r0 + tile, cols].astype(jnp.float32)
             q = rot(q, qc, qs).astype(jnp.bfloat16)
             s = lax.dot_general(q, kk, (((1,), (1,)), ((), ())), preferred_element_type=jnp.float32)
-            s = s * query_scale + bias
+            s = s + bias
             m = jnp.max(s, axis=1, keepdims=True)
             if final:
-                m1 = m_in[g, r0:r0 + tile]
+                m1 = st_in[0, r0:r0 + tile, g:g + 1]
                 mm = jnp.maximum(m, m1)
-                scale1 = jnp.exp(m1 - mm)
-                w = jnp.exp(s - mm)
-                tot = jnp.sum(w, axis=1, keepdims=True) + l_in[g, r0:r0 + tile] * scale1
+                scale1 = jnp.exp2((m1 - mm) * exp2_scale)
+                w = jnp.exp2((s - mm) * exp2_scale)
+                tot = jnp.sum(w, axis=1, keepdims=True) + st_in[0, r0:r0 + tile, 2 + g:3 + g] * scale1
                 pv = jnp.dot(w.astype(jnp.bfloat16), vv, preferred_element_type=jnp.float32)
                 pv = pv + acc_in[r0:r0 + tile, cols] * scale1
                 o_ref[r0:r0 + tile, cols] = (pv / tot).astype(jnp.bfloat16)
             else:
-                w = jnp.exp(s - m)
-                m_out[g, r0:r0 + tile] = m
-                l_out[g, r0:r0 + tile] = jnp.sum(w, axis=1, keepdims=True)
+                w = jnp.exp2((s - m) * exp2_scale)
+                st_out[0, r0:r0 + tile, g:g + 1] = m
+                st_out[0, r0:r0 + tile, 2 + g:3 + g] = jnp.sum(w, axis=1, keepdims=True)
                 acc_out[r0:r0 + tile, cols] = jnp.dot(
                     w.astype(jnp.bfloat16), vv, preferred_element_type=jnp.float32)
 
@@ -108,10 +109,9 @@
     span = (hops + 1) * rows
     shard = lax.axis_index("seq")
     count = lax.axis_size("seq")
+    near = lax.ppermute((keys, values), "seq", [(s, s + 1) for s in range(count - 1)])
     seg_all = lax.all_gather(segment_ids, "seq", tiled=True)
-    keys, values, seg_all = lax.optimization_barrier((keys, values, seg_all))
-    near = lax.ppermute((keys, values), "seq", [(s, s + 1) for s in range(count - 1)])
-    keys_b, values_b, near = lax.optimization_barrier((keys, values, near))
+    keys_b, values_b, seg_all = lax.optimization_barrier((keys, values, seg_all))
     far = lax.ppermute((keys_b, values_b), "seq", [(s, s + 2) for s in range(0, count - 2, 2)])
     relay = lax.ppermute(near, "seq", [(s, s + 1) for s in range(0, count - 1, 2)])
     total = seg_all.shape[0]
@@ -129,31 +129,31 @@
     kv_spec = pl.BlockSpec((rows, HD), lambda h, p: (0, h))
     full = lambda shape: pl.BlockSpec(shape, lambda h, p: (0, 0))
     head_spec = pl.BlockSpec((rows, 2 * HD), lambda h, p: (0, h))
-    stat_spec = pl.BlockSpec((2, rows, 1), lambda h, p: (h, 0, 0))
+    stat_spec = pl.BlockSpec((1, rows, 128), lambda h, p: (h, 0, 0))
     lead = [full((rows, 1)), full((span, HD)), full((span, HD)), head_spec]
     params = pltpu.CompilerParams(dimension_semantics=("arbitrary",))
     f32 = jnp.float32
-    stat_shape = jax.ShapeDtypeStruct((2 * heads, rows, 1), f32)
-    m1, l1, acc1 = pl.pallas_call(
+    stats, acc1 = pl.pallas_call(
         functools.partial(attend_kernel, rows=rows, tile=tile, first=rows, final=False),
         grid_spec=pltpu.PrefetchScalarGridSpec(
             num_scalar_prefetch=1, grid=(heads,),
             in_specs=lead + [kv_spec] * 4,
-            out_specs=[stat_spec, stat_spec, head_spec],
+            out_specs=[stat_spec, head_spec],
             scratch_shapes=[pltpu.VMEM((rows // tile, tile, 2 * rows), f32)]),
-        out_shape=[stat_shape, stat_shape, jax.ShapeDtypeStruct(queries.shape, f32)],
+        out_shape=[jax.ShapeDtypeStruct((heads, rows, 128), f32),
+                   jax.ShapeDtypeStruct(queries.shape, f32)],
         compiler_params=params,
     )(parity, pos_q, cos, sin, queries, near[0], keys, near[1], values)
     return pl.pallas_call(
         functools.partial(attend_kernel, rows=rows, tile=tile, first=0, final=True),
         grid_spec=pltpu.PrefetchScalarGridSpec(
             num_scalar_prefetch=1, grid=(heads,),
-            in_specs=lead + [kv_spec] * 4 + [stat_spec, stat_spec, head_spec],
+            in_specs=lead + [kv_spec] * 4 + [stat_spec, head_spec],
             out_specs=head_spec,
             scratch_shapes=[pltpu.VMEM((rows // tile, tile, rows), f32)]),
         out_shape=jax.ShapeDtypeStruct(queries.shape, jnp.bfloat16),
         compiler_params=params,
-    )(parity, pos_q, cos, sin, queries, far[0], relay[0], far[1], relay[1], m1, l1, acc1)
+    )(parity, pos_q, cos, sin, queries, far[0], relay[0], far[1], relay[1], stats, acc1)
 
 
 def solution(mesh):

time: 185 us -> 179 us (0.968)
  starting transfers between devices: 57.3 us -> 18.8 us
  blocking collectives: 23.4 us -> 55.6 us
  Pallas kernels: 92.3 us -> 95.6 us
  waiting for transfers between devices: 3.17 us -> 0.02 us
    ppermute x2, starting transfers between devices: 43.3 us -> 5.25 us  [local(): lax.ppermute(near, 'seq', [(s, s + 1) for s in range(0, count - 1, 2)])]
    all_gather x1, blocking collectives: 23.4 us -> 55.6 us  [local(): seg_all = lax.all_gather(segment_ids, 'seq', tiled=True)]
    pallas_call x2, Pallas kernels: 92.3 us -> 95.6 us  [local(): pl.pallas_call(functools.partial(attend_kernel, rows=rows, tile=tile, fir...]
    ppermute x2, waiting for transfers between devices: 3.16 us -> 0.01 us  [local(): lax.ppermute((keys, values), 'seq', [(s, s + 1) for s in range(count - 1)])]
    ppermute x2, starting transfers between devices: 7.76 us -> 5.34 us  [local(): lax.ppermute((keys_b, values_b), 'seq', [(s, s + 2) for s in range(0, cou...]
    ppermute x2, starting transfers between devices: 6.19 us -> 8.25 us  [local(): lax.ppermute((keys, values), 'seq', [(s, s + 1) for s in range(count - 1)])]
  transfers between devices with their start and end apart: 6 -> 6, of which waited for: 2 -> 0; matrix products, arithmetic and copies ran while one was open for 4% -> 4% of each run, Pallas kernels for 27% -> 28%
where the time goes in v7:
time: 179 us
  Pallas kernels  95.6 us (53%)
  blocking collectives  55.6 us (31%)
  starting transfers between devices  18.8 us (11%)
  other arithmetic  5.8 us (3%)
  local copies, waits for them, and re-layouts  2.96 us (2%)
    pallas_call x2, Pallas kernels, local(): pl.pallas_call(functools.partial(attend_kernel, rows=rows, tile=tile, fir...  95.6 us
    all_gather x1, blocking collectives, local(): seg_all = lax.all_gather(segment_ids, 'seq', tiled=True)  55.6 us
    ppermute x2, starting transfers between devices, local(): lax.ppermute((keys, values), 'seq', [(s, s + 1) for s in range(count - 1)])  8.25 us
    ppermute x2, starting transfers between devices, local(): lax.ppermute((keys_b, values_b), 'seq', [(s, s + 2) for s in range(0, cou...  5.34 us
    ppermute x2, starting transfers between devices, local(): lax.ppermute(near, 'seq', [(s, s + 1) for s in range(0, count - 1, 2)])  5.25 us
  transfers between devices with their start and end apart: 6, of which 0 were waited for; matrix products, arithmetic and copies ran while one was open for 4% of the time, Pallas kernels for 28%

profile of v7, /device:TPU:0, one launch (start us, length us, event | category | flops | bytes accessed | tf_op | source)
XLA Modules:
  0.0 179.0 jit_solution(11893067489367806177)
XLA Ops:
  0.0 3.7 %collective-permute-start.1 = (bf16[512,2048]{1,0:T(8,128)(2,1)}, bf16[512,2048]{1,0:T(8,128)(2,1)}, u32[]{:S(2)}, u32[]{:S(2)}) collective-permute-start(bf16[512,2048]{1,0:T(8,128)(2,1)} %refs_1_.1), channel_id=1, source_target_pairs={{0,1},{1,2},{2,3},{3,4},{4,5},{5,6},{6,7},{7,8},{8,9},{9,10},{10,1... | collective-permute-start | bytes 6291464 | tf_op jit(solution)/shard_map/ppermute | solution.py:112
  3.7 4.5 %collective-permute-start.4 = (bf16[512,2048]{1,0:T(8,128)(2,1)}, bf16[512,2048]{1,0:T(8,128)(2,1)}, u32[]{:S(2)}, u32[]{:S(2)}) collective-permute-start(bf16[512,2048]{1,0:T(8,128)(2,1)} %refs_3_.1), channel_id=1, source_target_pairs={{0,1},{1,2},{2,3},{3,4},{4,5},{5,6},{6,7},{7,8},{8,9},{9,10},{10,1... | collective-permute-start | bytes 6291464 | tf_op jit(solution)/shard_map/ppermute | solution.py:112
  8.3 55.6 %all-gather = s32[16,1,512]{2,1,0:T(1,128)S(1)} all-gather(s32[1,1,512]{2,1,0:T(1,128)} %bitcast.13), channel_id=1, replica_groups=mesh['grp'=2,'seq'=16] {'seq'}, dimensions={0}, use_global_device_ids=true | all-gather | bytes 34816 | tf_op jit(solution)/shard_map/all_gather | solution.py:113
  63.9 1.4 collective-permute-start
  65.3 3.9 %collective-permute-start.3 = (bf16[512,2048]{1,0:T(8,128)(2,1)}, bf16[512,2048]{1,0:T(8,128)(2,1)}, u32[]{:S(2)}, u32[]{:S(2)}) collective-permute-start(bf16[512,2048]{1,0:T(8,128)(2,1)} %refs_3_.1), channel_id=1, source_target_pairs={{0,2},{2,4},{4,6},{6,8},{8,10},{10,12},{12,14},{16,18},{18,20},{20... | collective-permute-start | bytes 6291464 | tf_op jit(solution)/shard_map/ppermute | solution.py:115
  69.2 0.0 collective-permute-done.1.refs_0_
  69.2 2.6 %collective-permute-start.2 = (bf16[512,2048]{1,0:T(8,128)(2,1)}, bf16[512,2048]{1,0:T(8,128)(2,1)}, u32[]{:S(2)}, u32[]{:S(2)}) collective-permute-start(bf16[512,2048]{1,0:T(8,128)(2,1)} %collective-permute-done.1.refs_0_), channel_id=1, source_target_pairs={{0,1},{2,3},{4,5},{6,7},{8,9},{10,11},{12,13},{14,15},{16,17},{18,... | collective-permute-start | bytes 6291464 | tf_op jit(solution)/shard_map/ppermute | solution.py:116
  71.9 0.0 collective-permute-done.4.refs_2_
  71.9 2.6 %collective-permute-start.5 = (bf16[512,2048]{1,0:T(8,128)(2,1)}, bf16[512,2048]{1,0:T(8,128)(2,1)}, u32[]{:S(2)}, u32[]{:S(2)}) collective-permute-start(bf16[512,2048]{1,0:T(8,128)(2,1)} %collective-permute-done.4.refs_2_), channel_id=1, source_target_pairs={{0,1},{2,3},{4,5},{6,7},{8,9},{10,11},{12,13},{14,15},{16,17},{18,... | collective-permute-start | bytes 6291464 | tf_op jit(solution)/shard_map/ppermute | solution.py:116
  74.5 0.5 slice.16
  75.0 0.7 select_bitcast_fusion
  75.7 0.3 reduce-window.9
  76.0 0.1 slice.21
  76.1 0.1 reduce-window.12
  76.2 0.1 slice_reduce_fusion
  76.3 0.1 bitcast_subtract_fusion
  76.4 0.1 pad_dynamic-slice_fusion
  76.5 0.9 copy.8.pos_ref
  77.4 0.1 fusion.2
  77.5 2.8 %fusion = (f32[1536,64]{1,0:T(8,128)S(1)}, f32[1536,64]{1,0:T(8,128)S(1)}, f32[1536,64]{1,0:T(8,128)S(1)}) fusion(f32[64]{0:T(128)S(1)} %multiply_power_fusion, f32[1536]{0:T(1024)S(1)} %fusion.2), kind=kLoop, calls=%fused_computation.4 | loop fusion | flops 196608 | bytes 1186048 | tf_op jit(solution)/shard_map/neg | solution.py:31
  80.3 1.7 pad_maximum_fusion
  82.0 50.0 %shard_map.46 = (f32[16,512,128]{2,1,0:T(8,128)}, f32[512,4096]{1,0:T(8,128)}) custom-call(s32[1]{0:T(128)} %bitcast.par_ref, s32[512,1]{1,0:T(8,128)} %copy.8.pos_ref, f32[1536,128]{1,0:T(8,128)} %get-tuple-element.18.cos_ref, f32[1536,128]{1,0:T(8,128)} %get-tuple-element.19.sin_ref, bf16[512,4096]{1,0:T(8,128)(2,1)} %q_ref.3, ...), custom_call_target="tpu_custom_call" | custom-call | tf_op jit(solution)/shard_map/pallas_call | solution.py:136
  132.0 0.0 collective-permute-done.refs_0_
  132.0 0.0 copy-start
  132.0 0.0 collective-permute-done.3.refs_2_
  132.0 0.0 collective-permute-done.2.refs_1_
  132.0 0.0 collective-permute-done.5.refs_3_
  132.0 1.3 copy-done
  133.3 45.6 %shard_map.47 = bf16[512,4096]{1,0:T(8,128)(2,1)} custom-call(s32[1]{0:T(128)} %bitcast.par_ref, s32[512,1]{1,0:T(8,128)} %copy.8.pos_ref, f32[1536,128]{1,0:T(8,128)} %get-tuple-element.18.cos_ref, f32[1536,128]{1,0:T(8,128)} %get-tuple-element.19.sin_ref, bf16[512,4096]{1,0:T(8,128)(2,1)} %q_ref.3, bf16[512,2048]{1,0:T(8,128)(2,1)} %copy-done, ...), custom_call_target="tpu_custom_call" | custom-call | tf_op jit(solution)/shard_map/pallas_call | solution.py:147
  (1 shorter events, 0.0 us)
Async XLA Ops:
  0.0 69.2 %collective-permute-start.1 = (bf16[512,2048]{1,0:T(8,128)(2,1)}, bf16[512,2048]{1,0:T(8,128)(2,1)}, u32[]{:S(2)}, u32[]{:S(2)}) collective-permute-start(bf16[512,2048]{1,0:T(8,128)(2,1)} %refs_1_.1), channel_id=1, source_target_pairs={{0,1},{1,2},{2,3},{3,4},{4,5},{5,6},{6,7},{7,8},{8,9},{9,10},{10,1... | collective-permute-start | bytes 6291464 | tf_op jit(solution)/shard_map/ppermute | solution.py:112
  3.7 68.2 %collective-permute-start.4 = (bf16[512,2048]{1,0:T(8,128)(2,1)}, bf16[512,2048]{1,0:T(8,128)(2,1)}, u32[]{:S(2)}, u32[]{:S(2)}) collective-permute-start(bf16[512,2048]{1,0:T(8,128)(2,1)} %refs_3_.1), channel_id=1, source_target_pairs={{0,1},{1,2},{2,3},{3,4},{4,5},{5,6},{6,7},{7,8},{8,9},{9,10},{10,1... | collective-permute-start | bytes 6291464 | tf_op jit(solution)/shard_map/ppermute | solution.py:112
  63.9 68.1 %collective-permute-start = (bf16[512,2048]{1,0:T(8,128)(2,1)}, bf16[512,2048]{1,0:T(8,128)(2,1)S(1)}, u32[]{:S(2)}, u32[]{:S(2)}) collective-permute-start(bf16[512,2048]{1,0:T(8,128)(2,1)} %refs_1_.1), channel_id=1, source_target_pairs={{0,2},{2,4},{4,6},{6,8},{8,10},{10,12},{12,14},{16,18},{18,20},{20... | collective-permute-start | bytes 6291464 | tf_op jit(solution)/shard_map/ppermute | solution.py:115
  65.3 66.7 %collective-permute-start.3 = (bf16[512,2048]{1,0:T(8,128)(2,1)}, bf16[512,2048]{1,0:T(8,128)(2,1)}, u32[]{:S(2)}, u32[]{:S(2)}) collective-permute-start(bf16[512,2048]{1,0:T(8,128)(2,1)} %refs_3_.1), channel_id=1, source_target_pairs={{0,2},{2,4},{4,6},{6,8},{8,10},{10,12},{12,14},{16,18},{18,20},{20... | collective-permute-start | bytes 6291464 | tf_op jit(solution)/shard_map/ppermute | solution.py:115
  69.2 62.8 %collective-permute-start.2 = (bf16[512,2048]{1,0:T(8,128)(2,1)}, bf16[512,2048]{1,0:T(8,128)(2,1)}, u32[]{:S(2)}, u32[]{:S(2)}) collective-permute-start(bf16[512,2048]{1,0:T(8,128)(2,1)} %collective-permute-done.1.refs_0_), channel_id=1, source_target_pairs={{0,1},{2,3},{4,5},{6,7},{8,9},{10,11},{12,13},{14,15},{16,17},{18,... | collective-permute-start | bytes 6291464 | tf_op jit(solution)/shard_map/ppermute | solution.py:116
  71.9 60.2 %collective-permute-start.5 = (bf16[512,2048]{1,0:T(8,128)(2,1)}, bf16[512,2048]{1,0:T(8,128)(2,1)}, u32[]{:S(2)}, u32[]{:S(2)}) collective-permute-start(bf16[512,2048]{1,0:T(8,128)(2,1)} %collective-permute-done.4.refs_2_), channel_id=1, source_target_pairs={{0,1},{2,3},{4,5},{6,7},{8,9},{10,11},{12,13},{14,15},{16,17},{18,... | collective-permute-start | bytes 6291464 | tf_op jit(solution)/shard_map/ppermute | solution.py:116
  132.0 1.3 copy-start

commit v8 on v5

--- a/solution.py
+++ b/solution.py
@@ -103,7 +103,7 @@
     parity = (shard % 2).astype(jnp.int32).reshape(1)
     kv_spec = pl.BlockSpec((rows, HD), lambda h, p: (0, h))
     full = lambda shape: pl.BlockSpec(shape, lambda h, p: (0, 0))
-    tile = 128
+    tile = 256
     kernel = functools.partial(attend_kernel, rows=rows, hops=hops, tile=tile)
     heads = keys.shape[1] // HD
     grid_spec = pltpu.PrefetchScalarGridSpec(

time: 170 us -> 158 us (0.929)
  Pallas kernels: 58 us -> 46.5 us
    pallas_call x1, Pallas kernels: 58 us -> 46.5 us  [local(): pl.pallas_call(kernel, grid_spec=grid_spec, out_shape=jax.ShapeDtypeStruc...]
  transfers between devices with their start and end apart: 6 -> 6, of which waited for: 2 -> 2; matrix products, arithmetic and copies ran while one was open for 4% -> 5% of each run, Pallas kernels for 0% -> 0%
where the time goes in v8:
time: 158 us
  blocking collectives  55.6 us (35%)
  Pallas kernels  46.5 us (29%)
  waiting for transfers between devices  29.6 us (19%)
  starting transfers between devices  18.9 us (12%)
  other arithmetic  5.77 us (4%)
  local copies, waits for them, and re-layouts  1.65 us (1%)
    all_gather x1, blocking collectives, local(): seg_all = lax.all_gather(segment_ids, 'seq', tiled=True)  55.6 us
    pallas_call x1, Pallas kernels, local(): pl.pallas_call(kernel, grid_spec=grid_spec, out_shape=jax.ShapeDtypeStruc...  46.5 us
    ppermute x2, waiting for transfers between devices, local(): lax.ppermute((keys, values), 'seq', [(s, s + 2) for s in range(0, count -...  29.6 us
    ppermute x2, starting transfers between devices, local(): lax.ppermute((keys, values), 'seq', [(s, s + 1) for s in range(count - 1)])  8.32 us
    ppermute x2, starting transfers between devices, local(): lax.ppermute((keys, values), 'seq', [(s, s + 2) for s in range(0, count -...  5.39 us
    ppermute x2, starting transfers between devices, local(): lax.ppermute(near, 'seq', [(s, s + 1) for s in range(0, count - 1, 2)])  5.19 us
  transfers between devices with their start and end apart: 6, of which 2 were waited for; matrix products, arithmetic and copies ran while one was open for 5% of the time, Pallas kernels for 0%

profile of v8, /device:TPU:0, one launch (start us, length us, event | category | flops | bytes accessed | tf_op | source)
XLA Modules:
  0.0 158.0 jit_solution(16874121918017755580)
XLA Ops:
  0.0 2.5 %collective-permute-start.1 = (bf16[512,2048]{1,0:T(8,128)(2,1)}, bf16[512,2048]{1,0:T(8,128)(2,1)S(1)}, u32[]{:S(2)}, u32[]{:S(2)}) collective-permute-start(bf16[512,2048]{1,0:T(8,128)(2,1)} %k0), channel_id=1, source_target_pairs={{0,1},{1,2},{2,3},{3,4},{4,5},{5,6},{6,7},{7,8},{8,9},{9,10},{10,1... | collective-permute-start | bytes 6291464 | tf_op jit(solution)/shard_map/ppermute | solution.py:89
  2.5 5.8 %collective-permute-start.4 = (bf16[512,2048]{1,0:T(8,128)(2,1)}, bf16[512,2048]{1,0:T(8,128)(2,1)}, u32[]{:S(2)}, u32[]{:S(2)}) collective-permute-start(bf16[512,2048]{1,0:T(8,128)(2,1)} %v0), channel_id=1, source_target_pairs={{0,1},{1,2},{2,3},{3,4},{4,5},{5,6},{6,7},{7,8},{8,9},{9,10},{10,1... | collective-permute-start | bytes 6291464 | tf_op jit(solution)/shard_map/ppermute | solution.py:89
  8.3 55.6 %all-gather = s32[16,1,512]{2,1,0:T(1,128)S(1)} all-gather(s32[1,1,512]{2,1,0:T(1,128)} %bitcast.13), channel_id=1, replica_groups=mesh['grp'=2,'seq'=16] {'seq'}, dimensions={0}, use_global_device_ids=true | all-gather | bytes 34816 | tf_op jit(solution)/shard_map/all_gather | solution.py:90
  63.9 2.6 %collective-permute-start = (bf16[512,2048]{1,0:T(8,128)(2,1)}, bf16[512,2048]{1,0:T(8,128)(2,1)}, u32[]{:S(2)}, u32[]{:S(2)}) collective-permute-start(bf16[512,2048]{1,0:T(8,128)(2,1)} %k0), channel_id=1, source_target_pairs={{0,2},{2,4},{4,6},{6,8},{8,10},{10,12},{12,14},{16,18},{18,20},{20... | collective-permute-start | bytes 6291464 | tf_op jit(solution)/shard_map/ppermute | solution.py:92
  66.5 2.8 %collective-permute-start.3 = (bf16[512,2048]{1,0:T(8,128)(2,1)}, bf16[512,2048]{1,0:T(8,128)(2,1)}, u32[]{:S(2)}, u32[]{:S(2)}) collective-permute-start(bf16[512,2048]{1,0:T(8,128)(2,1)} %v0), channel_id=1, source_target_pairs={{0,2},{2,4},{4,6},{6,8},{8,10},{10,12},{12,14},{16,18},{18,20},{20... | collective-permute-start | bytes 6291464 | tf_op jit(solution)/shard_map/ppermute | solution.py:92
  69.3 0.0 collective-permute-done.1.k1
  69.3 0.0 copy-start
  69.3 2.6 %collective-permute-start.2 = (bf16[512,2048]{1,0:T(8,128)(2,1)S(1)}, bf16[512,2048]{1,0:T(8,128)(2,1)}, u32[]{:S(2)}, u32[]{:S(2)}) collective-permute-start(bf16[512,2048]{1,0:T(8,128)(2,1)S(1)} %collective-permute-done.1.k1), channel_id=1, source_target_pairs={{0,1},{2,3},{4,5},{6,7},{8,9},{10,11},{12,13},{14,15},{16,17},{18,... | collective-permute-start | bytes 6291464 | tf_op jit(solution)/shard_map/ppermute | solution.py:93
  71.9 0.0 collective-permute-done.4.v1
  71.9 2.6 %collective-permute-start.5 = (bf16[512,2048]{1,0:T(8,128)(2,1)}, bf16[512,2048]{1,0:T(8,128)(2,1)}, u32[]{:S(2)}, u32[]{:S(2)}) collective-permute-start(bf16[512,2048]{1,0:T(8,128)(2,1)} %collective-permute-done.4.v1), channel_id=1, source_target_pairs={{0,1},{2,3},{4,5},{6,7},{8,9},{10,11},{12,13},{14,15},{16,17},{18,... | collective-permute-start | bytes 6291464 | tf_op jit(solution)/shard_map/ppermute | solution.py:93
  74.5 0.5 slice.16
  75.0 0.7 select_bitcast_fusion
  75.7 0.3 reduce-window.9
  76.0 0.1 slice.21
  76.1 0.1 reduce-window.12
  76.2 0.1 slice_reduce_fusion
  76.3 0.1 bitcast_subtract_fusion
  76.4 0.1 pad_dynamic-slice_fusion
  76.5 0.9 copy.6.pos_ref
  77.3 0.1 fusion.2
  77.4 2.8 %fusion = (f32[1536,64]{1,0:T(8,128)S(1)}, f32[1536,64]{1,0:T(8,128)S(1)}, f32[1536,64]{1,0:T(8,128)S(1)}) fusion(f32[64]{0:T(128)S(1)} %multiply_power_fusion, f32[1536]{0:T(1024)S(1)} %fusion.2), kind=kLoop, calls=%fused_computation.4 | loop fusion | flops 196608 | bytes 1186048 | tf_op jit(solution)/shard_map/neg | solution.py:31
  80.2 1.7 %pad_maximum_fusion = (f32[1536,128]{1,0:T(8,128)}, f32[1536,128]{1,0:T(8,128)}) fusion(f32[1536,64]{1,0:T(8,128)S(1)} %get-tuple-element.13, f32[1536,64]{1,0:T(8,128)S(1)} %get-tuple-element.12, f32[1536,64]{1,0:T(8,128)S(1)} %get-tuple-element.11), kind=kLoop, calls=%fused_computation.2 | loop fusion | flops 393216 | bytes 2752512 | tf_op jit(solution)/shard_map/concatenate | solution.py:31
  81.9 0.0 copy-done
  81.9 7.1 %collective-permute-done.k2a = bf16[512,2048]{1,0:T(8,128)(2,1)} collective-permute-done((bf16[512,2048]{1,0:T(8,128)(2,1)}, bf16[512,2048]{1,0:T(8,128)(2,1)}, u32[]{:S(2)}, u32[]{:S(2)}) %collective-permute-start) | collective-permute-done | bytes 2097184 | tf_op jit(solution)/shard_map/ppermute | solution.py:92
  89.0 22.5 %collective-permute-done.3.v2a = bf16[512,2048]{1,0:T(8,128)(2,1)} collective-permute-done((bf16[512,2048]{1,0:T(8,128)(2,1)}, bf16[512,2048]{1,0:T(8,128)(2,1)}, u32[]{:S(2)}, u32[]{:S(2)}) %collective-permute-start.3) | collective-permute-done | bytes 2097184 | tf_op jit(solution)/shard_map/ppermute | solution.py:92
  111.5 0.0 collective-permute-done.2.k2b
  111.5 0.0 collective-permute-done.5.v2b
  111.5 46.5 %shard_map.46 = bf16[512,4096]{1,0:T(8,128)(2,1)} custom-call(s32[1]{0:T(128)} %bitcast.par_ref, s32[512,1]{1,0:T(8,128)} %copy.6.pos_ref, f32[1536,128]{1,0:T(8,128)} %get-tuple-element.14.cos_ref, f32[1536,128]{1,0:T(8,128)} %get-tuple-element.15.sin_ref, bf16[512,4096]{1,0:T(8,128)(2,1)} %q_ref.1, bf16[512,2048]{1,0:T(8,128)(2,1)} %collective-permute-done.k2a, ...), custom_call_target="tpu_custom_call" | custom-call | tf_op jit(solution)/shard_map/pallas_call | solution.py:117
  (1 shorter events, 0.0 us)
Async XLA Ops:
  0.0 69.3 %collective-permute-start.1 = (bf16[512,2048]{1,0:T(8,128)(2,1)}, bf16[512,2048]{1,0:T(8,128)(2,1)S(1)}, u32[]{:S(2)}, u32[]{:S(2)}) collective-permute-start(bf16[512,2048]{1,0:T(8,128)(2,1)} %k0), channel_id=1, source_target_pairs={{0,1},{1,2},{2,3},{3,4},{4,5},{5,6},{6,7},{7,8},{8,9},{9,10},{10,1... | collective-permute-start | bytes 6291464 | tf_op jit(solution)/shard_map/ppermute | solution.py:89
  2.5 69.4 %collective-permute-start.4 = (bf16[512,2048]{1,0:T(8,128)(2,1)}, bf16[512,2048]{1,0:T(8,128)(2,1)}, u32[]{:S(2)}, u32[]{:S(2)}) collective-permute-start(bf16[512,2048]{1,0:T(8,128)(2,1)} %v0), channel_id=1, source_target_pairs={{0,1},{1,2},{2,3},{3,4},{4,5},{5,6},{6,7},{7,8},{8,9},{9,10},{10,1... | collective-permute-start | bytes 6291464 | tf_op jit(solution)/shard_map/ppermute | solution.py:89
  63.9 25.1 %collective-permute-start = (bf16[512,2048]{1,0:T(8,128)(2,1)}, bf16[512,2048]{1,0:T(8,128)(2,1)}, u32[]{:S(2)}, u32[]{:S(2)}) collective-permute-start(bf16[512,2048]{1,0:T(8,128)(2,1)} %k0), channel_id=1, source_target_pairs={{0,2},{2,4},{4,6},{6,8},{8,10},{10,12},{12,14},{16,18},{18,20},{20... | collective-permute-start | bytes 6291464 | tf_op jit(solution)/shard_map/ppermute | solution.py:92
  66.5 45.0 %collective-permute-start.3 = (bf16[512,2048]{1,0:T(8,128)(2,1)}, bf16[512,2048]{1,0:T(8,128)(2,1)}, u32[]{:S(2)}, u32[]{:S(2)}) collective-permute-start(bf16[512,2048]{1,0:T(8,128)(2,1)} %v0), channel_id=1, source_target_pairs={{0,2},{2,4},{4,6},{6,8},{8,10},{10,12},{12,14},{16,18},{18,20},{20... | collective-permute-start | bytes 6291464 | tf_op jit(solution)/shard_map/ppermute | solution.py:92
  69.3 12.6 %copy-start = (bf16[512,2048]{1,0:T(8,128)(2,1)}, bf16[512,2048]{1,0:T(8,128)(2,1)S(1)}, u32[]{:S(2)}) copy-start(bf16[512,2048]{1,0:T(8,128)(2,1)S(1)} %collective-permute-done.1.k1) | copy-start | bytes 6291460
  69.3 42.2 %collective-permute-start.2 = (bf16[512,2048]{1,0:T(8,128)(2,1)S(1)}, bf16[512,2048]{1,0:T(8,128)(2,1)}, u32[]{:S(2)}, u32[]{:S(2)}) collective-permute-start(bf16[512,2048]{1,0:T(8,128)(2,1)S(1)} %collective-permute-done.1.k1), channel_id=1, source_target_pairs={{0,1},{2,3},{4,5},{6,7},{8,9},{10,11},{12,13},{14,15},{16,17},{18,... | collective-permute-start | bytes 6291464 | tf_op jit(solution)/shard_map/ppermute | solution.py:93
  71.9 39.6 %collective-permute-start.5 = (bf16[512,2048]{1,0:T(8,128)(2,1)}, bf16[512,2048]{1,0:T(8,128)(2,1)}, u32[]{:S(2)}, u32[]{:S(2)}) collective-permute-start(bf16[512,2048]{1,0:T(8,128)(2,1)} %collective-permute-done.4.v1), channel_id=1, source_target_pairs={{0,1},{2,3},{4,5},{6,7},{8,9},{10,11},{12,13},{14,15},{16,17},{18,... | collective-permute-start | bytes 6291464 | tf_op jit(solution)/shard_map/ppermute | solution.py:93

commit v9 on v8

--- a/solution.py
+++ b/solution.py
@@ -7,20 +7,13 @@
 from jax.experimental.pallas import tpu as pltpu
 from jax.sharding import PartitionSpec as P
 
-H = 32
-KVH = 16
+
 HD = 128
 W = 1024
 
 
 query_scale = 168.0 ** (-0.5)
 exp2_scale = query_scale * 1.4426950408889634
-
-
-def passed_along(value, axis, steps):
-    count = lax.axis_size(axis)
-    first, last = (max(0, -steps), min(count, count - steps))
-    return lax.ppermute(value, axis, [(source, source + steps) for source in range(first, last)])
 
 
 def rope_tables(doc_pos):
@@ -87,9 +80,8 @@
     shard = lax.axis_index("seq")
     count = lax.axis_size("seq")
     near = lax.ppermute((keys, values), "seq", [(s, s + 1) for s in range(count - 1)])
+    far = lax.ppermute((keys, values), "seq", [(s, s + 2) for s in range(0, count - 2, 2)])
     seg_all = lax.all_gather(segment_ids, "seq", tiled=True)
-    keys, values, seg_all = lax.optimization_barrier((keys, values, seg_all))
-    far = lax.ppermute((keys, values), "seq", [(s, s + 2) for s in range(0, count - 2, 2)])
     relay = lax.ppermute(near, "seq", [(s, s + 1) for s in range(0, count - 1, 2)])
     total = seg_all.shape[0]
     places = jnp.arange(total, dtype=jnp.int32)

time: 158 us -> 171 us (1.082)
  starting transfers between devices: 18.9 us -> 92.8 us
  blocking collectives: 55.6 us -> 23.7 us
  waiting for transfers between devices: 29.6 us -> 0.02 us
    ppermute x2, starting transfers between devices: 5.19 us -> 77.7 us  [local(): lax.ppermute(near, 'seq', [(s, s + 1) for s in range(0, count - 1, 2)])]
    all_gather x1, blocking collectives: 55.6 us -> 23.7 us  [local(): seg_all = lax.all_gather(segment_ids, 'seq', tiled=True)]
    ppermute x2, waiting for transfers between devices: 29.6 us -> 0.01 us  [local(): lax.ppermute((keys, values), 'seq', [(s, s + 2) for s in range(0, count -...]
  transfers between devices with their start and end apart: 6 -> 6, of which waited for: 2 -> 0; matrix products, arithmetic and copies ran while one was open for 5% -> 4% of each run, Pallas kernels for 0% -> 0%
where the time goes in v9:
time: 171 us
  starting transfers between devices  92.8 us (54%)
  Pallas kernels  46.5 us (27%)
  blocking collectives  23.7 us (14%)
  other arithmetic  5.77 us (3%)
    ppermute x2, starting transfers between devices, local(): lax.ppermute(near, 'seq', [(s, s + 1) for s in range(0, count - 1, 2)])  77.7 us
    pallas_call x1, Pallas kernels, local(): pl.pallas_call(kernel, grid_spec=grid_spec, out_shape=jax.ShapeDtypeStruc...  46.5 us
    all_gather x1, blocking collectives, local(): seg_all = lax.all_gather(segment_ids, 'seq', tiled=True)  23.7 us
    ppermute x2, starting transfers between devices, local(): lax.ppermute((keys, values), 'seq', [(s, s + 1) for s in range(count - 1)])  8.32 us
    ppermute x2, starting transfers between devices, local(): lax.ppermute((keys, values), 'seq', [(s, s + 2) for s in range(0, count -...  6.83 us
  transfers between devices with their start and end apart: 6, of which 0 were waited for; matrix products, arithmetic and copies ran while one was open for 4% of the time, Pallas kernels for 0%

profile of v9, /device:TPU:0, one launch (start us, length us, event | category | flops | bytes accessed | tf_op | source)
XLA Modules:
  0.0 170.5 jit_solution(17336489757232411347)
XLA Ops:
  0.0 2.5 %collective-permute-start.1 = (bf16[512,2048]{1,0:T(8,128)(2,1)}, bf16[512,2048]{1,0:T(8,128)(2,1)S(1)}, u32[]{:S(2)}, u32[]{:S(2)}) collective-permute-start(bf16[512,2048]{1,0:T(8,128)(2,1)} %k0.1), channel_id=1, source_target_pairs={{0,1},{1,2},{2,3},{3,4},{4,5},{5,6},{6,7},{7,8},{8,9},{9,10},{10,1... | collective-permute-start | bytes 6291464 | tf_op jit(solution)/shard_map/ppermute | solution.py:82
  2.5 5.8 %collective-permute-start.4 = (bf16[512,2048]{1,0:T(8,128)(2,1)}, bf16[512,2048]{1,0:T(8,128)(2,1)}, u32[]{:S(2)}, u32[]{:S(2)}) collective-permute-start(bf16[512,2048]{1,0:T(8,128)(2,1)} %v0.1), channel_id=1, source_target_pairs={{0,1},{1,2},{2,3},{3,4},{4,5},{5,6},{6,7},{7,8},{8,9},{9,10},{10,1... | collective-permute-start | bytes 6291464 | tf_op jit(solution)/shard_map/ppermute | solution.py:82
  8.3 3.4 %collective-permute-start = (bf16[512,2048]{1,0:T(8,128)(2,1)}, bf16[512,2048]{1,0:T(8,128)(2,1)}, u32[]{:S(2)}, u32[]{:S(2)}) collective-permute-start(bf16[512,2048]{1,0:T(8,128)(2,1)} %k0.1), channel_id=1, source_target_pairs={{0,2},{2,4},{4,6},{6,8},{8,10},{10,12},{12,14},{16,18},{18,20},{20... | collective-permute-start | bytes 6291464 | tf_op jit(solution)/shard_map/ppermute | solution.py:83
  11.7 3.4 %collective-permute-start.3 = (bf16[512,2048]{1,0:T(8,128)(2,1)}, bf16[512,2048]{1,0:T(8,128)(2,1)}, u32[]{:S(2)}, u32[]{:S(2)}) collective-permute-start(bf16[512,2048]{1,0:T(8,128)(2,1)} %v0.1), channel_id=1, source_target_pairs={{0,2},{2,4},{4,6},{6,8},{8,10},{10,12},{12,14},{16,18},{18,20},{20... | collective-permute-start | bytes 6291464 | tf_op jit(solution)/shard_map/ppermute | solution.py:83
  15.2 0.0 collective-permute-done.1.k1
  15.2 0.0 copy-start
  15.2 32.8 %collective-permute-start.2 = (bf16[512,2048]{1,0:T(8,128)(2,1)S(1)}, bf16[512,2048]{1,0:T(8,128)(2,1)}, u32[]{:S(2)}, u32[]{:S(2)}) collective-permute-start(bf16[512,2048]{1,0:T(8,128)(2,1)S(1)} %collective-permute-done.1.k1), channel_id=1, source_target_pairs={{0,1},{2,3},{4,5},{6,7},{8,9},{10,11},{12,13},{14,15},{16,17},{18,... | collective-permute-start | bytes 6291464 | tf_op jit(solution)/shard_map/ppermute | solution.py:85
  47.9 0.0 collective-permute-done.4.v1
  47.9 44.9 %collective-permute-start.5 = (bf16[512,2048]{1,0:T(8,128)(2,1)}, bf16[512,2048]{1,0:T(8,128)(2,1)}, u32[]{:S(2)}, u32[]{:S(2)}) collective-permute-start(bf16[512,2048]{1,0:T(8,128)(2,1)} %collective-permute-done.4.v1), channel_id=1, source_target_pairs={{0,1},{2,3},{4,5},{6,7},{8,9},{10,11},{12,13},{14,15},{16,17},{18,... | collective-permute-start | bytes 6291464 | tf_op jit(solution)/shard_map/ppermute | solution.py:85
  92.9 23.7 %all-gather = s32[16,1,512]{2,1,0:T(1,128)S(1)} all-gather(s32[1,1,512]{2,1,0:T(1,128)} %bitcast.13), channel_id=1, replica_groups=mesh['grp'=2,'seq'=16] {'seq'}, dimensions={0}, use_global_device_ids=true | all-gather | bytes 34816 | tf_op jit(solution)/shard_map/all_gather | solution.py:84
  116.6 0.5 slice.21
  117.1 0.7 select_bitcast_fusion
  117.8 0.3 reduce-window.9
  118.1 0.1 slice.23
  118.2 0.1 reduce-window.12
  118.3 0.1 slice_reduce_fusion
  118.4 0.1 bitcast_subtract_fusion
  118.5 0.1 pad_dynamic-slice_fusion
  118.5 0.9 copy.6.pos_ref
  119.4 0.1 fusion.2
  119.5 2.8 %fusion = (f32[1536,64]{1,0:T(8,128)S(1)}, f32[1536,64]{1,0:T(8,128)S(1)}, f32[1536,64]{1,0:T(8,128)S(1)}) fusion(f32[64]{0:T(128)S(1)} %multiply_power_fusion, f32[1536]{0:T(1024)S(1)} %fusion.2), kind=kLoop, calls=%fused_computation.4 | loop fusion | flops 196608 | bytes 1186048 | tf_op jit(solution)/shard_map/neg | solution.py:24
  122.3 1.7 pad_maximum_fusion
  124.0 0.0 copy-done
  124.0 0.0 collective-permute-done.k2a
  124.0 0.0 collective-permute-done.3.v2a
  124.0 0.0 collective-permute-done.2.k2b
  124.0 0.0 collective-permute-done.5.v2b
  124.0 46.5 %shard_map.46 = bf16[512,4096]{1,0:T(8,128)(2,1)} custom-call(s32[1]{0:T(128)} %bitcast.par_ref, s32[512,1]{1,0:T(8,128)} %copy.6.pos_ref, f32[1536,128]{1,0:T(8,128)} %get-tuple-element.8.cos_ref, f32[1536,128]{1,0:T(8,128)} %get-tuple-element.9.sin_ref, bf16[512,4096]{1,0:T(8,128)(2,1)} %q_ref.1, bf16[512,2048]{1,0:T(8,128)(2,1)} %collective-permute-done.k2a, ...), custom_call_target="tpu_custom_call" | custom-call | tf_op jit(solution)/shard_map/pallas_call | solution.py:109
  (1 shorter events, 0.0 us)
Async XLA Ops:
  0.0 15.2 %collective-permute-start.1 = (bf16[512,2048]{1,0:T(8,128)(2,1)}, bf16[512,2048]{1,0:T(8,128)(2,1)S(1)}, u32[]{:S(2)}, u32[]{:S(2)}) collective-permute-start(bf16[512,2048]{1,0:T(8,128)(2,1)} %k0.1), channel_id=1, source_target_pairs={{0,1},{1,2},{2,3},{3,4},{4,5},{5,6},{6,7},{7,8},{8,9},{9,10},{10,1... | collective-permute-start | bytes 6291464 | tf_op jit(solution)/shard_map/ppermute | solution.py:82
  2.5 45.4 %collective-permute-start.4 = (bf16[512,2048]{1,0:T(8,128)(2,1)}, bf16[512,2048]{1,0:T(8,128)(2,1)}, u32[]{:S(2)}, u32[]{:S(2)}) collective-permute-start(bf16[512,2048]{1,0:T(8,128)(2,1)} %v0.1), channel_id=1, source_target_pairs={{0,1},{1,2},{2,3},{3,4},{4,5},{5,6},{6,7},{7,8},{8,9},{9,10},{10,1... | collective-permute-start | bytes 6291464 | tf_op jit(solution)/shard_map/ppermute | solution.py:82
  8.3 115.7 %collective-permute-start = (bf16[512,2048]{1,0:T(8,128)(2,1)}, bf16[512,2048]{1,0:T(8,128)(2,1)}, u32[]{:S(2)}, u32[]{:S(2)}) collective-permute-start(bf16[512,2048]{1,0:T(8,128)(2,1)} %k0.1), channel_id=1, source_target_pairs={{0,2},{2,4},{4,6},{6,8},{8,10},{10,12},{12,14},{16,18},{18,20},{20... | collective-permute-start | bytes 6291464 | tf_op jit(solution)/shard_map/ppermute | solution.py:83
  11.7 112.3 %collective-permute-start.3 = (bf16[512,2048]{1,0:T(8,128)(2,1)}, bf16[512,2048]{1,0:T(8,128)(2,1)}, u32[]{:S(2)}, u32[]{:S(2)}) collective-permute-start(bf16[512,2048]{1,0:T(8,128)(2,1)} %v0.1), channel_id=1, source_target_pairs={{0,2},{2,4},{4,6},{6,8},{8,10},{10,12},{12,14},{16,18},{18,20},{20... | collective-permute-start | bytes 6291464 | tf_op jit(solution)/shard_map/ppermute | solution.py:83
  15.2 108.8 %copy-start = (bf16[512,2048]{1,0:T(8,128)(2,1)}, bf16[512,2048]{1,0:T(8,128)(2,1)S(1)}, u32[]{:S(2)}) copy-start(bf16[512,2048]{1,0:T(8,128)(2,1)S(1)} %collective-permute-done.1.k1) | copy-start | bytes 6291460
  15.2 108.8 %collective-permute-start.2 = (bf16[512,2048]{1,0:T(8,128)(2,1)S(1)}, bf16[512,2048]{1,0:T(8,128)(2,1)}, u32[]{:S(2)}, u32[]{:S(2)}) collective-permute-start(bf16[512,2048]{1,0:T(8,128)(2,1)S(1)} %collective-permute-done.1.k1), channel_id=1, source_target_pairs={{0,1},{2,3},{4,5},{6,7},{8,9},{10,11},{12,13},{14,15},{16,17},{18,... | collective-permute-start | bytes 6291464 | tf_op jit(solution)/shard_map/ppermute | solution.py:85
  47.9 76.1 %collective-permute-start.5 = (bf16[512,2048]{1,0:T(8,128)(2,1)}, bf16[512,2048]{1,0:T(8,128)(2,1)}, u32[]{:S(2)}, u32[]{:S(2)}) collective-permute-start(bf16[512,2048]{1,0:T(8,128)(2,1)} %collective-permute-done.4.v1), channel_id=1, source_target_pairs={{0,1},{2,3},{4,5},{6,7},{8,9},{10,11},{12,13},{14,15},{16,17},{18,... | collective-permute-start | bytes 6291464 | tf_op jit(solution)/shard_map/ppermute | solution.py:85

commit v10 on v7

--- a/solution.py
+++ b/solution.py
@@ -124,7 +124,7 @@
     cos, sin = rope_tables(pos_win)
     pos_q = pos_win[span - rows:].reshape(rows, 1)
     parity = (shard % 2).astype(jnp.int32).reshape(1)
-    tile = 128
+    tile = 256
     heads = keys.shape[1] // HD
     kv_spec = pl.BlockSpec((rows, HD), lambda h, p: (0, h))
     full = lambda shape: pl.BlockSpec(shape, lambda h, p: (0, 0))

time: 179 us -> 168 us (0.939)
  Pallas kernels: 95.6 us -> 84.7 us
    pallas_call x2, Pallas kernels: 95.6 us -> 84.7 us  [local(): pl.pallas_call(functools.partial(attend_kernel, rows=rows, tile=tile, fir...]
  transfers between devices with their start and end apart: 6 -> 6, of which waited for: 0 -> 0; matrix products, arithmetic and copies ran while one was open for 4% -> 4% of each run, Pallas kernels for 28% -> 22%
where the time goes in v10:
time: 168 us
  Pallas kernels  84.7 us (50%)
  blocking collectives  55.6 us (33%)
  starting transfers between devices  18.8 us (11%)
  other arithmetic  5.8 us (3%)
  local copies, waits for them, and re-layouts  2.96 us (2%)
    pallas_call x2, Pallas kernels, local(): pl.pallas_call(functools.partial(attend_kernel, rows=rows, tile=tile, fir...  84.7 us
    all_gather x1, blocking collectives, local(): seg_all = lax.all_gather(segment_ids, 'seq', tiled=True)  55.6 us
    ppermute x2, starting transfers between devices, local(): lax.ppermute((keys, values), 'seq', [(s, s + 1) for s in range(count - 1)])  8.25 us
    ppermute x2, starting transfers between devices, local(): lax.ppermute((keys_b, values_b), 'seq', [(s, s + 2) for s in range(0, cou...  5.34 us
    ppermute x2, starting transfers between devices, local(): lax.ppermute(near, 'seq', [(s, s + 1) for s in range(0, count - 1, 2)])  5.25 us
  transfers between devices with their start and end apart: 6, of which 0 were waited for; matrix products, arithmetic and copies ran while one was open for 4% of the time, Pallas kernels for 22%

profile of v10, /device:TPU:0, one launch (start us, length us, event | category | flops | bytes accessed | tf_op | source)
XLA Modules:
  0.0 168.0 jit_solution(8293335804402247676)
XLA Ops:
  0.0 3.7 %collective-permute-start.1 = (bf16[512,2048]{1,0:T(8,128)(2,1)}, bf16[512,2048]{1,0:T(8,128)(2,1)}, u32[]{:S(2)}, u32[]{:S(2)}) collective-permute-start(bf16[512,2048]{1,0:T(8,128)(2,1)} %refs_1_.1), channel_id=1, source_target_pairs={{0,1},{1,2},{2,3},{3,4},{4,5},{5,6},{6,7},{7,8},{8,9},{9,10},{10,1... | collective-permute-start | bytes 6291464 | tf_op jit(solution)/shard_map/ppermute | solution.py:112
  3.7 4.5 %collective-permute-start.4 = (bf16[512,2048]{1,0:T(8,128)(2,1)}, bf16[512,2048]{1,0:T(8,128)(2,1)}, u32[]{:S(2)}, u32[]{:S(2)}) collective-permute-start(bf16[512,2048]{1,0:T(8,128)(2,1)} %refs_3_.1), channel_id=1, source_target_pairs={{0,1},{1,2},{2,3},{3,4},{4,5},{5,6},{6,7},{7,8},{8,9},{9,10},{10,1... | collective-permute-start | bytes 6291464 | tf_op jit(solution)/shard_map/ppermute | solution.py:112
  8.3 55.6 %all-gather = s32[16,1,512]{2,1,0:T(1,128)S(1)} all-gather(s32[1,1,512]{2,1,0:T(1,128)} %bitcast.13), channel_id=1, replica_groups=mesh['grp'=2,'seq'=16] {'seq'}, dimensions={0}, use_global_device_ids=true | all-gather | bytes 34816 | tf_op jit(solution)/shard_map/all_gather | solution.py:113
  63.9 1.4 collective-permute-start
  65.3 3.9 %collective-permute-start.3 = (bf16[512,2048]{1,0:T(8,128)(2,1)}, bf16[512,2048]{1,0:T(8,128)(2,1)}, u32[]{:S(2)}, u32[]{:S(2)}) collective-permute-start(bf16[512,2048]{1,0:T(8,128)(2,1)} %refs_3_.1), channel_id=1, source_target_pairs={{0,2},{2,4},{4,6},{6,8},{8,10},{10,12},{12,14},{16,18},{18,20},{20... | collective-permute-start | bytes 6291464 | tf_op jit(solution)/shard_map/ppermute | solution.py:115
  69.2 0.0 collective-permute-done.1.refs_0_
  69.2 2.6 %collective-permute-start.2 = (bf16[512,2048]{1,0:T(8,128)(2,1)}, bf16[512,2048]{1,0:T(8,128)(2,1)}, u32[]{:S(2)}, u32[]{:S(2)}) collective-permute-start(bf16[512,2048]{1,0:T(8,128)(2,1)} %collective-permute-done.1.refs_0_), channel_id=1, source_target_pairs={{0,1},{2,3},{4,5},{6,7},{8,9},{10,11},{12,13},{14,15},{16,17},{18,... | collective-permute-start | bytes 6291464 | tf_op jit(solution)/shard_map/ppermute | solution.py:116
  71.9 0.0 collective-permute-done.4.refs_2_
  71.9 2.6 %collective-permute-start.5 = (bf16[512,2048]{1,0:T(8,128)(2,1)}, bf16[512,2048]{1,0:T(8,128)(2,1)}, u32[]{:S(2)}, u32[]{:S(2)}) collective-permute-start(bf16[512,2048]{1,0:T(8,128)(2,1)} %collective-permute-done.4.refs_2_), channel_id=1, source_target_pairs={{0,1},{2,3},{4,5},{6,7},{8,9},{10,11},{12,13},{14,15},{16,17},{18,... | collective-permute-start | bytes 6291464 | tf_op jit(solution)/shard_map/ppermute | solution.py:116
  74.5 0.5 slice.16
  75.0 0.7 select_bitcast_fusion
  75.7 0.3 reduce-window.9
  76.0 0.1 slice.21
  76.1 0.1 reduce-window.12
  76.2 0.1 slice_reduce_fusion
  76.3 0.1 bitcast_subtract_fusion
  76.4 0.1 pad_dynamic-slice_fusion
  76.5 0.9 copy.8.pos_ref
  77.4 0.1 fusion.2
  77.5 2.8 %fusion = (f32[1536,64]{1,0:T(8,128)S(1)}, f32[1536,64]{1,0:T(8,128)S(1)}, f32[1536,64]{1,0:T(8,128)S(1)}) fusion(f32[64]{0:T(128)S(1)} %multiply_power_fusion, f32[1536]{0:T(1024)S(1)} %fusion.2), kind=kLoop, calls=%fused_computation.4 | loop fusion | flops 196608 | bytes 1186048 | tf_op jit(solution)/shard_map/neg | solution.py:31
  80.3 1.7 %pad_maximum_fusion = (f32[1536,128]{1,0:T(8,128)}, f32[1536,128]{1,0:T(8,128)}) fusion(f32[1536,64]{1,0:T(8,128)S(1)} %get-tuple-element.17, f32[1536,64]{1,0:T(8,128)S(1)} %get-tuple-element.16, f32[1536,64]{1,0:T(8,128)S(1)} %get-tuple-element.15), kind=kLoop, calls=%fused_computation.2 | loop fusion | flops 393216 | bytes 2752512 | tf_op jit(solution)/shard_map/concatenate | solution.py:31
  82.0 36.4 %shard_map.46 = (f32[16,512,128]{2,1,0:T(8,128)}, f32[512,4096]{1,0:T(8,128)}) custom-call(s32[1]{0:T(128)} %bitcast.par_ref, s32[512,1]{1,0:T(8,128)} %copy.8.pos_ref, f32[1536,128]{1,0:T(8,128)} %get-tuple-element.18.cos_ref, f32[1536,128]{1,0:T(8,128)} %get-tuple-element.19.sin_ref, bf16[512,4096]{1,0:T(8,128)(2,1)} %q_ref.3, ...), custom_call_target="tpu_custom_call" | custom-call | tf_op jit(solution)/shard_map/pallas_call | solution.py:136
  118.4 0.0 collective-permute-done.refs_0_
  118.4 0.0 copy-start
  118.4 0.0 collective-permute-done.3.refs_2_
  118.5 0.0 collective-permute-done.2.refs_1_
  118.5 0.0 collective-permute-done.5.refs_3_
  118.5 1.3 copy-done
  119.8 48.2 %shard_map.47 = bf16[512,4096]{1,0:T(8,128)(2,1)} custom-call(s32[1]{0:T(128)} %bitcast.par_ref, s32[512,1]{1,0:T(8,128)} %copy.8.pos_ref, f32[1536,128]{1,0:T(8,128)} %get-tuple-element.18.cos_ref, f32[1536,128]{1,0:T(8,128)} %get-tuple-element.19.sin_ref, bf16[512,4096]{1,0:T(8,128)(2,1)} %q_ref.3, bf16[512,2048]{1,0:T(8,128)(2,1)} %copy-done, ...), custom_call_target="tpu_custom_call" | custom-call | tf_op jit(solution)/shard_map/pallas_call | solution.py:147
  (1 shorter events, 0.0 us)
Async XLA Ops:
  0.0 69.2 %collective-permute-start.1 = (bf16[512,2048]{1,0:T(8,128)(2,1)}, bf16[512,2048]{1,0:T(8,128)(2,1)}, u32[]{:S(2)}, u32[]{:S(2)}) collective-permute-start(bf16[512,2048]{1,0:T(8,128)(2,1)} %refs_1_.1), channel_id=1, source_target_pairs={{0,1},{1,2},{2,3},{3,4},{4,5},{5,6},{6,7},{7,8},{8,9},{9,10},{10,1... | collective-permute-start | bytes 6291464 | tf_op jit(solution)/shard_map/ppermute | solution.py:112
  3.7 68.2 %collective-permute-start.4 = (bf16[512,2048]{1,0:T(8,128)(2,1)}, bf16[512,2048]{1,0:T(8,128)(2,1)}, u32[]{:S(2)}, u32[]{:S(2)}) collective-permute-start(bf16[512,2048]{1,0:T(8,128)(2,1)} %refs_3_.1), channel_id=1, source_target_pairs={{0,1},{1,2},{2,3},{3,4},{4,5},{5,6},{6,7},{7,8},{8,9},{9,10},{10,1... | collective-permute-start | bytes 6291464 | tf_op jit(solution)/shard_map/ppermute | solution.py:112
  63.9 54.5 %collective-permute-start = (bf16[512,2048]{1,0:T(8,128)(2,1)}, bf16[512,2048]{1,0:T(8,128)(2,1)S(1)}, u32[]{:S(2)}, u32[]{:S(2)}) collective-permute-start(bf16[512,2048]{1,0:T(8,128)(2,1)} %refs_1_.1), channel_id=1, source_target_pairs={{0,2},{2,4},{4,6},{6,8},{8,10},{10,12},{12,14},{16,18},{18,20},{20... | collective-permute-start | bytes 6291464 | tf_op jit(solution)/shard_map/ppermute | solution.py:115
  65.3 53.1 %collective-permute-start.3 = (bf16[512,2048]{1,0:T(8,128)(2,1)}, bf16[512,2048]{1,0:T(8,128)(2,1)}, u32[]{:S(2)}, u32[]{:S(2)}) collective-permute-start(bf16[512,2048]{1,0:T(8,128)(2,1)} %refs_3_.1), channel_id=1, source_target_pairs={{0,2},{2,4},{4,6},{6,8},{8,10},{10,12},{12,14},{16,18},{18,20},{20... | collective-permute-start | bytes 6291464 | tf_op jit(solution)/shard_map/ppermute | solution.py:115
  69.2 49.2 %collective-permute-start.2 = (bf16[512,2048]{1,0:T(8,128)(2,1)}, bf16[512,2048]{1,0:T(8,128)(2,1)}, u32[]{:S(2)}, u32[]{:S(2)}) collective-permute-start(bf16[512,2048]{1,0:T(8,128)(2,1)} %collective-permute-done.1.refs_0_), channel_id=1, source_target_pairs={{0,1},{2,3},{4,5},{6,7},{8,9},{10,11},{12,13},{14,15},{16,17},{18,... | collective-permute-start | bytes 6291464 | tf_op jit(solution)/shard_map/ppermute | solution.py:116
  71.9 46.6 %collective-permute-start.5 = (bf16[512,2048]{1,0:T(8,128)(2,1)}, bf16[512,2048]{1,0:T(8,128)(2,1)}, u32[]{:S(2)}, u32[]{:S(2)}) collective-permute-start(bf16[512,2048]{1,0:T(8,128)(2,1)} %collective-permute-done.4.refs_2_), channel_id=1, source_target_pairs={{0,1},{2,3},{4,5},{6,7},{8,9},{10,11},{12,13},{14,15},{16,17},{18,... | collective-permute-start | bytes 6291464 | tf_op jit(solution)/shard_map/ppermute | solution.py:116
  118.4 1.3 copy-start

commit v11 on v10

--- a/solution.py
+++ b/solution.py
@@ -70,9 +70,13 @@
         v = jnp.concatenate([v1[...], v0[...]], 0)
     k = rot(k.astype(jnp.float32), cos[first:first + nkeys], sin[first:first + nkeys])
     k = k.astype(jnp.bfloat16)
+    lane = lax.broadcasted_iota(jnp.int32, (tile, 128), 1)
     for a in range(tiles):
         lo, hi = bounds(a)
         r0 = a * tile
+        packed = []
+        if final:
+            st = st_in[0, r0:r0 + tile, :]
         kk = k[lo:hi]
         vv = v[lo:hi]
         bias = bias_ref[a, :, lo:hi]
@@ -86,20 +90,24 @@
             s = s + bias
             m = jnp.max(s, axis=1, keepdims=True)
             if final:
-                m1 = st_in[0, r0:r0 + tile, g:g + 1]
+                m1 = jnp.max(jnp.where(lane == g, st, -3e38), axis=1, keepdims=True)
+                l1 = jnp.max(jnp.where(lane == 2 + g, st, -3e38), axis=1, keepdims=True)
                 mm = jnp.maximum(m, m1)
                 scale1 = jnp.exp2((m1 - mm) * exp2_scale)
                 w = jnp.exp2((s - mm) * exp2_scale)
-                tot = jnp.sum(w, axis=1, keepdims=True) + st_in[0, r0:r0 + tile, 2 + g:3 + g] * scale1
+                tot = jnp.sum(w, axis=1, keepdims=True) + l1 * scale1
                 pv = jnp.dot(w.astype(jnp.bfloat16), vv, preferred_element_type=jnp.float32)
                 pv = pv + acc_in[r0:r0 + tile, cols] * scale1
                 o_ref[r0:r0 + tile, cols] = (pv / tot).astype(jnp.bfloat16)
             else:
                 w = jnp.exp2((s - m) * exp2_scale)
-                st_out[0, r0:r0 + tile, g:g + 1] = m
-                st_out[0, r0:r0 + tile, 2 + g:3 + g] = jnp.sum(w, axis=1, keepdims=True)
+                packed.append((m, jnp.sum(w, axis=1, keepdims=True)))
                 acc_out[r0:r0 + tile, cols] = jnp.dot(
                     w.astype(jnp.bfloat16), vv, preferred_element_type=jnp.float32)
+        if not final:
+            (m0, l0), (m1_, l1_) = packed
+            st = jnp.where(lane == 0, m0, jnp.where(lane == 1, m1_, jnp.where(lane == 2, l0, l1_)))
+            st_out[0, r0:r0 + tile, :] = st
 
 
 def local(queries, keys, values, segment_ids):

time: 168 us -> 146 us (0.87)
  Pallas kernels: 84.7 us -> 62 us
    pallas_call x2, Pallas kernels: 84.7 us -> 62 us  [local(): pl.pallas_call(functools.partial(attend_kernel, rows=rows, tile=tile, fir...]
  transfers between devices with their start and end apart: 6 -> 6, of which waited for: 0 -> 0; matrix products, arithmetic and copies ran while one was open for 4% -> 5% of each run, Pallas kernels for 22% -> 25%
where the time goes in v11:
time: 146 us; the launch traced here: 145 us
  Pallas kernels  62 us (42%)
  blocking collectives  55.6 us (38%)
  starting transfers between devices  18.8 us (13%)
  other arithmetic  5.8 us (4%)
  local copies, waits for them, and re-layouts  2.96 us (2%)
    pallas_call x2, Pallas kernels, local(): pl.pallas_call(functools.partial(attend_kernel, rows=rows, tile=tile, fir...  62 us
    all_gather x1, blocking collectives, local(): seg_all = lax.all_gather(segment_ids, 'seq', tiled=True)  55.6 us
    ppermute x2, starting transfers between devices, local(): lax.ppermute((keys, values), 'seq', [(s, s + 1) for s in range(count - 1)])  8.25 us
    ppermute x2, starting transfers between devices, local(): lax.ppermute((keys_b, values_b), 'seq', [(s, s + 2) for s in range(0, cou...  5.34 us
    ppermute x2, starting transfers between devices, local(): lax.ppermute(near, 'seq', [(s, s + 1) for s in range(0, count - 1, 2)])  5.25 us
  transfers between devices with their start and end apart: 6, of which 0 were waited for; matrix products, arithmetic and copies ran while one was open for 5% of the time, Pallas kernels for 25%

profile of v11, /device:TPU:0, one launch (start us, length us, event | category | flops | bytes accessed | tf_op | source)
XLA Modules:
  0.0 145.3 jit_solution(14057211958162911316)
XLA Ops:
  0.0 3.7 %collective-permute-start.1 = (bf16[512,2048]{1,0:T(8,128)(2,1)}, bf16[512,2048]{1,0:T(8,128)(2,1)}, u32[]{:S(2)}, u32[]{:S(2)}) collective-permute-start(bf16[512,2048]{1,0:T(8,128)(2,1)} %refs_1_.1), channel_id=1, source_target_pairs={{0,1},{1,2},{2,3},{3,4},{4,5},{5,6},{6,7},{7,8},{8,9},{9,10},{10,1... | collective-permute-start | bytes 6291464 | tf_op jit(solution)/shard_map/ppermute | solution.py:120
  3.7 4.5 %collective-permute-start.4 = (bf16[512,2048]{1,0:T(8,128)(2,1)}, bf16[512,2048]{1,0:T(8,128)(2,1)}, u32[]{:S(2)}, u32[]{:S(2)}) collective-permute-start(bf16[512,2048]{1,0:T(8,128)(2,1)} %refs_3_.1), channel_id=1, source_target_pairs={{0,1},{1,2},{2,3},{3,4},{4,5},{5,6},{6,7},{7,8},{8,9},{9,10},{10,1... | collective-permute-start | bytes 6291464 | tf_op jit(solution)/shard_map/ppermute | solution.py:120
  8.3 55.6 %all-gather = s32[16,1,512]{2,1,0:T(1,128)S(1)} all-gather(s32[1,1,512]{2,1,0:T(1,128)} %bitcast.13), channel_id=1, replica_groups=mesh['grp'=2,'seq'=16] {'seq'}, dimensions={0}, use_global_device_ids=true | all-gather | bytes 34816 | tf_op jit(solution)/shard_map/all_gather | solution.py:121
  63.9 1.4 collective-permute-start
  65.3 3.9 %collective-permute-start.3 = (bf16[512,2048]{1,0:T(8,128)(2,1)}, bf16[512,2048]{1,0:T(8,128)(2,1)}, u32[]{:S(2)}, u32[]{:S(2)}) collective-permute-start(bf16[512,2048]{1,0:T(8,128)(2,1)} %refs_3_.1), channel_id=1, source_target_pairs={{0,2},{2,4},{4,6},{6,8},{8,10},{10,12},{12,14},{16,18},{18,20},{20... | collective-permute-start | bytes 6291464 | tf_op jit(solution)/shard_map/ppermute | solution.py:123
  69.2 0.0 collective-permute-done.1.refs_0_
  69.2 2.6 %collective-permute-start.2 = (bf16[512,2048]{1,0:T(8,128)(2,1)}, bf16[512,2048]{1,0:T(8,128)(2,1)}, u32[]{:S(2)}, u32[]{:S(2)}) collective-permute-start(bf16[512,2048]{1,0:T(8,128)(2,1)} %collective-permute-done.1.refs_0_), channel_id=1, source_target_pairs={{0,1},{2,3},{4,5},{6,7},{8,9},{10,11},{12,13},{14,15},{16,17},{18,... | collective-permute-start | bytes 6291464 | tf_op jit(solution)/shard_map/ppermute | solution.py:124
  71.9 0.0 collective-permute-done.4.refs_2_
  71.9 2.6 %collective-permute-start.5 = (bf16[512,2048]{1,0:T(8,128)(2,1)}, bf16[512,2048]{1,0:T(8,128)(2,1)}, u32[]{:S(2)}, u32[]{:S(2)}) collective-permute-start(bf16[512,2048]{1,0:T(8,128)(2,1)} %collective-permute-done.4.refs_2_), channel_id=1, source_target_pairs={{0,1},{2,3},{4,5},{6,7},{8,9},{10,11},{12,13},{14,15},{16,17},{18,... | collective-permute-start | bytes 6291464 | tf_op jit(solution)/shard_map/ppermute | solution.py:124
  74.5 0.5 slice.16
  75.0 0.7 select_bitcast_fusion
  75.7 0.3 reduce-window.9
  76.0 0.1 slice.21
  76.1 0.1 reduce-window.12
  76.2 0.1 slice_reduce_fusion
  76.3 0.1 bitcast_subtract_fusion
  76.4 0.1 pad_dynamic-slice_fusion
  76.5 0.9 copy.8.pos_ref
  77.4 0.1 fusion.2
  77.5 2.8 %fusion = (f32[1536,64]{1,0:T(8,128)S(1)}, f32[1536,64]{1,0:T(8,128)S(1)}, f32[1536,64]{1,0:T(8,128)S(1)}) fusion(f32[64]{0:T(128)S(1)} %multiply_power_fusion, f32[1536]{0:T(1024)S(1)} %fusion.2), kind=kLoop, calls=%fused_computation.4 | loop fusion | flops 196608 | bytes 1186048 | tf_op jit(solution)/shard_map/neg | solution.py:31
  80.3 1.7 %pad_maximum_fusion = (f32[1536,128]{1,0:T(8,128)}, f32[1536,128]{1,0:T(8,128)}) fusion(f32[1536,64]{1,0:T(8,128)S(1)} %get-tuple-element.17, f32[1536,64]{1,0:T(8,128)S(1)} %get-tuple-element.16, f32[1536,64]{1,0:T(8,128)S(1)} %get-tuple-element.15), kind=kLoop, calls=%fused_computation.2 | loop fusion | flops 393216 | bytes 2752512 | tf_op jit(solution)/shard_map/concatenate | solution.py:31
  82.0 36.4 %shard_map.46 = (f32[16,512,128]{2,1,0:T(8,128)}, f32[512,4096]{1,0:T(8,128)}) custom-call(s32[1]{0:T(128)} %bitcast.par_ref, s32[512,1]{1,0:T(8,128)} %copy.8.pos_ref, f32[1536,128]{1,0:T(8,128)} %get-tuple-element.18.cos_ref, f32[1536,128]{1,0:T(8,128)} %get-tuple-element.19.sin_ref, bf16[512,4096]{1,0:T(8,128)(2,1)} %q_ref.3, ...), custom_call_target="tpu_custom_call" | custom-call | tf_op jit(solution)/shard_map/pallas_call | solution.py:144
  118.4 0.0 collective-permute-done.refs_0_
  118.4 0.0 copy-start
  118.4 0.0 collective-permute-done.3.refs_2_
  118.5 0.0 collective-permute-done.2.refs_1_
  118.5 0.0 collective-permute-done.5.refs_3_
  118.5 1.3 copy-done
  119.8 25.6 %shard_map.47 = bf16[512,4096]{1,0:T(8,128)(2,1)} custom-call(s32[1]{0:T(128)} %bitcast.par_ref, s32[512,1]{1,0:T(8,128)} %copy.8.pos_ref, f32[1536,128]{1,0:T(8,128)} %get-tuple-element.18.cos_ref, f32[1536,128]{1,0:T(8,128)} %get-tuple-element.19.sin_ref, bf16[512,4096]{1,0:T(8,128)(2,1)} %q_ref.3, bf16[512,2048]{1,0:T(8,128)(2,1)} %copy-done, ...), custom_call_target="tpu_custom_call" | custom-call | tf_op jit(solution)/shard_map/pallas_call | solution.py:155
  (1 shorter events, 0.0 us)
Async XLA Ops:
  0.0 69.2 %collective-permute-start.1 = (bf16[512,2048]{1,0:T(8,128)(2,1)}, bf16[512,2048]{1,0:T(8,128)(2,1)}, u32[]{:S(2)}, u32[]{:S(2)}) collective-permute-start(bf16[512,2048]{1,0:T(8,128)(2,1)} %refs_1_.1), channel_id=1, source_target_pairs={{0,1},{1,2},{2,3},{3,4},{4,5},{5,6},{6,7},{7,8},{8,9},{9,10},{10,1... | collective-permute-start | bytes 6291464 | tf_op jit(solution)/shard_map/ppermute | solution.py:120
  3.7 68.2 %collective-permute-start.4 = (bf16[512,2048]{1,0:T(8,128)(2,1)}, bf16[512,2048]{1,0:T(8,128)(2,1)}, u32[]{:S(2)}, u32[]{:S(2)}) collective-permute-start(bf16[512,2048]{1,0:T(8,128)(2,1)} %refs_3_.1), channel_id=1, source_target_pairs={{0,1},{1,2},{2,3},{3,4},{4,5},{5,6},{6,7},{7,8},{8,9},{9,10},{10,1... | collective-permute-start | bytes 6291464 | tf_op jit(solution)/shard_map/ppermute | solution.py:120
  63.9 54.5 %collective-permute-start = (bf16[512,2048]{1,0:T(8,128)(2,1)}, bf16[512,2048]{1,0:T(8,128)(2,1)S(1)}, u32[]{:S(2)}, u32[]{:S(2)}) collective-permute-start(bf16[512,2048]{1,0:T(8,128)(2,1)} %refs_1_.1), channel_id=1, source_target_pairs={{0,2},{2,4},{4,6},{6,8},{8,10},{10,12},{12,14},{16,18},{18,20},{20... | collective-permute-start | bytes 6291464 | tf_op jit(solution)/shard_map/ppermute | solution.py:123
  65.3 53.1 %collective-permute-start.3 = (bf16[512,2048]{1,0:T(8,128)(2,1)}, bf16[512,2048]{1,0:T(8,128)(2,1)}, u32[]{:S(2)}, u32[]{:S(2)}) collective-permute-start(bf16[512,2048]{1,0:T(8,128)(2,1)} %refs_3_.1), channel_id=1, source_target_pairs={{0,2},{2,4},{4,6},{6,8},{8,10},{10,12},{12,14},{16,18},{18,20},{20... | collective-permute-start | bytes 6291464 | tf_op jit(solution)/shard_map/ppermute | solution.py:123
  69.2 49.2 %collective-permute-start.2 = (bf16[512,2048]{1,0:T(8,128)(2,1)}, bf16[512,2048]{1,0:T(8,128)(2,1)}, u32[]{:S(2)}, u32[]{:S(2)}) collective-permute-start(bf16[512,2048]{1,0:T(8,128)(2,1)} %collective-permute-done.1.refs_0_), channel_id=1, source_target_pairs={{0,1},{2,3},{4,5},{6,7},{8,9},{10,11},{12,13},{14,15},{16,17},{18,... | collective-permute-start | bytes 6291464 | tf_op jit(solution)/shard_map/ppermute | solution.py:124
  71.9 46.6 %collective-permute-start.5 = (bf16[512,2048]{1,0:T(8,128)(2,1)}, bf16[512,2048]{1,0:T(8,128)(2,1)}, u32[]{:S(2)}, u32[]{:S(2)}) collective-permute-start(bf16[512,2048]{1,0:T(8,128)(2,1)} %collective-permute-done.4.refs_2_), channel_id=1, source_target_pairs={{0,1},{2,3},{4,5},{6,7},{8,9},{10,11},{12,13},{14,15},{16,17},{18,... | collective-permute-start | bytes 6291464 | tf_op jit(solution)/shard_map/ppermute | solution.py:124
  118.4 1.3 copy-start

commit v12 on v11

--- a/solution.py
+++ b/solution.py
@@ -117,10 +117,11 @@
     span = (hops + 1) * rows
     shard = lax.axis_index("seq")
     count = lax.axis_size("seq")
-    near = lax.ppermute((keys, values), "seq", [(s, s + 1) for s in range(count - 1)])
+    both = jnp.concatenate([keys, values], 1)
+    near = lax.ppermute(both, "seq", [(s, s + 1) for s in range(count - 1)])
     seg_all = lax.all_gather(segment_ids, "seq", tiled=True)
-    keys_b, values_b, seg_all = lax.optimization_barrier((keys, values, seg_all))
-    far = lax.ppermute((keys_b, values_b), "seq", [(s, s + 2) for s in range(0, count - 2, 2)])
+    both, seg_all = lax.optimization_barrier((both, seg_all))
+    far = lax.ppermute(both, "seq", [(s, s + 2) for s in range(0, count - 2, 2)])
     relay = lax.ppermute(near, "seq", [(s, s + 1) for s in range(0, count - 1, 2)])
     total = seg_all.shape[0]
     places = jnp.arange(total, dtype=jnp.int32)
@@ -135,6 +136,7 @@
     tile = 256
     heads = keys.shape[1] // HD
     kv_spec = pl.BlockSpec((rows, HD), lambda h, p: (0, h))
+    v_spec = pl.BlockSpec((rows, HD), lambda h, p: (0, h + heads))
     full = lambda shape: pl.BlockSpec(shape, lambda h, p: (0, 0))
     head_spec = pl.BlockSpec((rows, 2 * HD), lambda h, p: (0, h))
     stat_spec = pl.BlockSpec((1, rows, 128), lambda h, p: (h, 0, 0))
@@ -145,23 +147,23 @@
         functools.partial(attend_kernel, rows=rows, tile=tile, first=rows, final=False),
         grid_spec=pltpu.PrefetchScalarGridSpec(
             num_scalar_prefetch=1, grid=(heads,),
-            in_specs=lead + [kv_spec] * 4,
+            in_specs=lead + [kv_spec, kv_spec, v_spec, kv_spec],
             out_specs=[stat_spec, head_spec],
             scratch_shapes=[pltpu.VMEM((rows // tile, tile, 2 * rows), f32)]),
         out_shape=[jax.ShapeDtypeStruct((heads, rows, 128), f32),
                    jax.ShapeDtypeStruct(queries.shape, f32)],
         compiler_params=params,
-    )(parity, pos_q, cos, sin, queries, near[0], keys, near[1], values)
+    )(parity, pos_q, cos, sin, queries, near, keys, near, values)
     return pl.pallas_call(
         functools.partial(attend_kernel, rows=rows, tile=tile, first=0, final=True),
         grid_spec=pltpu.PrefetchScalarGridSpec(
             num_scalar_prefetch=1, grid=(heads,),
-            in_specs=lead + [kv_spec] * 4 + [stat_spec, head_spec],
+            in_specs=lead + [kv_spec, kv_spec, v_spec, v_spec] + [stat_spec, head_spec],
             out_specs=head_spec,
             scratch_shapes=[pltpu.VMEM((rows // tile, tile, rows), f32)]),
         out_shape=jax.ShapeDtypeStruct(queries.shape, jnp.bfloat16),
         compiler_params=params,
-    )(parity, pos_q, cos, sin, queries, far[0], relay[0], far[1], relay[1], stats, acc1)
+    )(parity, pos_q, cos, sin, queries, far, relay, far, relay, stats, acc1)
 
 
 def solution(mesh):

time: 146 us -> 146 us (level)
  starting transfers between devices: 18.8 us -> 11 us
  blocking collectives: 55.6 us -> 59.5 us
  local copies, waits for them, and re-layouts: 2.96 us -> 6.5 us
    ppermute x4 -> x2, starting transfers between devices: 13.6 us -> 7.62 us  [the longest x1 4.35 us: local(): near = lax.ppermute(both, 'seq', [(s, s + 1) for s in range(count - 1)])]
    all_gather x1, blocking collectives: 55.6 us -> 59.5 us  [local(): seg_all = lax.all_gather(segment_ids, 'seq', tiled=True)]
    unnamed x2 -> x5, local copies, waits for them, and re-layouts: 1.3 us -> 3.31 us
    ppermute x2 -> x1, starting transfers between devices: 5.25 us -> 3.36 us  [local(): lax.ppermute(near, 'seq', [(s, s + 1) for s in range(0, count - 1, 2)])]
  transfers between devices with their start and end apart: 6 -> 3, of which waited for: 0 -> 0; matrix products, arithmetic and copies ran while one was open for 5% -> 5% of each run, Pallas kernels for 25% -> 25%
where the time goes in v12:
time: 146 us; the launch traced here: 145 us
  Pallas kernels  62.1 us (43%)
  blocking collectives  59.5 us (41%)
  starting transfers between devices  11 us (8%)
  local copies, waits for them, and re-layouts  6.5 us (4%)
  other arithmetic  5.85 us (4%)
    pallas_call x2, Pallas kernels, local(): pl.pallas_call(functools.partial(attend_kernel, rows=rows, tile=tile, fir...  62.1 us
    all_gather x1, blocking collectives, local(): seg_all = lax.all_gather(segment_ids, 'seq', tiled=True)  59.5 us
    ppermute x1, starting transfers between devices, local(): near = lax.ppermute(both, 'seq', [(s, s + 1) for s in range(count - 1)])  4.35 us
    ppermute x1, starting transfers between devices, local(): lax.ppermute(near, 'seq', [(s, s + 1) for s in range(0, count - 1, 2)])  3.36 us
    unnamed x5, local copies, waits for them, and re-layouts  3.31 us
    ppermute x1, starting transfers between devices, local(): lax.ppermute(both, 'seq', [(s, s + 2) for s in range(0, count - 2, 2)])  3.26 us
  transfers between devices with their start and end apart: 3, of which 0 were waited for; matrix products, arithmetic and copies ran while one was open for 5% of the time, Pallas kernels for 25%

profile of v12, /device:TPU:0, one launch (start us, length us, event | category | flops | bytes accessed | tf_op | source)
XLA Modules:
  0.0 145.0 jit_solution(13852957795430302703)
XLA Ops:
  0.0 0.0 copy-start
  0.0 0.0 copy-start.1
  0.0 3.3 %constant_dynamic-update-slice_fusion.1 = bf16[512,4096]{1,0:T(8,128)(2,1)} fusion(bf16[512,2048]{1,0:T(8,128)(2,1)} %refs_1_.1), kind=kLoop, calls=%fused_computation.15 | loop fusion | bytes 4194304
  3.3 0.0 copy-done
  3.3 1.5 %constant_dynamic-update-slice_fusion = bf16[512,4096]{1,0:T(8,128)(2,1)} fusion(bf16[512,4096]{1,0:T(8,128)(2,1)} %constant_dynamic-update-slice_fusion.1, bf16[512,2048]{1,0:T(8,128)(2,1)S(1)} %copy-done), kind=kLoop, calls=%fused_computation.14 | loop fusion | bytes 4194304 | tf_op jit(solution)/shard_map/concatenate | solution.py:120
  4.8 4.4 %collective-permute-start.1 = (bf16[512,4096]{1,0:T(8,128)(2,1)}, bf16[512,4096]{1,0:T(8,128)(2,1)}, u32[]{:S(2)}, u32[]{:S(2)}) collective-permute-start(bf16[512,4096]{1,0:T(8,128)(2,1)} %constant_dynamic-update-slice_fusion), channel_id=1, source_target_pairs={{0,1},{1,2},{2,3},{3,4},{4,5},{5,6},{6,7},{7,8},{8,9},{9,10},{10,1... | collective-permute-start | bytes 12582920 | tf_op jit(solution)/shard_map/ppermute | solution.py:121
  9.1 0.0 copy-done.1
  9.1 59.5 %all-gather = s32[16,1,512]{2,1,0:T(1,128)S(1)} all-gather(s32[1,1,512]{2,1,0:T(1,128)S(1)} %bitcast.13), channel_id=1, replica_groups=mesh['grp'=2,'seq'=16] {'seq'}, dimensions={0}, use_global_device_ids=true | all-gather | bytes 34816 | tf_op jit(solution)/shard_map/all_gather | solution.py:122
  68.7 3.3 %collective-permute-start = (bf16[512,4096]{1,0:T(8,128)(2,1)}, bf16[512,4096]{1,0:T(8,128)(2,1)}, u32[]{:S(2)}, u32[]{:S(2)}) collective-permute-start(bf16[512,4096]{1,0:T(8,128)(2,1)} %constant_dynamic-update-slice_fusion), channel_id=1, source_target_pairs={{0,2},{2,4},{4,6},{6,8},{8,10},{10,12},{12,14},{16,18},{18,20},{20... | collective-permute-start | bytes 12582920 | tf_op jit(solution)/shard_map/ppermute | solution.py:124
  71.9 0.0 collective-permute-done.1.refs_0_.refs_2_
  71.9 3.4 %collective-permute-start.2 = (bf16[512,4096]{1,0:T(8,128)(2,1)}, bf16[512,4096]{1,0:T(8,128)(2,1)}, u32[]{:S(2)}, u32[]{:S(2)}) collective-permute-start(bf16[512,4096]{1,0:T(8,128)(2,1)} %collective-permute-done.1.refs_0_.refs_2_), channel_id=1, source_target_pairs={{0,1},{2,3},{4,5},{6,7},{8,9},{10,11},{12,13},{14,15},{16,17},{18,... | collective-permute-start | bytes 12582920 | tf_op jit(solution)/shard_map/ppermute | solution.py:125
  75.3 0.6 slice.16
  75.9 0.8 select_bitcast_fusion
  76.6 0.3 reduce-window.9
  76.9 0.1 slice.21
  77.0 0.1 reduce-window.12
  77.1 0.1 slice_reduce_fusion
  77.2 0.1 bitcast_subtract_fusion
  77.3 0.1 pad_dynamic-slice_fusion
  77.4 0.9 copy.8.pos_ref
  78.3 0.1 fusion.2
  78.4 2.8 %fusion = (f32[1536,64]{1,0:T(8,128)S(1)}, f32[1536,64]{1,0:T(8,128)S(1)}, f32[1536,64]{1,0:T(8,128)S(1)}) fusion(f32[64]{0:T(128)S(1)} %multiply_power_fusion, f32[1536]{0:T(1024)S(1)} %fusion.2), kind=kLoop, calls=%fused_computation.4 | loop fusion | flops 196608 | bytes 1186048 | tf_op jit(solution)/shard_map/neg | solution.py:31
  81.2 1.7 %pad_maximum_fusion = (f32[1536,128]{1,0:T(8,128)}, f32[1536,128]{1,0:T(8,128)}) fusion(f32[1536,64]{1,0:T(8,128)S(1)} %get-tuple-element.15, f32[1536,64]{1,0:T(8,128)S(1)} %get-tuple-element.14, f32[1536,64]{1,0:T(8,128)S(1)} %get-tuple-element.13), kind=kLoop, calls=%fused_computation.2 | loop fusion | flops 393216 | bytes 2752512 | tf_op jit(solution)/shard_map/concatenate | solution.py:31
  82.9 36.6 %shard_map.46 = (f32[16,512,128]{2,1,0:T(8,128)}, f32[512,4096]{1,0:T(8,128)}) custom-call(s32[1]{0:T(128)} %bitcast.par_ref, s32[512,1]{1,0:T(8,128)} %copy.8.pos_ref, f32[1536,128]{1,0:T(8,128)} %get-tuple-element.16.cos_ref, f32[1536,128]{1,0:T(8,128)} %get-tuple-element.17.sin_ref, bf16[512,4096]{1,0:T(8,128)(2,1)} %q_ref.3, ...), custom_call_target="tpu_custom_call" | custom-call | tf_op jit(solution)/shard_map/pallas_call | solution.py:146
  119.5 0.0 collective-permute-done.refs_0_.refs_2_
  119.5 0.0 collective-permute-done.2.refs_1_.refs_3_
  119.5 25.5 %shard_map.47 = bf16[512,4096]{1,0:T(8,128)(2,1)} custom-call(s32[1]{0:T(128)} %bitcast.par_ref, s32[512,1]{1,0:T(8,128)} %copy.8.pos_ref, f32[1536,128]{1,0:T(8,128)} %get-tuple-element.16.cos_ref, f32[1536,128]{1,0:T(8,128)} %get-tuple-element.17.sin_ref, bf16[512,4096]{1,0:T(8,128)(2,1)} %q_ref.3, bf16[512,4096]{1,0:T(8,128)(2,1)} %collective-permute-done.refs_0_.refs_2_, ...), custom_call_target="tpu_custom_call" | custom-call | tf_op jit(solution)/shard_map/pallas_call | solution.py:157
  (1 shorter events, 0.0 us)
Async XLA Ops:
  0.0 3.3 %copy-start = (bf16[512,2048]{1,0:T(8,128)(2,1)S(1)}, bf16[512,2048]{1,0:T(8,128)(2,1)}, u32[]{:S(2)}) copy-start(bf16[512,2048]{1,0:T(8,128)(2,1)} %refs_3_.1) | copy-start | bytes 6291460
  0.0 9.1 %copy-start.1 = (s32[512]{0:T(512)S(1)}, s32[512]{0:T(512)}, u32[]{:S(2)}) copy-start(s32[512]{0:T(512)} %param.7) | copy-start | bytes 6148
  4.8 67.2 %collective-permute-start.1 = (bf16[512,4096]{1,0:T(8,128)(2,1)}, bf16[512,4096]{1,0:T(8,128)(2,1)}, u32[]{:S(2)}, u32[]{:S(2)}) collective-permute-start(bf16[512,4096]{1,0:T(8,128)(2,1)} %constant_dynamic-update-slice_fusion), channel_id=1, source_target_pairs={{0,1},{1,2},{2,3},{3,4},{4,5},{5,6},{6,7},{7,8},{8,9},{9,10},{10,1... | collective-permute-start | bytes 12582920 | tf_op jit(solution)/shard_map/ppermute | solution.py:121
  68.7 50.8 %collective-permute-start = (bf16[512,4096]{1,0:T(8,128)(2,1)}, bf16[512,4096]{1,0:T(8,128)(2,1)}, u32[]{:S(2)}, u32[]{:S(2)}) collective-permute-start(bf16[512,4096]{1,0:T(8,128)(2,1)} %constant_dynamic-update-slice_fusion), channel_id=1, source_target_pairs={{0,2},{2,4},{4,6},{6,8},{8,10},{10,12},{12,14},{16,18},{18,20},{20... | collective-permute-start | bytes 12582920 | tf_op jit(solution)/shard_map/ppermute | solution.py:124
  71.9 47.6 %collective-permute-start.2 = (bf16[512,4096]{1,0:T(8,128)(2,1)}, bf16[512,4096]{1,0:T(8,128)(2,1)}, u32[]{:S(2)}, u32[]{:S(2)}) collective-permute-start(bf16[512,4096]{1,0:T(8,128)(2,1)} %collective-permute-done.1.refs_0_.refs_2_), channel_id=1, source_target_pairs={{0,1},{2,3},{4,5},{6,7},{8,9},{10,11},{12,13},{14,15},{16,17},{18,... | collective-permute-start | bytes 12582920 | tf_op jit(solution)/shard_map/ppermute | solution.py:125

commit v13 on v12

--- a/solution.py
+++ b/solution.py
@@ -117,12 +117,10 @@
     span = (hops + 1) * rows
     shard = lax.axis_index("seq")
     count = lax.axis_size("seq")
+    seg_all = lax.all_gather(segment_ids, "seq", tiled=True)
+    keys, values, seg_all = lax.optimization_barrier((keys, values, seg_all))
     both = jnp.concatenate([keys, values], 1)
     near = lax.ppermute(both, "seq", [(s, s + 1) for s in range(count - 1)])
-    seg_all = lax.all_gather(segment_ids, "seq", tiled=True)
-    both, seg_all = lax.optimization_barrier((both, seg_all))
-    far = lax.ppermute(both, "seq", [(s, s + 2) for s in range(0, count - 2, 2)])
-    relay = lax.ppermute(near, "seq", [(s, s + 1) for s in range(0, count - 1, 2)])
     total = seg_all.shape[0]
     places = jnp.arange(total, dtype=jnp.int32)
     previous = jnp.concatenate([seg_all[:1], seg_all[:-1]])
@@ -133,6 +131,9 @@
     cos, sin = rope_tables(pos_win)
     pos_q = pos_win[span - rows:].reshape(rows, 1)
     parity = (shard % 2).astype(jnp.int32).reshape(1)
+    both, near, cos, sin, pos_q = lax.optimization_barrier((both, near, cos, sin, pos_q))
+    far = lax.ppermute(both, "seq", [(s, s + 2) for s in range(0, count - 2, 2)])
+    relay = lax.ppermute(near, "seq", [(s, s + 1) for s in range(0, count - 1, 2)])
     tile = 256
     heads = keys.shape[1] // HD
     kv_spec = pl.BlockSpec((rows, HD), lambda h, p: (0, h))

time: 146 us -> 153 us (1.048)
  starting transfers between devices: 11 us -> 50.7 us
  blocking collectives: 59.5 us -> 23.6 us
  waiting for transfers between devices: 0.01 us -> 3.7 us
    ppermute x1, starting transfers between devices: 3.26 us -> 43.3 us  [local(): lax.ppermute(both, 'seq', [(s, s + 2) for s in range(0, count - 2, 2)])]
    all_gather x1, blocking collectives: 59.5 us -> 23.6 us  [local(): seg_all = lax.all_gather(segment_ids, 'seq', tiled=True)]
    ppermute x1, waiting for transfers between devices: 0.01 us -> 3.7 us  [local(): lax.ppermute(both, 'seq', [(s, s + 2) for s in range(0, count - 2, 2)])]
    unnamed x5 -> x3, local copies, waits for them, and re-layouts: 3.31 us -> 3.16 us
  transfers between devices with their start and end apart: 3 -> 3, of which waited for: 0 -> 1; matrix products, arithmetic and copies ran while one was open for 5% -> 5% of each run, Pallas kernels for 25% -> 24%
where the time goes in v13:
time: 153 us; the launch traced here: 152 us
  Pallas kernels  62.1 us (41%)
  starting transfers between devices  50.7 us (33%)
  blocking collectives  23.6 us (15%)
  local copies, waits for them, and re-layouts  6.35 us (4%)
  other arithmetic  5.84 us (4%)
  waiting for transfers between devices  3.7 us (2%)
    pallas_call x2, Pallas kernels, local(): pl.pallas_call(functools.partial(attend_kernel, rows=rows, tile=tile, fir...  62.1 us
    ppermute x1, starting transfers between devices, local(): lax.ppermute(both, 'seq', [(s, s + 2) for s in range(0, count - 2, 2)])  43.3 us
    all_gather x1, blocking collectives, local(): seg_all = lax.all_gather(segment_ids, 'seq', tiled=True)  23.6 us
    ppermute x1, starting transfers between devices, local(): near = lax.ppermute(both, 'seq', [(s, s + 1) for s in range(count - 1)])  4.22 us
    ppermute x1, waiting for transfers between devices, local(): lax.ppermute(both, 'seq', [(s, s + 2) for s in range(0, count - 2, 2)])  3.7 us
    ppermute x1, starting transfers between devices, local(): lax.ppermute(near, 'seq', [(s, s + 1) for s in range(0, count - 1, 2)])  3.21 us
    unnamed x3, local copies, waits for them, and re-layouts  3.16 us
  transfers between devices with their start and end apart: 3, of which 1 were waited for; matrix products, arithmetic and copies ran while one was open for 5% of the time, Pallas kernels for 24%

profile of v13, /device:TPU:0, one launch (start us, length us, event | category | flops | bytes accessed | tf_op | source)
XLA Modules:
  0.0 152.3 jit_solution(17271643341475351224)
XLA Ops:
  0.0 0.0 copy-start
  0.0 23.6 %all-gather = s32[16,1,512]{2,1,0:T(1,128)S(1)} all-gather(s32[1,1,512]{2,1,0:T(1,128)} %bitcast.13), channel_id=1, replica_groups=mesh['grp'=2,'seq'=16] {'seq'}, dimensions={0}, use_global_device_ids=true | all-gather | bytes 34816 | tf_op jit(solution)/shard_map/all_gather | solution.py:120
  23.6 3.2 %constant_dynamic-update-slice_fusion.1 = bf16[512,4096]{1,0:T(8,128)(2,1)} fusion(bf16[512,2048]{1,0:T(8,128)(2,1)} %refs_1_), kind=kLoop, calls=%fused_computation.15 | loop fusion | bytes 4194304
  26.7 0.0 copy-done
  26.7 1.5 constant_dynamic-update-slice_fusion
  28.2 4.2 %collective-permute-start = (bf16[512,4096]{1,0:T(8,128)(2,1)}, bf16[512,4096]{1,0:T(8,128)(2,1)}, u32[]{:S(2)}, u32[]{:S(2)}) collective-permute-start(bf16[512,4096]{1,0:T(8,128)(2,1)} %constant_dynamic-update-slice_fusion), channel_id=1, source_target_pairs={{0,1},{1,2},{2,3},{3,4},{4,5},{5,6},{6,7},{7,8},{8,9},{9,10},{10,1... | collective-permute-start | bytes 12582920 | tf_op jit(solution)/shard_map/ppermute | solution.py:123
  32.4 0.6 slice.16
  33.0 0.8 select_bitcast_fusion
  33.8 0.3 reduce-window.9
  34.0 0.1 slice.21
  34.1 0.1 reduce-window.12
  34.2 0.1 slice_reduce_fusion
  34.4 0.1 bitcast_subtract_fusion
  34.4 0.1 pad_dynamic-slice_fusion
  34.5 0.1 fusion.2
  34.6 2.8 %fusion = (f32[1536,64]{1,0:T(8,128)S(1)}, f32[1536,64]{1,0:T(8,128)S(1)}, f32[1536,64]{1,0:T(8,128)S(1)}) fusion(f32[64]{0:T(128)S(1)} %multiply_power_fusion, f32[1536]{0:T(1024)S(1)} %fusion.2), kind=kLoop, calls=%fused_computation.4 | loop fusion | flops 196608 | bytes 1186048 | tf_op jit(solution)/shard_map/neg | solution.py:31
  37.4 1.7 %pad_maximum_fusion = (f32[1536,128]{1,0:T(8,128)}, f32[1536,128]{1,0:T(8,128)}) fusion(f32[1536,64]{1,0:T(8,128)S(1)} %get-tuple-element.27, f32[1536,64]{1,0:T(8,128)S(1)} %get-tuple-element.26, f32[1536,64]{1,0:T(8,128)S(1)} %get-tuple-element.25), kind=kLoop, calls=%fused_computation.2 | loop fusion | flops 393216 | bytes 2752512 | tf_op jit(solution)/shard_map/concatenate | solution.py:31
  39.1 0.0 collective-permute-done.refs_0_.refs_2_
  39.1 43.3 %collective-permute-start.1 = (bf16[512,4096]{1,0:T(8,128)(2,1)}, bf16[512,4096]{1,0:T(8,128)(2,1)}, u32[]{:S(2)}, u32[]{:S(2)}) collective-permute-start(bf16[512,4096]{1,0:T(8,128)(2,1)} %constant_dynamic-update-slice_fusion), channel_id=1, source_target_pairs={{0,2},{2,4},{4,6},{6,8},{8,10},{10,12},{12,14},{16,18},{18,20},{20... | collective-permute-start | bytes 12582920 | tf_op jit(solution)/shard_map/ppermute | solution.py:135
  82.4 3.2 %collective-permute-start.2 = (bf16[512,4096]{1,0:T(8,128)(2,1)}, bf16[512,4096]{1,0:T(8,128)(2,1)}, u32[]{:S(2)}, u32[]{:S(2)}) collective-permute-start(bf16[512,4096]{1,0:T(8,128)(2,1)} %collective-permute-done.refs_0_.refs_2_), channel_id=1, source_target_pairs={{0,1},{2,3},{4,5},{6,7},{8,9},{10,11},{12,13},{14,15},{16,17},{18,... | collective-permute-start | bytes 12582920 | tf_op jit(solution)/shard_map/ppermute | solution.py:136
  85.6 0.9 copy.8.pos_ref
  86.5 36.6 %shard_map.46 = (f32[16,512,128]{2,1,0:T(8,128)}, f32[512,4096]{1,0:T(8,128)}) custom-call(s32[1]{0:T(128)} %bitcast.par_ref, s32[512,1]{1,0:T(8,128)} %copy.8.pos_ref, f32[1536,128]{1,0:T(8,128)} %get-tuple-element.19.cos_ref, f32[1536,128]{1,0:T(8,128)} %get-tuple-element.20.sin_ref, bf16[512,4096]{1,0:T(8,128)(2,1)} %q_ref.3, ...), custom_call_target="tpu_custom_call" | custom-call | tf_op jit(solution)/shard_map/pallas_call | solution.py:147
  123.1 3.7 %collective-permute-done.1.refs_0_.refs_2_ = bf16[512,4096]{1,0:T(8,128)(2,1)} collective-permute-done((bf16[512,4096]{1,0:T(8,128)(2,1)}, bf16[512,4096]{1,0:T(8,128)(2,1)}, u32[]{:S(2)}, u32[]{:S(2)}) %collective-permute-start.1) | collective-permute-done | bytes 4194336 | tf_op jit(solution)/shard_map/ppermute | solution.py:135
  126.8 0.0 collective-permute-done.2.refs_1_.refs_3_
  126.8 25.5 %shard_map.47 = bf16[512,4096]{1,0:T(8,128)(2,1)} custom-call(s32[1]{0:T(128)} %bitcast.par_ref, s32[512,1]{1,0:T(8,128)} %copy.8.pos_ref, f32[1536,128]{1,0:T(8,128)} %get-tuple-element.19.cos_ref, f32[1536,128]{1,0:T(8,128)} %get-tuple-element.20.sin_ref, bf16[512,4096]{1,0:T(8,128)(2,1)} %q_ref.3, ...), custom_call_target="tpu_custom_call" | custom-call | tf_op jit(solution)/shard_map/pallas_call | solution.py:158
  (1 shorter events, 0.0 us)
Async XLA Ops:
  0.0 26.7 %copy-start = (bf16[512,2048]{1,0:T(8,128)(2,1)S(1)}, bf16[512,2048]{1,0:T(8,128)(2,1)}, u32[]{:S(2)}) copy-start(bf16[512,2048]{1,0:T(8,128)(2,1)} %refs_3_) | copy-start | bytes 6291460
  28.2 11.0 %collective-permute-start = (bf16[512,4096]{1,0:T(8,128)(2,1)}, bf16[512,4096]{1,0:T(8,128)(2,1)}, u32[]{:S(2)}, u32[]{:S(2)}) collective-permute-start(bf16[512,4096]{1,0:T(8,128)(2,1)} %constant_dynamic-update-slice_fusion), channel_id=1, source_target_pairs={{0,1},{1,2},{2,3},{3,4},{4,5},{5,6},{6,7},{7,8},{8,9},{9,10},{10,1... | collective-permute-start | bytes 12582920 | tf_op jit(solution)/shard_map/ppermute | solution.py:123
  39.1 87.6 %collective-permute-start.1 = (bf16[512,4096]{1,0:T(8,128)(2,1)}, bf16[512,4096]{1,0:T(8,128)(2,1)}, u32[]{:S(2)}, u32[]{:S(2)}) collective-permute-start(bf16[512,4096]{1,0:T(8,128)(2,1)} %constant_dynamic-update-slice_fusion), channel_id=1, source_target_pairs={{0,2},{2,4},{4,6},{6,8},{8,10},{10,12},{12,14},{16,18},{18,20},{20... | collective-permute-start | bytes 12582920 | tf_op jit(solution)/shard_map/ppermute | solution.py:135
  82.4 44.4 %collective-permute-start.2 = (bf16[512,4096]{1,0:T(8,128)(2,1)}, bf16[512,4096]{1,0:T(8,128)(2,1)}, u32[]{:S(2)}, u32[]{:S(2)}) collective-permute-start(bf16[512,4096]{1,0:T(8,128)(2,1)} %collective-permute-done.refs_0_.refs_2_), channel_id=1, source_target_pairs={{0,1},{2,3},{4,5},{6,7},{8,9},{10,11},{12,13},{14,15},{16,17},{18,... | collective-permute-start | bytes 12582920 | tf_op jit(solution)/shard_map/ppermute | solution.py:136

commit v14 on v12

--- a/solution.py
+++ b/solution.py
@@ -119,7 +119,8 @@
     count = lax.axis_size("seq")
     both = jnp.concatenate([keys, values], 1)
     near = lax.ppermute(both, "seq", [(s, s + 1) for s in range(count - 1)])
-    seg_all = lax.all_gather(segment_ids, "seq", tiled=True)
+    placed = jnp.zeros((count, rows), jnp.int32).at[shard].set(segment_ids)
+    seg_all = lax.psum(placed, "seq").reshape(count * rows)
     both, seg_all = lax.optimization_barrier((both, seg_all))
     far = lax.ppermute(both, "seq", [(s, s + 2) for s in range(0, count - 2, 2)])
     relay = lax.ppermute(near, "seq", [(s, s + 1) for s in range(0, count - 1, 2)])

time: 146 us -> 184 us (1.26)
  blocking collectives: 59.5 us -> 96.1 us
    psum x0 -> x1, blocking collectives: none -> 96.1 us  [local(): seg_all = lax.psum(placed, 'seq').reshape(count * rows)]
    all_gather x1 -> x0, blocking collectives: 59.5 us -> none  [local(): seg_all = lax.all_gather(segment_ids, 'seq', tiled=True)]
    another operation x2 -> x5, other arithmetic: 0.39 us -> 2.42 us
  transfers between devices with their start and end apart: 3 -> 3, of which waited for: 0 -> 0; matrix products, arithmetic and copies ran while one was open for 5% -> 5% of each run, Pallas kernels for 25% -> 20%
where the time goes in v14:
time: 184 us; the launch traced here: 183 us
  blocking collectives  96.1 us (52%)
  Pallas kernels  62.1 us (34%)
  starting transfers between devices  10.8 us (6%)
  other arithmetic  7.11 us (4%)
  local copies, waits for them, and re-layouts  6.59 us (4%)
    psum x1, blocking collectives, local(): seg_all = lax.psum(placed, 'seq').reshape(count * rows)  96.1 us
    pallas_call x2, Pallas kernels, local(): pl.pallas_call(functools.partial(attend_kernel, rows=rows, tile=tile, fir...  62.1 us
    ppermute x1, starting transfers between devices, local(): near = lax.ppermute(both, 'seq', [(s, s + 1) for s in range(count - 1)])  4.38 us
  transfers between devices with their start and end apart: 3, of which 0 were waited for; matrix products, arithmetic and copies ran while one was open for 5% of the time, Pallas kernels for 20%

profile of v14, /device:TPU:0, one launch (start us, length us, event | category | flops | bytes accessed | tf_op | source)
XLA Modules:
  0.0 182.8 jit_solution(9439619305331275495)
XLA Ops:
  0.0 0.0 copy-start.2
  0.0 0.0 copy-start
  0.0 0.0 copy-start.1
  0.0 3.3 %constant_dynamic-update-slice_fusion.1 = bf16[512,4096]{1,0:T(8,128)(2,1)} fusion(bf16[512,2048]{1,0:T(8,128)(2,1)} %refs_1_.1), kind=kLoop, calls=%fused_computation.15 | loop fusion | bytes 4194304
  3.3 0.0 copy-done
  3.3 1.5 constant_dynamic-update-slice_fusion
  4.8 4.4 %collective-permute-start.1 = (bf16[512,4096]{1,0:T(8,128)(2,1)}, bf16[512,4096]{1,0:T(8,128)(2,1)}, u32[]{:S(2)}, u32[]{:S(2)}) collective-permute-start(bf16[512,4096]{1,0:T(8,128)(2,1)} %constant_dynamic-update-slice_fusion), channel_id=1, source_target_pairs={{0,1},{1,2},{2,3},{3,4},{4,5},{5,6},{6,7},{7,8},{8,9},{9,10},{10,1... | collective-permute-start | bytes 12582920 | tf_op jit(solution)/shard_map/ppermute | solution.py:121
  9.1 0.0 copy-done.2
  9.2 0.7 and_reduce_fusion
  9.9 0.0 copy-done.1
  9.9 0.6 broadcast_select_fusion
  10.4 0.1 scatter.4
  10.5 96.1 %psum.7 = s32[8192]{0:T(1024)S(1)} all-reduce(s32[8192]{0:T(1024)S(1)} %bitcast.13), channel_id=1, replica_groups=mesh['grp'=2,'seq'=16] {'seq'}, use_global_device_ids=true, to_apply=%region_1.0 | all-reduce | flops 8192 | bytes 65536 | tf_op jit(solution)/shard_map/psum | solution.py:123
  106.6 3.2 %collective-permute-start = (bf16[512,4096]{1,0:T(8,128)(2,1)}, bf16[512,4096]{1,0:T(8,128)(2,1)}, u32[]{:S(2)}, u32[]{:S(2)}) collective-permute-start(bf16[512,4096]{1,0:T(8,128)(2,1)} %constant_dynamic-update-slice_fusion), channel_id=1, source_target_pairs={{0,2},{2,4},{4,6},{6,8},{8,10},{10,12},{12,14},{16,18},{18,20},{20... | collective-permute-start | bytes 12582920 | tf_op jit(solution)/shard_map/ppermute | solution.py:125
  109.8 0.0 collective-permute-done.1.refs_0_.refs_2_
  109.8 3.2 %collective-permute-start.2 = (bf16[512,4096]{1,0:T(8,128)(2,1)}, bf16[512,4096]{1,0:T(8,128)(2,1)}, u32[]{:S(2)}, u32[]{:S(2)}) collective-permute-start(bf16[512,4096]{1,0:T(8,128)(2,1)} %collective-permute-done.1.refs_0_.refs_2_), channel_id=1, source_target_pairs={{0,1},{2,3},{4,5},{6,7},{8,9},{10,11},{12,13},{14,15},{16,17},{18,... | collective-permute-start | bytes 12582920 | tf_op jit(solution)/shard_map/ppermute | solution.py:126
  113.1 0.6 slice.30
  113.6 0.8 select_bitcast_fusion
  114.4 0.3 reduce-window.9
  114.7 0.1 slice.35
  114.8 0.1 reduce-window.12
  114.9 0.1 slice_reduce_fusion
  115.0 0.1 bitcast_subtract_fusion
  115.1 0.1 pad_dynamic-slice_fusion
  115.2 0.9 copy.6.pos_ref
  116.1 0.1 fusion.2
  116.1 2.8 %fusion = (f32[1536,64]{1,0:T(8,128)S(1)}, f32[1536,64]{1,0:T(8,128)S(1)}, f32[1536,64]{1,0:T(8,128)S(1)}) fusion(f32[64]{0:T(128)S(1)} %multiply_power_fusion, f32[1536]{0:T(1024)S(1)} %fusion.2), kind=kLoop, calls=%fused_computation.4 | loop fusion | flops 196608 | bytes 1186048 | tf_op jit(solution)/shard_map/neg | solution.py:31
  119.0 1.7 pad_maximum_fusion
  120.7 36.6 %shard_map.46 = (f32[16,512,128]{2,1,0:T(8,128)}, f32[512,4096]{1,0:T(8,128)}) custom-call(s32[1]{0:T(128)} %bitcast.par_ref, s32[512,1]{1,0:T(8,128)} %copy.6.pos_ref, f32[1536,128]{1,0:T(8,128)} %get-tuple-element.28.cos_ref, f32[1536,128]{1,0:T(8,128)} %get-tuple-element.29.sin_ref, bf16[512,4096]{1,0:T(8,128)(2,1)} %q_ref.3, ...), custom_call_target="tpu_custom_call" | custom-call | tf_op jit(solution)/shard_map/pallas_call | solution.py:147
  157.3 0.0 collective-permute-done.refs_0_.refs_2_
  157.3 0.0 collective-permute-done.2.refs_1_.refs_3_
  157.3 25.5 %shard_map.47 = bf16[512,4096]{1,0:T(8,128)(2,1)} custom-call(s32[1]{0:T(128)} %bitcast.par_ref, s32[512,1]{1,0:T(8,128)} %copy.6.pos_ref, f32[1536,128]{1,0:T(8,128)} %get-tuple-element.28.cos_ref, f32[1536,128]{1,0:T(8,128)} %get-tuple-element.29.sin_ref, bf16[512,4096]{1,0:T(8,128)(2,1)} %q_ref.3, bf16[512,4096]{1,0:T(8,128)(2,1)} %collective-permute-done.refs_0_.refs_2_, ...), custom_call_target="tpu_custom_call" | custom-call | tf_op jit(solution)/shard_map/pallas_call | solution.py:158
  (3 shorter events, 0.0 us)
Async XLA Ops:
  0.0 9.2 %copy-start.2 = (s32[2]{0:T(128)S(1)}, s32[2]{0:T(128)}, u32[]{:S(2)}) copy-start(s32[2]{0:T(128)} %constant.52.clone.1) | copy-start | bytes 28
  0.0 3.3 %copy-start = (bf16[512,2048]{1,0:T(8,128)(2,1)S(1)}, bf16[512,2048]{1,0:T(8,128)(2,1)}, u32[]{:S(2)}) copy-start(bf16[512,2048]{1,0:T(8,128)(2,1)} %refs_3_.1) | copy-start | bytes 6291460
  0.0 9.8 %copy-start.1 = (s32[512]{0:T(512)S(1)}, s32[512]{0:T(512)}, u32[]{:S(2)}) copy-start(s32[512]{0:T(512)} %param.9) | copy-start | bytes 6148
  4.8 105.1 %collective-permute-start.1 = (bf16[512,4096]{1,0:T(8,128)(2,1)}, bf16[512,4096]{1,0:T(8,128)(2,1)}, u32[]{:S(2)}, u32[]{:S(2)}) collective-permute-start(bf16[512,4096]{1,0:T(8,128)(2,1)} %constant_dynamic-update-slice_fusion), channel_id=1, source_target_pairs={{0,1},{1,2},{2,3},{3,4},{4,5},{5,6},{6,7},{7,8},{8,9},{9,10},{10,1... | collective-permute-start | bytes 12582920 | tf_op jit(solution)/shard_map/ppermute | solution.py:121
  106.6 50.7 %collective-permute-start = (bf16[512,4096]{1,0:T(8,128)(2,1)}, bf16[512,4096]{1,0:T(8,128)(2,1)}, u32[]{:S(2)}, u32[]{:S(2)}) collective-permute-start(bf16[512,4096]{1,0:T(8,128)(2,1)} %constant_dynamic-update-slice_fusion), channel_id=1, source_target_pairs={{0,2},{2,4},{4,6},{6,8},{8,10},{10,12},{12,14},{16,18},{18,20},{20... | collective-permute-start | bytes 12582920 | tf_op jit(solution)/shard_map/ppermute | solution.py:125
  109.8 47.4 %collective-permute-start.2 = (bf16[512,4096]{1,0:T(8,128)(2,1)}, bf16[512,4096]{1,0:T(8,128)(2,1)}, u32[]{:S(2)}, u32[]{:S(2)}) collective-permute-start(bf16[512,4096]{1,0:T(8,128)(2,1)} %collective-permute-done.1.refs_0_.refs_2_), channel_id=1, source_target_pairs={{0,1},{2,3},{4,5},{6,7},{8,9},{10,11},{12,13},{14,15},{16,17},{18,... | collective-permute-start | bytes 12582920 | tf_op jit(solution)/shard_map/ppermute | solution.py:126

commit v15 on v12

--- a/solution.py
+++ b/solution.py
@@ -120,9 +120,8 @@
     both = jnp.concatenate([keys, values], 1)
     near = lax.ppermute(both, "seq", [(s, s + 1) for s in range(count - 1)])
     seg_all = lax.all_gather(segment_ids, "seq", tiled=True)
-    both, seg_all = lax.optimization_barrier((both, seg_all))
-    far = lax.ppermute(both, "seq", [(s, s + 2) for s in range(0, count - 2, 2)])
-    relay = lax.ppermute(near, "seq", [(s, s + 1) for s in range(0, count - 1, 2)])
+    near, seg_all = lax.optimization_barrier((near, seg_all))
+    far = lax.ppermute(near, "seq", [(s, s + 1) for s in range(count - 1)])
     total = seg_all.shape[0]
     places = jnp.arange(total, dtype=jnp.int32)
     previous = jnp.concatenate([seg_all[:1], seg_all[:-1]])
@@ -163,7 +162,7 @@
             scratch_shapes=[pltpu.VMEM((rows // tile, tile, rows), f32)]),
         out_shape=jax.ShapeDtypeStruct(queries.shape, jnp.bfloat16),
         compiler_params=params,
-    )(parity, pos_q, cos, sin, queries, far, relay, far, relay, stats, acc1)
+    )(parity, pos_q, cos, sin, queries, far, far, far, far, stats, acc1)
 
 
 def solution(mesh):

time: 146 us -> 141 us (0.966)
  local copies, waits for them, and re-layouts: 6.5 us -> 1.66 us
  other arithmetic: 5.85 us -> 8.46 us
  starting transfers between devices: 11 us -> 8.41 us
    unnamed x5 -> x2, local copies, waits for them, and re-layouts: 3.31 us -> 0.01 us
    concatenate x0 -> x1, other arithmetic: none -> 2.72 us  [local(): both = jnp.concatenate([keys, values], 1)]
    ppermute x2 -> x1, starting transfers between devices: 6.63 us -> 4.03 us  [local(): far = lax.ppermute(near, 'seq', [(s, s + 1) for s in range(count - 1)])]
  transfers between devices with their start and end apart: 3 -> 2, of which waited for: 0 -> 0; matrix products, arithmetic and copies ran while one was open for 5% -> 5% of each run, Pallas kernels for 25% -> 26%
where the time goes in v15:
time: 141 us; the launch traced here: 140 us
  Pallas kernels  62.1 us (44%)
  blocking collectives  59.3 us (42%)
  other arithmetic  8.46 us (6%)
  starting transfers between devices  8.41 us (6%)
  local copies, waits for them, and re-layouts  1.66 us (1%)
    pallas_call x2, Pallas kernels, local(): pl.pallas_call(functools.partial(attend_kernel, rows=rows, tile=tile, fir...  62.1 us
    all_gather x1, blocking collectives, local(): seg_all = lax.all_gather(segment_ids, 'seq', tiled=True)  59.3 us
    ppermute x1, starting transfers between devices, local(): near = lax.ppermute(both, 'seq', [(s, s + 1) for s in range(count - 1)])  4.38 us
    ppermute x1, starting transfers between devices, local(): far = lax.ppermute(near, 'seq', [(s, s + 1) for s in range(count - 1)])  4.03 us
  transfers between devices with their start and end apart: 2, of which 0 were waited for; matrix products, arithmetic and copies ran while one was open for 5% of the time, Pallas kernels for 26%

profile of v15, /device:TPU:0, one launch (start us, length us, event | category | flops | bytes accessed | tf_op | source)
XLA Modules:
  0.0 140.0 jit_solution(16408675506635612907)
XLA Ops:
  0.0 0.0 copy-start
  0.0 2.7 %pad_maximum_fusion = bf16[512,4096]{1,0:T(8,128)(2,1)S(1)} fusion(bf16[512,2048]{1,0:T(8,128)(2,1)} %refs_3_.1, bf16[512,2048]{1,0:T(8,128)(2,1)} %refs_1_.1), kind=kLoop, calls=%fused_computation | loop fusion | flops 8388608 | bytes 8388608 | tf_op jit(solution)/shard_map/concatenate | solution.py:120
  2.7 4.4 %collective-permute-start = (bf16[512,4096]{1,0:T(8,128)(2,1)S(1)}, bf16[512,4096]{1,0:T(8,128)(2,1)}, u32[]{:S(2)}, u32[]{:S(2)}) collective-permute-start(bf16[512,4096]{1,0:T(8,128)(2,1)S(1)} %pad_maximum_fusion), channel_id=1, source_target_pairs={{0,1},{1,2},{2,3},{3,4},{4,5},{5,6},{6,7},{7,8},{8,9},{9,10},{10,1... | collective-permute-start | bytes 12582920 | tf_op jit(solution)/shard_map/ppermute | solution.py:121
  7.1 0.0 copy-done
  7.1 59.3 %all-gather = s32[16,1,512]{2,1,0:T(1,128)S(1)} all-gather(s32[1,1,512]{2,1,0:T(1,128)S(1)} %bitcast.13), channel_id=1, replica_groups=mesh['grp'=2,'seq'=16] {'seq'}, dimensions={0}, use_global_device_ids=true | all-gather | bytes 34816 | tf_op jit(solution)/shard_map/all_gather | solution.py:122
  66.4 0.0 collective-permute-done.refs_0_.refs_2_
  66.4 4.0 %collective-permute-start.1 = (bf16[512,4096]{1,0:T(8,128)(2,1)}, bf16[512,4096]{1,0:T(8,128)(2,1)}, u32[]{:S(2)}, u32[]{:S(2)}) collective-permute-start(bf16[512,4096]{1,0:T(8,128)(2,1)} %collective-permute-done.refs_0_.refs_2_), channel_id=1, source_target_pairs={{0,1},{1,2},{2,3},{3,4},{4,5},{5,6},{6,7},{7,8},{8,9},{9,10},{10,1... | collective-permute-start | bytes 12582920 | tf_op jit(solution)/shard_map/ppermute | solution.py:124
  70.5 0.5 slice.16
  71.0 0.7 select_bitcast_fusion
  71.7 0.3 reduce-window.9
  72.0 0.1 slice.21
  72.1 0.1 reduce-window.12
  72.2 0.1 slice_reduce_fusion
  72.3 0.1 bitcast_subtract_fusion
  72.4 0.1 pad_dynamic-slice_fusion
  72.5 0.9 copy.8.pos_ref
  73.3 0.1 fusion.2
  73.4 2.8 %fusion = (f32[1536,64]{1,0:T(8,128)S(1)}, f32[1536,64]{1,0:T(8,128)S(1)}, f32[1536,64]{1,0:T(8,128)S(1)}) fusion(f32[64]{0:T(128)S(1)} %multiply_power_fusion, f32[1536]{0:T(1024)S(1)} %fusion.2), kind=kLoop, calls=%fused_computation.5 | loop fusion | flops 196608 | bytes 1186048 | tf_op jit(solution)/shard_map/neg | solution.py:31
  76.2 1.7 %pad_maximum_fusion.1 = (f32[1536,128]{1,0:T(8,128)}, f32[1536,128]{1,0:T(8,128)}) fusion(f32[1536,64]{1,0:T(8,128)S(1)} %get-tuple-element.15, f32[1536,64]{1,0:T(8,128)S(1)} %get-tuple-element.14, f32[1536,64]{1,0:T(8,128)S(1)} %get-tuple-element.13), kind=kLoop, calls=%fused_computation.3 | loop fusion | flops 393216 | bytes 2752512 | tf_op jit(solution)/shard_map/concatenate | solution.py:31
  77.9 36.6 %shard_map.46 = (f32[16,512,128]{2,1,0:T(8,128)}, f32[512,4096]{1,0:T(8,128)}) custom-call(s32[1]{0:T(128)} %bitcast.par_ref, s32[512,1]{1,0:T(8,128)} %copy.8.pos_ref, f32[1536,128]{1,0:T(8,128)} %get-tuple-element.16.cos_ref, f32[1536,128]{1,0:T(8,128)} %get-tuple-element.17.sin_ref, bf16[512,4096]{1,0:T(8,128)(2,1)} %q_ref.3, ...), custom_call_target="tpu_custom_call" | custom-call | tf_op jit(solution)/shard_map/pallas_call | solution.py:145
  114.4 0.0 collective-permute-done.1.refs_0_.refs_1_.refs_2_.refs_3_
  114.4 25.5 %shard_map.47 = bf16[512,4096]{1,0:T(8,128)(2,1)} custom-call(s32[1]{0:T(128)} %bitcast.par_ref, s32[512,1]{1,0:T(8,128)} %copy.8.pos_ref, f32[1536,128]{1,0:T(8,128)} %get-tuple-element.16.cos_ref, f32[1536,128]{1,0:T(8,128)} %get-tuple-element.17.sin_ref, bf16[512,4096]{1,0:T(8,128)(2,1)} %q_ref.3, ...), custom_call_target="tpu_custom_call" | custom-call | tf_op jit(solution)/shard_map/pallas_call | solution.py:156
  (1 shorter events, 0.0 us)
Async XLA Ops:
  0.0 7.1 %copy-start = (s32[512]{0:T(512)S(1)}, s32[512]{0:T(512)}, u32[]{:S(2)}) copy-start(s32[512]{0:T(512)} %param.7) | copy-start | bytes 6148
  2.7 63.7 %collective-permute-start = (bf16[512,4096]{1,0:T(8,128)(2,1)S(1)}, bf16[512,4096]{1,0:T(8,128)(2,1)}, u32[]{:S(2)}, u32[]{:S(2)}) collective-permute-start(bf16[512,4096]{1,0:T(8,128)(2,1)S(1)} %pad_maximum_fusion), channel_id=1, source_target_pairs={{0,1},{1,2},{2,3},{3,4},{4,5},{5,6},{6,7},{7,8},{8,9},{9,10},{10,1... | collective-permute-start | bytes 12582920 | tf_op jit(solution)/shard_map/ppermute | solution.py:121
  66.4 48.0 %collective-permute-start.1 = (bf16[512,4096]{1,0:T(8,128)(2,1)}, bf16[512,4096]{1,0:T(8,128)(2,1)}, u32[]{:S(2)}, u32[]{:S(2)}) collective-permute-start(bf16[512,4096]{1,0:T(8,128)(2,1)} %collective-permute-done.refs_0_.refs_2_), channel_id=1, source_target_pairs={{0,1},{1,2},{2,3},{3,4},{4,5},{5,6},{6,7},{7,8},{8,9},{9,10},{10,1... | collective-permute-start | bytes 12582920 | tf_op jit(solution)/shard_map/ppermute | solution.py:124

commit v16 on v15

--- a/solution.py
+++ b/solution.py
@@ -117,11 +117,13 @@
     span = (hops + 1) * rows
     shard = lax.axis_index("seq")
     count = lax.axis_size("seq")
-    both = jnp.concatenate([keys, values], 1)
-    near = lax.ppermute(both, "seq", [(s, s + 1) for s in range(count - 1)])
+    pairs = [(s, s + 1) for s in range(count - 1)]
+    near_k = lax.ppermute(keys, "seq", pairs)
     seg_all = lax.all_gather(segment_ids, "seq", tiled=True)
-    near, seg_all = lax.optimization_barrier((near, seg_all))
-    far = lax.ppermute(near, "seq", [(s, s + 1) for s in range(count - 1)])
+    values_b, seg_all = lax.optimization_barrier((values, seg_all))
+    near_v = lax.ppermute(values_b, "seq", pairs)
+    near = jnp.concatenate([near_k, near_v], 1)
+    far = lax.ppermute(near, "seq", pairs)
     total = seg_all.shape[0]
     places = jnp.arange(total, dtype=jnp.int32)
     previous = jnp.concatenate([seg_all[:1], seg_all[:-1]])

time: 141 us -> 144 us (1.021)
  blocking collectives: 59.3 us -> 38.8 us
  starting transfers between devices: 8.41 us -> 27.9 us
  local copies, waits for them, and re-layouts: 1.66 us -> 4.64 us
  other arithmetic: 8.46 us -> 5.77 us
  waiting for transfers between devices: 0.01 us -> 2.38 us
    all_gather x1, blocking collectives: 59.3 us -> 38.8 us  [local(): seg_all = lax.all_gather(segment_ids, 'seq', tiled=True)]
    ppermute x2 -> x3, starting transfers between devices: 8.41 us -> 27.9 us  [the longest x1 23.2 us: local(): far = lax.ppermute(near, 'seq', pairs)]
    concatenate x1 -> x0, other arithmetic: 2.72 us -> none  [local(): both = jnp.concatenate([keys, values], 1)]
    ppermute x2 -> x3, waiting for transfers between devices: 0.01 us -> 2.38 us  [the longest x1 2.38 us: local(): near_v = lax.ppermute(values_b, 'seq', pairs)]
    concatenate x0 -> x1, local copies, waits for them, and re-layouts: none -> 1.45 us  [local(): near = jnp.concatenate([near_k, near_v], 1)]
    unnamed x2 -> x1, local copies, waits for them, and re-layouts: 0.01 us -> 1.46 us
  transfers between devices with their start and end apart: 2 -> 3, of which waited for: 0 -> 1; matrix products, arithmetic and copies ran while one was open for 5% -> 6% of each run, Pallas kernels for 26% -> 26%
where the time goes in v16:
time: 144 us; the launch traced here: 142 us
  Pallas kernels  62.1 us (43%)
  blocking collectives  38.8 us (27%)
  starting transfers between devices  27.9 us (19%)
  other arithmetic  5.77 us (4%)
  local copies, waits for them, and re-layouts  4.64 us (3%)
  waiting for transfers between devices  2.38 us (2%)
    pallas_call x2, Pallas kernels, local(): pl.pallas_call(functools.partial(attend_kernel, rows=rows, tile=tile, fir...  62.1 us
    all_gather x1, blocking collectives, local(): seg_all = lax.all_gather(segment_ids, 'seq', tiled=True)  38.8 us
    ppermute x1, starting transfers between devices, local(): far = lax.ppermute(near, 'seq', pairs)  23.2 us
  transfers between devices with their start and end apart: 3, of which 1 were waited for; matrix products, arithmetic and copies ran while one was open for 6% of the time, Pallas kernels for 26%

profile of v16, /device:TPU:0, one launch (start us, length us, event | category | flops | bytes accessed | tf_op | source)
XLA Modules:
  0.0 141.6 jit_solution(9772028086534271129)
XLA Ops:
  0.0 2.5 %collective-permute-start = (bf16[512,2048]{1,0:T(8,128)(2,1)}, bf16[512,2048]{1,0:T(8,128)(2,1)S(1)}, u32[]{:S(2)}, u32[]{:S(2)}) collective-permute-start(bf16[512,2048]{1,0:T(8,128)(2,1)} %refs_1_.1), channel_id=1, source_target_pairs={{0,1},{1,2},{2,3},{3,4},{4,5},{5,6},{6,7},{7,8},{8,9},{9,10},{10,1... | collective-permute-start | bytes 6291464 | tf_op jit(solution)/shard_map/ppermute | solution.py:121
  2.5 38.8 %all-gather = s32[16,1,512]{2,1,0:T(1,128)S(1)} all-gather(s32[1,1,512]{2,1,0:T(1,128)} %bitcast.13), channel_id=1, replica_groups=mesh['grp'=2,'seq'=16] {'seq'}, dimensions={0}, use_global_device_ids=true | all-gather | bytes 34816 | tf_op jit(solution)/shard_map/all_gather | solution.py:122
  41.3 2.2 %collective-permute-start.1 = (bf16[512,2048]{1,0:T(8,128)(2,1)}, bf16[512,2048]{1,0:T(8,128)(2,1)S(1)}, u32[]{:S(2)}, u32[]{:S(2)}) collective-permute-start(bf16[512,2048]{1,0:T(8,128)(2,1)} %refs_3_.1), channel_id=1, source_target_pairs={{0,1},{1,2},{2,3},{3,4},{4,5},{5,6},{6,7},{7,8},{8,9},{9,10},{10,1... | collective-permute-start | bytes 6291464 | tf_op jit(solution)/shard_map/ppermute | solution.py:124
  43.5 0.0 collective-permute-done
  43.5 1.5 %constant_dynamic-update-slice_fusion.1 = bf16[512,4096]{1,0:T(8,128)(2,1)} fusion(bf16[512,2048]{1,0:T(8,128)(2,1)S(1)} %collective-permute-done), kind=kLoop, calls=%fused_computation.15 | loop fusion | bytes 4194304
  45.0 2.4 %collective-permute-done.1 = bf16[512,2048]{1,0:T(8,128)(2,1)S(1)} collective-permute-done((bf16[512,2048]{1,0:T(8,128)(2,1)}, bf16[512,2048]{1,0:T(8,128)(2,1)S(1)}, u32[]{:S(2)}, u32[]{:S(2)}) %collective-permute-start.1) | collective-permute-done | bytes 2097184 | tf_op jit(solution)/shard_map/ppermute | solution.py:124
  47.4 1.5 %constant_dynamic-update-slice_fusion.refs_0_.refs_2_ = bf16[512,4096]{1,0:T(8,128)(2,1)} fusion(bf16[512,4096]{1,0:T(8,128)(2,1)} %constant_dynamic-update-slice_fusion.1, bf16[512,2048]{1,0:T(8,128)(2,1)S(1)} %collective-permute-done.1), kind=kLoop, calls=%fused_computation.14 | loop fusion | bytes 4194304 | tf_op jit(solution)/shard_map/concatenate | solution.py:125
  48.8 23.2 %collective-permute-start.2 = (bf16[512,4096]{1,0:T(8,128)(2,1)}, bf16[512,4096]{1,0:T(8,128)(2,1)}, u32[]{:S(2)}, u32[]{:S(2)}) collective-permute-start(bf16[512,4096]{1,0:T(8,128)(2,1)} %constant_dynamic-update-slice_fusion.refs_0_.refs_2_), channel_id=1, source_target_pairs={{0,1},{1,2},{2,3},{3,4},{4,5},{5,6},{6,7},{7,8},{8,9},{9,10},{10,1... | collective-permute-start | bytes 12582920 | tf_op jit(solution)/shard_map/ppermute | solution.py:126
  72.0 0.6 slice.16
  72.6 0.8 select_bitcast_fusion
  73.4 0.3 reduce-window.9
  73.7 0.1 slice.21
  73.7 0.1 reduce-window.12
  73.8 0.1 slice_reduce_fusion
  74.0 0.1 bitcast_subtract_fusion
  74.0 0.1 pad_dynamic-slice_fusion
  74.1 0.9 copy.8.pos_ref
  75.0 0.1 fusion.2
  75.1 2.8 %fusion = (f32[1536,64]{1,0:T(8,128)S(1)}, f32[1536,64]{1,0:T(8,128)S(1)}, f32[1536,64]{1,0:T(8,128)S(1)}) fusion(f32[64]{0:T(128)S(1)} %multiply_power_fusion, f32[1536]{0:T(1024)S(1)} %fusion.2), kind=kLoop, calls=%fused_computation.4 | loop fusion | flops 196608 | bytes 1186048 | tf_op jit(solution)/shard_map/neg | solution.py:31
  77.9 1.6 %pad_maximum_fusion = (f32[1536,128]{1,0:T(8,128)}, f32[1536,128]{1,0:T(8,128)}) fusion(f32[1536,64]{1,0:T(8,128)S(1)} %get-tuple-element.15, f32[1536,64]{1,0:T(8,128)S(1)} %get-tuple-element.14, f32[1536,64]{1,0:T(8,128)S(1)} %get-tuple-element.13), kind=kLoop, calls=%fused_computation.2 | loop fusion | flops 393216 | bytes 2752512 | tf_op jit(solution)/shard_map/concatenate | solution.py:31
  79.5 36.6 %shard_map.46 = (f32[16,512,128]{2,1,0:T(8,128)}, f32[512,4096]{1,0:T(8,128)}) custom-call(s32[1]{0:T(128)} %bitcast.par_ref, s32[512,1]{1,0:T(8,128)} %copy.8.pos_ref, f32[1536,128]{1,0:T(8,128)} %get-tuple-element.16.cos_ref, f32[1536,128]{1,0:T(8,128)} %get-tuple-element.17.sin_ref, bf16[512,4096]{1,0:T(8,128)(2,1)} %q_ref.3, ...), custom_call_target="tpu_custom_call" | custom-call | tf_op jit(solution)/shard_map/pallas_call | solution.py:147
  116.1 0.0 collective-permute-done.2.refs_0_.refs_1_.refs_2_.refs_3_
  116.1 25.5 %shard_map.47 = bf16[512,4096]{1,0:T(8,128)(2,1)} custom-call(s32[1]{0:T(128)} %bitcast.par_ref, s32[512,1]{1,0:T(8,128)} %copy.8.pos_ref, f32[1536,128]{1,0:T(8,128)} %get-tuple-element.16.cos_ref, f32[1536,128]{1,0:T(8,128)} %get-tuple-element.17.sin_ref, bf16[512,4096]{1,0:T(8,128)(2,1)} %q_ref.3, ...), custom_call_target="tpu_custom_call" | custom-call | tf_op jit(solution)/shard_map/pallas_call | solution.py:158
  (1 shorter events, 0.0 us)
Async XLA Ops:
  0.0 43.5 %collective-permute-start = (bf16[512,2048]{1,0:T(8,128)(2,1)}, bf16[512,2048]{1,0:T(8,128)(2,1)S(1)}, u32[]{:S(2)}, u32[]{:S(2)}) collective-permute-start(bf16[512,2048]{1,0:T(8,128)(2,1)} %refs_1_.1), channel_id=1, source_target_pairs={{0,1},{1,2},{2,3},{3,4},{4,5},{5,6},{6,7},{7,8},{8,9},{9,10},{10,1... | collective-permute-start | bytes 6291464 | tf_op jit(solution)/shard_map/ppermute | solution.py:121
  41.3 6.0 %collective-permute-start.1 = (bf16[512,2048]{1,0:T(8,128)(2,1)}, bf16[512,2048]{1,0:T(8,128)(2,1)S(1)}, u32[]{:S(2)}, u32[]{:S(2)}) collective-permute-start(bf16[512,2048]{1,0:T(8,128)(2,1)} %refs_3_.1), channel_id=1, source_target_pairs={{0,1},{1,2},{2,3},{3,4},{4,5},{5,6},{6,7},{7,8},{8,9},{9,10},{10,1... | collective-permute-start | bytes 6291464 | tf_op jit(solution)/shard_map/ppermute | solution.py:124
  48.8 67.3 %collective-permute-start.2 = (bf16[512,4096]{1,0:T(8,128)(2,1)}, bf16[512,4096]{1,0:T(8,128)(2,1)}, u32[]{:S(2)}, u32[]{:S(2)}) collective-permute-start(bf16[512,4096]{1,0:T(8,128)(2,1)} %constant_dynamic-update-slice_fusion.refs_0_.refs_2_), channel_id=1, source_target_pairs={{0,1},{1,2},{2,3},{3,4},{4,5},{5,6},{6,7},{7,8},{8,9},{9,10},{10,1... | collective-permute-start | bytes 12582920 | tf_op jit(solution)/shard_map/ppermute | solution.py:126

commit v17 on v16

--- a/solution.py
+++ b/solution.py
@@ -7,20 +7,13 @@
 from jax.experimental.pallas import tpu as pltpu
 from jax.sharding import PartitionSpec as P
 
-H = 32
-KVH = 16
+
 HD = 128
 W = 1024
 
 
 query_scale = 168.0 ** (-0.5)
 exp2_scale = query_scale * 1.4426950408889634
-
-
-def passed_along(value, axis, steps):
-    count = lax.axis_size(axis)
-    first, last = (max(0, -steps), min(count, count - steps))
-    return lax.ppermute(value, axis, [(source, source + steps) for source in range(first, last)])
 
 
 def rope_tables(doc_pos):
@@ -123,7 +116,6 @@
     values_b, seg_all = lax.optimization_barrier((values, seg_all))
     near_v = lax.ppermute(values_b, "seq", pairs)
     near = jnp.concatenate([near_k, near_v], 1)
-    far = lax.ppermute(near, "seq", pairs)
     total = seg_all.shape[0]
     places = jnp.arange(total, dtype=jnp.int32)
     previous = jnp.concatenate([seg_all[:1], seg_all[:-1]])
@@ -134,6 +126,8 @@
     cos, sin = rope_tables(pos_win)
     pos_q = pos_win[span - rows:].reshape(rows, 1)
     parity = (shard % 2).astype(jnp.int32).reshape(1)
+    near, cos, sin, pos_q = lax.optimization_barrier((near, cos, sin, pos_q))
+    far = lax.ppermute(near, "seq", pairs)
     tile = 256
     heads = keys.shape[1] // HD
     kv_spec = pl.BlockSpec((rows, HD), lambda h, p: (0, h))

time: 144 us -> 151 us (1.049)
  the two profiles are of different devices: /device:TPU:0 before, /device:TPU:8 now
where the time goes in v17:
time: 151 us
  Pallas kernels  62.1 us (41%)
  waiting for transfers between devices  52 us (34%)
  blocking collectives  19.1 us (13%)
  other arithmetic  9.71 us (6%)
  starting transfers between devices  6.08 us (4%)
  local copies, waits for them, and re-layouts  1.65 us (1%)
    pallas_call x2, Pallas kernels, local(): pl.pallas_call(functools.partial(attend_kernel, rows=rows, tile=tile, fir...  62.1 us
    ppermute x1, waiting for transfers between devices, local(): near_k = lax.ppermute(keys, 'seq', pairs)  22.6 us
    all_gather x1, blocking collectives, local(): seg_all = lax.all_gather(segment_ids, 'seq', tiled=True)  19.1 us
    ppermute x1, waiting for transfers between devices, local(): near_v = lax.ppermute(values_b, 'seq', pairs)  17.7 us
    ppermute x1, waiting for transfers between devices, local(): far = lax.ppermute(near, 'seq', pairs)  11.7 us
    concatenate x1, other arithmetic, local(): near = jnp.concatenate([near_k, near_v], 1)  3.99 us
  transfers between devices with their start and end apart: 3, of which 3 were waited for; matrix products, arithmetic and copies ran while one was open for 5% of the time, Pallas kernels for 24%

profile of v17, /device:TPU:8, one launch (start us, length us, event | category | flops | bytes accessed | tf_op | source)
XLA Modules:
  0.0 150.7 jit_solution(12732974468838897816)
XLA Ops:
  0.0 19.1 %all-gather = s32[16,1,512]{2,1,0:T(1,128)S(1)} all-gather(s32[1,1,512]{2,1,0:T(1,128)} %bitcast.13), channel_id=1, replica_groups=mesh['grp'=2,'seq'=16] {'seq'}, dimensions={0}, use_global_device_ids=true | all-gather | bytes 34816 | tf_op jit(solution)/shard_map/all_gather | solution.py:115
  19.1 2.2 %collective-permute-start.1 = (bf16[512,2048]{1,0:T(8,128)(2,1)}, bf16[512,2048]{1,0:T(8,128)(2,1)S(1)}, u32[]{:S(2)}, u32[]{:S(2)}) collective-permute-start(bf16[512,2048]{1,0:T(8,128)(2,1)} %refs_3_.1), channel_id=1, source_target_pairs={{0,1},{1,2},{2,3},{3,4},{4,5},{5,6},{6,7},{7,8},{8,9},{9,10},{10,1... | collective-permute-start | bytes 6291464 | tf_op jit(solution)/shard_map/ppermute | solution.py:117
  21.4 1.9 %collective-permute-start = (bf16[512,2048]{1,0:T(8,128)(2,1)}, bf16[512,2048]{1,0:T(8,128)(2,1)}, u32[]{:S(2)}, u32[]{:S(2)}) collective-permute-start(bf16[512,2048]{1,0:T(8,128)(2,1)} %refs_1_.1), channel_id=1, source_target_pairs={{0,1},{1,2},{2,3},{3,4},{4,5},{5,6},{6,7},{7,8},{8,9},{9,10},{10,1... | collective-permute-start | bytes 6291464 | tf_op jit(solution)/shard_map/ppermute | solution.py:114
  23.3 0.5 slice.16
  23.8 0.7 select_bitcast_fusion
  24.6 0.3 reduce-window.9
  24.9 0.1 slice.21
  24.9 0.1 reduce-window.12
  25.1 0.1 slice_reduce_fusion
  25.2 0.1 bitcast_subtract_fusion
  25.2 0.1 pad_dynamic-slice_fusion
  25.3 0.1 fusion.2
  25.4 2.8 %fusion = (f32[1536,64]{1,0:T(8,128)S(1)}, f32[1536,64]{1,0:T(8,128)S(1)}, f32[1536,64]{1,0:T(8,128)S(1)}) fusion(f32[64]{0:T(128)S(1)} %multiply_power_fusion, f32[1536]{0:T(1024)S(1)} %fusion.2), kind=kLoop, calls=%fused_computation.5 | loop fusion | flops 196608 | bytes 1186048 | tf_op jit(solution)/shard_map/neg | solution.py:24
  28.2 1.6 %pad_maximum_fusion.1 = (f32[1536,128]{1,0:T(8,128)}, f32[1536,128]{1,0:T(8,128)}) fusion(f32[1536,64]{1,0:T(8,128)S(1)} %get-tuple-element.23, f32[1536,64]{1,0:T(8,128)S(1)} %get-tuple-element.22, f32[1536,64]{1,0:T(8,128)S(1)} %get-tuple-element.21), kind=kLoop, calls=%fused_computation.3 | loop fusion | flops 393216 | bytes 2752512 | tf_op jit(solution)/shard_map/concatenate | solution.py:24
  29.9 17.7 %collective-permute-done.1 = bf16[512,2048]{1,0:T(8,128)(2,1)S(1)} collective-permute-done((bf16[512,2048]{1,0:T(8,128)(2,1)}, bf16[512,2048]{1,0:T(8,128)(2,1)S(1)}, u32[]{:S(2)}, u32[]{:S(2)}) %collective-permute-start.1) | collective-permute-done | bytes 2097184 | tf_op jit(solution)/shard_map/ppermute | solution.py:117
  47.6 22.6 %collective-permute-done = bf16[512,2048]{1,0:T(8,128)(2,1)} collective-permute-done((bf16[512,2048]{1,0:T(8,128)(2,1)}, bf16[512,2048]{1,0:T(8,128)(2,1)}, u32[]{:S(2)}, u32[]{:S(2)}) %collective-permute-start) | collective-permute-done | bytes 2097184 | tf_op jit(solution)/shard_map/ppermute | solution.py:114
  70.2 4.0 %pad_maximum_fusion.refs_0_.refs_2_ = bf16[512,4096]{1,0:T(8,128)(2,1)} fusion(bf16[512,2048]{1,0:T(8,128)(2,1)S(1)} %collective-permute-done.1, bf16[512,2048]{1,0:T(8,128)(2,1)} %collective-permute-done), kind=kLoop, calls=%fused_computation | loop fusion | flops 8388608 | bytes 8388608 | tf_op jit(solution)/shard_map/concatenate | solution.py:118
  74.2 1.9 %collective-permute-start.2 = (bf16[512,4096]{1,0:T(8,128)(2,1)}, bf16[512,4096]{1,0:T(8,128)(2,1)}, u32[]{:S(2)}, u32[]{:S(2)}) collective-permute-start(bf16[512,4096]{1,0:T(8,128)(2,1)} %pad_maximum_fusion.refs_0_.refs_2_), channel_id=1, source_target_pairs={{0,1},{1,2},{2,3},{3,4},{4,5},{5,6},{6,7},{7,8},{8,9},{9,10},{10,1... | collective-permute-start | bytes 12582920 | tf_op jit(solution)/shard_map/ppermute | solution.py:130
  76.1 0.9 copy.8.pos_ref
  77.0 36.6 %shard_map.46 = (f32[16,512,128]{2,1,0:T(8,128)}, f32[512,4096]{1,0:T(8,128)}) custom-call(s32[1]{0:T(128)} %bitcast.par_ref, s32[512,1]{1,0:T(8,128)} %copy.8.pos_ref, f32[1536,128]{1,0:T(8,128)} %get-tuple-element.16.cos_ref, f32[1536,128]{1,0:T(8,128)} %get-tuple-element.17.sin_ref, bf16[512,4096]{1,0:T(8,128)(2,1)} %q_ref.3, ...), custom_call_target="tpu_custom_call" | custom-call | tf_op jit(solution)/shard_map/pallas_call | solution.py:141
  113.5 11.7 %collective-permute-done.2.refs_0_.refs_1_.refs_2_.refs_3_ = bf16[512,4096]{1,0:T(8,128)(2,1)} collective-permute-done((bf16[512,4096]{1,0:T(8,128)(2,1)}, bf16[512,4096]{1,0:T(8,128)(2,1)}, u32[]{:S(2)}, u32[]{:S(2)}) %collective-permute-start.2) | collective-permute-done | bytes 4194336 | tf_op jit(solution)/shard_map/ppermute | solution.py:130
  125.2 25.5 %shard_map.47 = bf16[512,4096]{1,0:T(8,128)(2,1)} custom-call(s32[1]{0:T(128)} %bitcast.par_ref, s32[512,1]{1,0:T(8,128)} %copy.8.pos_ref, f32[1536,128]{1,0:T(8,128)} %get-tuple-element.16.cos_ref, f32[1536,128]{1,0:T(8,128)} %get-tuple-element.17.sin_ref, bf16[512,4096]{1,0:T(8,128)(2,1)} %q_ref.3, ...), custom_call_target="tpu_custom_call" | custom-call | tf_op jit(solution)/shard_map/pallas_call | solution.py:152
  (1 shorter events, 0.0 us)
Async XLA Ops:
  19.1 28.5 %collective-permute-start.1 = (bf16[512,2048]{1,0:T(8,128)(2,1)}, bf16[512,2048]{1,0:T(8,128)(2,1)S(1)}, u32[]{:S(2)}, u32[]{:S(2)}) collective-permute-start(bf16[512,2048]{1,0:T(8,128)(2,1)} %refs_3_.1), channel_id=1, source_target_pairs={{0,1},{1,2},{2,3},{3,4},{4,5},{5,6},{6,7},{7,8},{8,9},{9,10},{10,1... | collective-permute-start | bytes 6291464 | tf_op jit(solution)/shard_map/ppermute | solution.py:117
  21.4 48.8 %collective-permute-start = (bf16[512,2048]{1,0:T(8,128)(2,1)}, bf16[512,2048]{1,0:T(8,128)(2,1)}, u32[]{:S(2)}, u32[]{:S(2)}) collective-permute-start(bf16[512,2048]{1,0:T(8,128)(2,1)} %refs_1_.1), channel_id=1, source_target_pairs={{0,1},{1,2},{2,3},{3,4},{4,5},{5,6},{6,7},{7,8},{8,9},{9,10},{10,1... | collective-permute-start | bytes 6291464 | tf_op jit(solution)/shard_map/ppermute | solution.py:114
  74.2 51.0 %collective-permute-start.2 = (bf16[512,4096]{1,0:T(8,128)(2,1)}, bf16[512,4096]{1,0:T(8,128)(2,1)}, u32[]{:S(2)}, u32[]{:S(2)}) collective-permute-start(bf16[512,4096]{1,0:T(8,128)(2,1)} %pad_maximum_fusion.refs_0_.refs_2_), channel_id=1, source_target_pairs={{0,1},{1,2},{2,3},{3,4},{4,5},{5,6},{6,7},{7,8},{8,9},{9,10},{10,1... | collective-permute-start | bytes 12582920 | tf_op jit(solution)/shard_map/ppermute | solution.py:130

commit v18 on v15

--- a/solution.py
+++ b/solution.py
@@ -33,9 +33,9 @@
 
 def attend_kernel(par_ref, pos_ref, cos_ref, sin_ref, q_ref, *refs, rows, tile, first, final):
     if final:
-        k2a, k2b, v2a, v2b, st_in, acc_in, o_ref, bias_ref = refs
+        k2, v2, st_in, acc_in, o_ref, bias_ref = refs
     else:
-        k1, k0, v1, v0, st_out, acc_out, bias_ref = refs
+        k1, k0, v1, v0, st_out, acc_out, qr_out, bias_ref = refs
     tiles = rows // tile
     nkeys = bias_ref.shape[2]
     qoff = W
@@ -62,9 +62,8 @@
         return x * c + pltpu.roll(x, HD // 2, 1) * s
 
     if final:
-        even = par_ref[0] == 0
-        k = jnp.where(even, k2a[...], k2b[...])
-        v = jnp.where(even, v2a[...], v2b[...])
+        k = k2[...]
+        v = v2[...]
     else:
         k = jnp.concatenate([k1[...], k0[...]], 0)
         v = jnp.concatenate([v1[...], v0[...]], 0)
@@ -84,8 +83,12 @@
         qs = sin[qoff + r0:qoff + r0 + tile]
         for g in range(2):
             cols = slice(g * HD, (g + 1) * HD)
-            q = q_ref[r0:r0 + tile, cols].astype(jnp.float32)
-            q = rot(q, qc, qs).astype(jnp.bfloat16)
+            if final:
+                q = q_ref[r0:r0 + tile, cols]
+            else:
+                q = q_ref[r0:r0 + tile, cols].astype(jnp.float32)
+                q = rot(q, qc, qs).astype(jnp.bfloat16)
+                qr_out[r0:r0 + tile, cols] = q
             s = lax.dot_general(q, kk, (((1,), (1,)), ((), ())), preferred_element_type=jnp.float32)
             s = s + bias
             m = jnp.max(s, axis=1, keepdims=True)
@@ -142,27 +145,28 @@
     lead = [full((rows, 1)), full((span, HD)), full((span, HD)), head_spec]
     params = pltpu.CompilerParams(dimension_semantics=("arbitrary",))
     f32 = jnp.float32
-    stats, acc1 = pl.pallas_call(
+    stats, acc1, q_rot = pl.pallas_call(
         functools.partial(attend_kernel, rows=rows, tile=tile, first=rows, final=False),
         grid_spec=pltpu.PrefetchScalarGridSpec(
             num_scalar_prefetch=1, grid=(heads,),
             in_specs=lead + [kv_spec, kv_spec, v_spec, kv_spec],
-            out_specs=[stat_spec, head_spec],
+            out_specs=[stat_spec, head_spec, head_spec],
             scratch_shapes=[pltpu.VMEM((rows // tile, tile, 2 * rows), f32)]),
         out_shape=[jax.ShapeDtypeStruct((heads, rows, 128), f32),
-                   jax.ShapeDtypeStruct(queries.shape, f32)],
+                   jax.ShapeDtypeStruct(queries.shape, f32),
+                   jax.ShapeDtypeStruct(queries.shape, jnp.bfloat16)],
         compiler_params=params,
     )(parity, pos_q, cos, sin, queries, near, keys, near, values)
     return pl.pallas_call(
         functools.partial(attend_kernel, rows=rows, tile=tile, first=0, final=True),
         grid_spec=pltpu.PrefetchScalarGridSpec(
             num_scalar_prefetch=1, grid=(heads,),
-            in_specs=lead + [kv_spec, kv_spec, v_spec, v_spec] + [stat_spec, head_spec],
+            in_specs=lead + [kv_spec, v_spec] + [stat_spec, head_spec],
             out_specs=head_spec,
             scratch_shapes=[pltpu.VMEM((rows // tile, tile, rows), f32)]),
         out_shape=jax.ShapeDtypeStruct(queries.shape, jnp.bfloat16),
         compiler_params=params,
-    )(parity, pos_q, cos, sin, queries, far, far, far, far, stats, acc1)
+    )(parity, pos_q, cos, sin, q_rot, far, far, stats, acc1)
 
 
 def solution(mesh):

time: 141 us -> 139 us (0.986)
  Pallas kernels: 62.1 us -> 60.6 us
    pallas_call x2, Pallas kernels: 62.1 us -> 60.6 us  [local(): pl.pallas_call(functools.partial(attend_kernel, rows=rows, tile=tile, fir...]
  transfers between devices with their start and end apart: 2 -> 2, of which waited for: 0 -> 0; matrix products, arithmetic and copies ran while one was open for 5% -> 5% of each run, Pallas kernels for 26% -> 27%
where the time goes in v18:
time: 139 us
  Pallas kernels  60.6 us (44%)
  blocking collectives  59.3 us (43%)
  other arithmetic  8.52 us (6%)
  starting transfers between devices  8.42 us (6%)
  local copies, waits for them, and re-layouts  1.67 us (1%)
    pallas_call x2, Pallas kernels, local(): pl.pallas_call(functools.partial(attend_kernel, rows=rows, tile=tile, fir...  60.6 us
    all_gather x1, blocking collectives, local(): seg_all = lax.all_gather(segment_ids, 'seq', tiled=True)  59.3 us
    ppermute x1, starting transfers between devices, local(): near = lax.ppermute(both, 'seq', [(s, s + 1) for s in range(count - 1)])  4.38 us
    ppermute x1, starting transfers between devices, local(): far = lax.ppermute(near, 'seq', [(s, s + 1) for s in range(count - 1)])  4.04 us
    neg x1, other arithmetic, rope_tables(): return (jnp.concatenate([cos, cos], -1), jnp.concatenate([-sin, sin], -1))  2.81 us
  transfers between devices with their start and end apart: 2, of which 0 were waited for; matrix products, arithmetic and copies ran while one was open for 5% of the time, Pallas kernels for 27%

profile of v18, /device:TPU:0, one launch (start us, length us, event | category | flops | bytes accessed | tf_op | source)
XLA Modules:
  0.0 138.6 jit_solution(10322253384337866834)
XLA Ops:
  0.0 0.0 copy-start
  0.0 2.7 %pad_maximum_fusion = bf16[512,4096]{1,0:T(8,128)(2,1)S(1)} fusion(bf16[512,2048]{1,0:T(8,128)(2,1)} %refs_3_.1, bf16[512,2048]{1,0:T(8,128)(2,1)} %refs_1_.1), kind=kLoop, calls=%fused_computation | loop fusion | flops 8388608 | bytes 8388608 | tf_op jit(solution)/shard_map/concatenate | solution.py:123
  2.7 4.4 %collective-permute-start = (bf16[512,4096]{1,0:T(8,128)(2,1)S(1)}, bf16[512,4096]{1,0:T(8,128)(2,1)}, u32[]{:S(2)}, u32[]{:S(2)}) collective-permute-start(bf16[512,4096]{1,0:T(8,128)(2,1)S(1)} %pad_maximum_fusion), channel_id=1, source_target_pairs={{0,1},{1,2},{2,3},{3,4},{4,5},{5,6},{6,7},{7,8},{8,9},{9,10},{10,1... | collective-permute-start | bytes 12582920 | tf_op jit(solution)/shard_map/ppermute | solution.py:124
  7.1 0.0 copy-done
  7.1 59.3 %all-gather = s32[16,1,512]{2,1,0:T(1,128)S(1)} all-gather(s32[1,1,512]{2,1,0:T(1,128)S(1)} %bitcast.13), channel_id=1, replica_groups=mesh['grp'=2,'seq'=16] {'seq'}, dimensions={0}, use_global_device_ids=true | all-gather | bytes 34816 | tf_op jit(solution)/shard_map/all_gather | solution.py:125
  66.4 0.0 collective-permute-done.refs_0_.refs_2_
  66.4 4.0 %collective-permute-start.1 = (bf16[512,4096]{1,0:T(8,128)(2,1)}, bf16[512,4096]{1,0:T(8,128)(2,1)}, u32[]{:S(2)}, u32[]{:S(2)}) collective-permute-start(bf16[512,4096]{1,0:T(8,128)(2,1)} %collective-permute-done.refs_0_.refs_2_), channel_id=1, source_target_pairs={{0,1},{1,2},{2,3},{3,4},{4,5},{5,6},{6,7},{7,8},{8,9},{9,10},{10,1... | collective-permute-start | bytes 12582920 | tf_op jit(solution)/shard_map/ppermute | solution.py:127
  70.5 0.5 slice.16
  71.0 0.7 select_bitcast_fusion
  71.7 0.3 reduce-window.9
  72.0 0.1 slice.21
  72.1 0.1 reduce-window.12
  72.2 0.1 slice_reduce_fusion
  72.3 0.1 bitcast_subtract_fusion
  72.4 0.1 pad_dynamic-slice_fusion
  72.5 0.9 copy.8.pos_ref
  73.3 0.1 fusion.2
  73.4 2.8 %fusion = (f32[1536,64]{1,0:T(8,128)S(1)}, f32[1536,64]{1,0:T(8,128)S(1)}, f32[1536,64]{1,0:T(8,128)S(1)}) fusion(f32[64]{0:T(128)S(1)} %multiply_power_fusion, f32[1536]{0:T(1024)S(1)} %fusion.2), kind=kLoop, calls=%fused_computation.5 | loop fusion | flops 196608 | bytes 1186048 | tf_op jit(solution)/shard_map/neg | solution.py:31
  76.2 1.7 %pad_maximum_fusion.1 = (f32[1536,128]{1,0:T(8,128)}, f32[1536,128]{1,0:T(8,128)}) fusion(f32[1536,64]{1,0:T(8,128)S(1)} %get-tuple-element.17, f32[1536,64]{1,0:T(8,128)S(1)} %get-tuple-element.16, f32[1536,64]{1,0:T(8,128)S(1)} %get-tuple-element.15), kind=kLoop, calls=%fused_computation.3 | loop fusion | flops 393216 | bytes 2752512 | tf_op jit(solution)/shard_map/concatenate | solution.py:31
  77.9 37.0 %shard_map.46 = (f32[16,512,128]{2,1,0:T(8,128)}, f32[512,4096]{1,0:T(8,128)}, bf16[512,4096]{1,0:T(8,128)(2,1)}) custom-call(s32[1]{0:T(128)} %bitcast.par_ref, s32[512,1]{1,0:T(8,128)} %copy.8.pos_ref, f32[1536,128]{1,0:T(8,128)} %get-tuple-element.18.cos_ref, f32[1536,128]{1,0:T(8,128)} %get-tuple-element.19.sin_ref, bf16[512,4096]{1,0:T(8,128)(2,1)} %q_ref.1, ...), custom_call_target="tpu_custom_call" | custom-call | tf_op jit(solution)/shard_map/pallas_call | solution.py:148
  114.9 0.0 collective-permute-done.1.refs_0_.refs_1_
  114.9 23.7 %shard_map.47 = bf16[512,4096]{1,0:T(8,128)(2,1)} custom-call(s32[1]{0:T(128)} %bitcast.par_ref, s32[512,1]{1,0:T(8,128)} %copy.8.pos_ref, f32[1536,128]{1,0:T(8,128)} %get-tuple-element.18.cos_ref, f32[1536,128]{1,0:T(8,128)} %get-tuple-element.19.sin_ref, bf16[512,4096]{1,0:T(8,128)(2,1)} %get-tuple-element.12.q_ref, ...), custom_call_target="tpu_custom_call" | custom-call | tf_op jit(solution)/shard_map/pallas_call | solution.py:160
  (1 shorter events, 0.0 us)
Async XLA Ops:
  0.0 7.1 %copy-start = (s32[512]{0:T(512)S(1)}, s32[512]{0:T(512)}, u32[]{:S(2)}) copy-start(s32[512]{0:T(512)} %param.7) | copy-start | bytes 6148
  2.7 63.7 %collective-permute-start = (bf16[512,4096]{1,0:T(8,128)(2,1)S(1)}, bf16[512,4096]{1,0:T(8,128)(2,1)}, u32[]{:S(2)}, u32[]{:S(2)}) collective-permute-start(bf16[512,4096]{1,0:T(8,128)(2,1)S(1)} %pad_maximum_fusion), channel_id=1, source_target_pairs={{0,1},{1,2},{2,3},{3,4},{4,5},{5,6},{6,7},{7,8},{8,9},{9,10},{10,1... | collective-permute-start | bytes 12582920 | tf_op jit(solution)/shard_map/ppermute | solution.py:124
  66.4 48.5 %collective-permute-start.1 = (bf16[512,4096]{1,0:T(8,128)(2,1)}, bf16[512,4096]{1,0:T(8,128)(2,1)}, u32[]{:S(2)}, u32[]{:S(2)}) collective-permute-start(bf16[512,4096]{1,0:T(8,128)(2,1)} %collective-permute-done.refs_0_.refs_2_), channel_id=1, source_target_pairs={{0,1},{1,2},{2,3},{3,4},{4,5},{5,6},{6,7},{7,8},{8,9},{9,10},{10,1... | collective-permute-start | bytes 12582920 | tf_op jit(solution)/shard_map/ppermute | solution.py:127

commit v19 on v18

--- a/solution.py
+++ b/solution.py
@@ -55,9 +55,6 @@
             vis = (gap >= 0) & (gap < W) & (gap <= dp[a * tile:(a + 1) * tile])
             bias_ref[a] = jnp.where(vis, 0.0, -1e30).astype(jnp.float32)
 
-    cos = cos_ref[...]
-    sin = sin_ref[...]
-
     def rot(x, c, s):
         return x * c + pltpu.roll(x, HD // 2, 1) * s
 
@@ -67,7 +64,7 @@
     else:
         k = jnp.concatenate([k1[...], k0[...]], 0)
         v = jnp.concatenate([v1[...], v0[...]], 0)
-    k = rot(k.astype(jnp.float32), cos[first:first + nkeys], sin[first:first + nkeys])
+    k = rot(k.astype(jnp.float32), cos_ref[first:first + nkeys, :], sin_ref[first:first + nkeys, :])
     k = k.astype(jnp.bfloat16)
     lane = lax.broadcasted_iota(jnp.int32, (tile, 128), 1)
     for a in range(tiles):
@@ -79,14 +76,14 @@
         kk = k[lo:hi]
         vv = v[lo:hi]
         bias = bias_ref[a, :, lo:hi]
-        qc = cos[qoff + r0:qoff + r0 + tile]
-        qs = sin[qoff + r0:qoff + r0 + tile]
         for g in range(2):
             cols = slice(g * HD, (g + 1) * HD)
             if final:
                 q = q_ref[r0:r0 + tile, cols]
             else:
                 q = q_ref[r0:r0 + tile, cols].astype(jnp.float32)
+                qc = cos_ref[qoff + r0:qoff + r0 + tile, :]
+                qs = sin_ref[qoff + r0:qoff + r0 + tile, :]
                 q = rot(q, qc, qs).astype(jnp.bfloat16)
                 qr_out[r0:r0 + tile, cols] = q
             s = lax.dot_general(q, kk, (((1,), (1,)), ((), ())), preferred_element_type=jnp.float32)

time: 139 us -> 140 us (level)
  no operation moved by 1% of the time
where the time goes in v19:
time: 140 us; the launch traced here: 139 us
  Pallas kernels  60.9 us (44%)
  blocking collectives  59.3 us (42%)
  other arithmetic  8.52 us (6%)
  starting transfers between devices  8.42 us (6%)
  local copies, waits for them, and re-layouts  1.67 us (1%)
    pallas_call x2, Pallas kernels, local(): pl.pallas_call(functools.partial(attend_kernel, rows=rows, tile=tile, fir...  60.9 us
    all_gather x1, blocking collectives, local(): seg_all = lax.all_gather(segment_ids, 'seq', tiled=True)  59.3 us
    ppermute x1, starting transfers between devices, local(): near = lax.ppermute(both, 'seq', [(s, s + 1) for s in range(count - 1)])  4.38 us
    ppermute x1, starting transfers between devices, local(): far = lax.ppermute(near, 'seq', [(s, s + 1) for s in range(count - 1)])  4.04 us
    neg x1, other arithmetic, rope_tables(): return (jnp.concatenate([cos, cos], -1), jnp.concatenate([-sin, sin], -1))  2.81 us
  transfers between devices with their start and end apart: 2, of which 0 were waited for; matrix products, arithmetic and copies ran while one was open for 5% of the time, Pallas kernels for 27%

profile of v19, /device:TPU:0, one launch (start us, length us, event | category | flops | bytes accessed | tf_op | source)
XLA Modules:
  0.0 138.8 jit_solution(7881670534015715312)
XLA Ops:
  0.0 0.0 copy-start
  0.0 2.7 %pad_maximum_fusion = bf16[512,4096]{1,0:T(8,128)(2,1)S(1)} fusion(bf16[512,2048]{1,0:T(8,128)(2,1)} %refs_3_.1, bf16[512,2048]{1,0:T(8,128)(2,1)} %refs_1_.1), kind=kLoop, calls=%fused_computation | loop fusion | flops 8388608 | bytes 8388608 | tf_op jit(solution)/shard_map/concatenate | solution.py:120
  2.7 4.4 %collective-permute-start = (bf16[512,4096]{1,0:T(8,128)(2,1)S(1)}, bf16[512,4096]{1,0:T(8,128)(2,1)}, u32[]{:S(2)}, u32[]{:S(2)}) collective-permute-start(bf16[512,4096]{1,0:T(8,128)(2,1)S(1)} %pad_maximum_fusion), channel_id=1, source_target_pairs={{0,1},{1,2},{2,3},{3,4},{4,5},{5,6},{6,7},{7,8},{8,9},{9,10},{10,1... | collective-permute-start | bytes 12582920 | tf_op jit(solution)/shard_map/ppermute | solution.py:121
  7.1 0.0 copy-done
  7.1 59.3 %all-gather = s32[16,1,512]{2,1,0:T(1,128)S(1)} all-gather(s32[1,1,512]{2,1,0:T(1,128)S(1)} %bitcast.13), channel_id=1, replica_groups=mesh['grp'=2,'seq'=16] {'seq'}, dimensions={0}, use_global_device_ids=true | all-gather | bytes 34816 | tf_op jit(solution)/shard_map/all_gather | solution.py:122
  66.4 0.0 collective-permute-done.refs_0_.refs_2_
  66.4 4.0 %collective-permute-start.1 = (bf16[512,4096]{1,0:T(8,128)(2,1)}, bf16[512,4096]{1,0:T(8,128)(2,1)}, u32[]{:S(2)}, u32[]{:S(2)}) collective-permute-start(bf16[512,4096]{1,0:T(8,128)(2,1)} %collective-permute-done.refs_0_.refs_2_), channel_id=1, source_target_pairs={{0,1},{1,2},{2,3},{3,4},{4,5},{5,6},{6,7},{7,8},{8,9},{9,10},{10,1... | collective-permute-start | bytes 12582920 | tf_op jit(solution)/shard_map/ppermute | solution.py:124
  70.5 0.5 slice.16
  71.0 0.7 select_bitcast_fusion
  71.7 0.3 reduce-window.9
  72.0 0.1 slice.21
  72.1 0.1 reduce-window.12
  72.2 0.1 slice_reduce_fusion
  72.3 0.1 bitcast_subtract_fusion
  72.4 0.1 pad_dynamic-slice_fusion
  72.5 0.9 copy.8.pos_ref
  73.3 0.1 fusion.2
  73.4 2.8 %fusion = (f32[1536,64]{1,0:T(8,128)S(1)}, f32[1536,64]{1,0:T(8,128)S(1)}, f32[1536,64]{1,0:T(8,128)S(1)}) fusion(f32[64]{0:T(128)S(1)} %multiply_power_fusion, f32[1536]{0:T(1024)S(1)} %fusion.2), kind=kLoop, calls=%fused_computation.5 | loop fusion | flops 196608 | bytes 1186048 | tf_op jit(solution)/shard_map/neg | solution.py:31
  76.2 1.7 %pad_maximum_fusion.1 = (f32[1536,128]{1,0:T(8,128)}, f32[1536,128]{1,0:T(8,128)}) fusion(f32[1536,64]{1,0:T(8,128)S(1)} %get-tuple-element.17, f32[1536,64]{1,0:T(8,128)S(1)} %get-tuple-element.16, f32[1536,64]{1,0:T(8,128)S(1)} %get-tuple-element.15), kind=kLoop, calls=%fused_computation.3 | loop fusion | flops 393216 | bytes 2752512 | tf_op jit(solution)/shard_map/concatenate | solution.py:31
  77.9 37.2 %shard_map.46 = (f32[16,512,128]{2,1,0:T(8,128)}, f32[512,4096]{1,0:T(8,128)}, bf16[512,4096]{1,0:T(8,128)(2,1)}) custom-call(s32[1]{0:T(128)} %bitcast.par_ref, s32[512,1]{1,0:T(8,128)} %copy.8.pos_ref, f32[1536,128]{1,0:T(8,128)} %get-tuple-element.18.cos_ref, f32[1536,128]{1,0:T(8,128)} %get-tuple-element.19.sin_ref, bf16[512,4096]{1,0:T(8,128)(2,1)} %q_ref.1, ...), custom_call_target="tpu_custom_call" | custom-call | tf_op jit(solution)/shard_map/pallas_call | solution.py:145
  115.2 0.0 collective-permute-done.1.refs_0_.refs_1_
  115.2 23.7 %shard_map.47 = bf16[512,4096]{1,0:T(8,128)(2,1)} custom-call(s32[1]{0:T(128)} %bitcast.par_ref, s32[512,1]{1,0:T(8,128)} %copy.8.pos_ref, f32[1536,128]{1,0:T(8,128)} %get-tuple-element.18.cos_ref, f32[1536,128]{1,0:T(8,128)} %get-tuple-element.19.sin_ref, bf16[512,4096]{1,0:T(8,128)(2,1)} %get-tuple-element.12.q_ref, ...), custom_call_target="tpu_custom_call" | custom-call | tf_op jit(solution)/shard_map/pallas_call | solution.py:157
  (1 shorter events, 0.0 us)
Async XLA Ops:
  0.0 7.1 %copy-start = (s32[512]{0:T(512)S(1)}, s32[512]{0:T(512)}, u32[]{:S(2)}) copy-start(s32[512]{0:T(512)} %param.7) | copy-start | bytes 6148
  2.7 63.7 %collective-permute-start = (bf16[512,4096]{1,0:T(8,128)(2,1)S(1)}, bf16[512,4096]{1,0:T(8,128)(2,1)}, u32[]{:S(2)}, u32[]{:S(2)}) collective-permute-start(bf16[512,4096]{1,0:T(8,128)(2,1)S(1)} %pad_maximum_fusion), channel_id=1, source_target_pairs={{0,1},{1,2},{2,3},{3,4},{4,5},{5,6},{6,7},{7,8},{8,9},{9,10},{10,1... | collective-permute-start | bytes 12582920 | tf_op jit(solution)/shard_map/ppermute | solution.py:121
  66.4 48.7 %collective-permute-start.1 = (bf16[512,4096]{1,0:T(8,128)(2,1)}, bf16[512,4096]{1,0:T(8,128)(2,1)}, u32[]{:S(2)}, u32[]{:S(2)}) collective-permute-start(bf16[512,4096]{1,0:T(8,128)(2,1)} %collective-permute-done.refs_0_.refs_2_), channel_id=1, source_target_pairs={{0,1},{1,2},{2,3},{3,4},{4,5},{5,6},{6,7},{7,8},{8,9},{9,10},{10,1... | collective-permute-start | bytes 12582920 | tf_op jit(solution)/shard_map/ppermute | solution.py:124
